TPU v7x, 512 devices: a whole 4x8x8 slice. The times are simulated.
512 devices in a mesh: seq: 64 (over y, z_lo, x), ch: 8 (over z_hi, core).
Axes of the slice: x: 4, y: 8, z: 8 (z_hi: 4, z_lo: 2; z = z_hi * 2 + z_lo), core: 2. Of those that a mesh axis runs over, the one named last changes fastest.
Arguments:
- inputs: bfloat16 [16384, 1024], P('seq', 'ch'), may hold values from -6 to 6
- gate_values: bfloat16 [16384, 1024], P('seq', 'ch'), may hold values from -600 to 1100
- causal_filter: bfloat16 [16384, 1024], P('seq', 'ch'), may hold values from -0.046875 to 0.046875
- anti_filter: bfloat16 [16384, 1024], P('seq', 'ch'), may hold values from -0.046875 to 0.046875
- skip_gain: float32 [1024], P('ch'), may hold values from 0.25 to 1.75
- norm_gain: float32 [1024], P('ch'), may hold values from 0.25 to 1.75
Outputs:
- mixer_out: bfloat16 [16384, 1024], P('seq', 'ch')
All inputs are finite; a program needn't handle non-finite values.
Results may differ from a plain program's by a relative error of at most 0.007.
Values may be sent and summed in bfloat16 or wider, within the bound.
No kernel may reach another device: no remote copies, remote signals or barrier semaphores. Data moves between devices by JAX's collectives and lax.ppermute only.
A program may use at most 128 MiB of HBM per device.

v0:
```python
import math

import jax
import jax.numpy as jnp
from jax import lax
from jax.sharding import PartitionSpec as P

D = 1024


def passed_along(block, axis, distance):
    devices = range(lax.axis_size(axis))
    route = [((i - distance) % len(devices), i) for i in devices]
    return lax.ppermute(block, axis, route)


def forward_table(rows_dev):
    freq_ids = jnp.arange(rows_dev + 1, dtype=jnp.int32)[:, None]
    place_ids = jnp.arange(rows_dev, dtype=jnp.int32)[None, :]
    phases = (freq_ids * place_ids % (2 * rows_dev)).astype(jnp.float32) * jnp.float32(
        math.pi / rows_dev
    )
    return jnp.concatenate([jnp.cos(phases), -jnp.sin(phases)], axis=0).astype(jnp.bfloat16)


def inverse_table(rows_dev):
    place_ids = jnp.arange(rows_dev, dtype=jnp.int32)[:, None] + rows_dev
    freq_ids = jnp.arange(rows_dev + 1, dtype=jnp.int32)[None, :]
    phases = (freq_ids * place_ids % (2 * rows_dev)).astype(jnp.float32) * jnp.float32(
        math.pi / rows_dev
    )
    edges = jnp.logical_or(freq_ids == 0, freq_ids == rows_dev)
    weights = jnp.where(edges, jnp.float32(1.0), jnp.float32(2.0)) / jnp.float32(2 * rows_dev)
    return jnp.concatenate([weights * jnp.cos(phases), -weights * jnp.sin(phases)], axis=1)


def alternating(rows_dev):
    parity = (jnp.arange(rows_dev + 1, dtype=jnp.int32) % 2).astype(jnp.float32)
    signs_half = jnp.float32(1.0) - jnp.float32(2.0) * parity
    return jnp.concatenate([signs_half, signs_half])[:, None]


def complex_product(segment, block_spec, conj_sign):
    freq_rows = segment.shape[-2] // 2
    seg_re = segment[..., :freq_rows, :]
    seg_im = segment[..., freq_rows:, :] * conj_sign
    blk_re = block_spec[..., :freq_rows, :]
    blk_im = block_spec[..., freq_rows:, :]
    return jnp.concatenate(
        [seg_re * blk_re - seg_im * blk_im, seg_re * blk_im + seg_im * blk_re], axis=-2
    )


def accumulate(spectrum_sum, arrivals, forward_lookup, alternate):
    chan_dev = arrivals[0][0].shape[1]
    stacked = jnp.concatenate(
        [piece_blk for arrival in arrivals for piece_blk in arrival[:3]], axis=1
    )
    filter_spectrum = jnp.dot(forward_lookup, stacked, preferred_element_type=jnp.float32).astype(
        jnp.bfloat16
    )
    filter_spectrum = lax.optimization_barrier(filter_spectrum)
    for number, arrival in enumerate(arrivals):
        offset = 3 * number * chan_dev
        block_spec = filter_spectrum[:, offset : offset + chan_dev].astype(jnp.float32)
        lower_spec = filter_spectrum[:, offset + chan_dev : offset + 2 * chan_dev].astype(
            jnp.float32
        )
        upper_spec = filter_spectrum[:, offset + 2 * chan_dev : offset + 3 * chan_dev].astype(
            jnp.float32
        )
        spectrum_sum = spectrum_sum + complex_product(
            lower_spec + alternate * upper_spec, block_spec, arrival[3]
        )
    return spectrum_sum


def pass_forward(held):
    return passed_along(held, "seq", 1)


def on_device(inputs, gate_values, causal_filter, anti_filter, skip_gain, norm_gain):
    rows_dev, chan_dev = inputs.shape
    freq_rows = rows_dev + 1
    blocks = lax.axis_size("seq")
    own_index = lax.axis_index("seq")
    row_ids = lax.broadcasted_iota(jnp.int32, (rows_dev, 1), 0) + own_index * rows_dev
    anti_masked = jnp.where(row_ids > 0, anti_filter, jnp.zeros_like(anti_filter))
    forward_lookup = forward_table(rows_dev)
    inv_table = inverse_table(rows_dev)
    alternate = alternating(rows_dev)
    empty_sum = jnp.zeros((2 * freq_rows, chan_dev), jnp.float32)
    plus_one = jnp.float32(1.0)
    minus_one = jnp.float32(-1.0)
    all_causal, all_anti = (
        lax.all_gather(causal_filter, "seq", axis=0, tiled=True),
        lax.all_gather(anti_masked, "seq", axis=0, tiled=True),
    )
    lead_pad = jnp.zeros((rows_dev, chan_dev), all_causal.dtype)
    causal_rows = jnp.concatenate([lead_pad, all_causal], axis=0)
    anti_rows = jnp.concatenate([lead_pad, all_anti], axis=0)

    def lag_item(held, is_causal, lag_now):
        lower_at = lag_now * rows_dev
        upper_at = lower_at + rows_dev
        lower_blk = jnp.where(
            is_causal,
            lax.dynamic_slice_in_dim(causal_rows, lower_at, rows_dev, 0),
            lax.dynamic_slice_in_dim(anti_rows, lower_at, rows_dev, 0),
        )
        upper_blk = jnp.where(
            is_causal,
            lax.dynamic_slice_in_dim(causal_rows, upper_at, rows_dev, 0),
            lax.dynamic_slice_in_dim(anti_rows, upper_at, rows_dev, 0),
        )
        return (held, lower_blk, upper_blk, jnp.where(is_causal, plus_one, minus_one))

    def forward_entry(held, step_index):
        is_causal = step_index <= own_index
        return lag_item(held, is_causal, jnp.where(is_causal, step_index, blocks - step_index))

    def backward_item(held, step_index):
        is_causal = own_index + step_index > blocks - 1
        return lag_item(held, is_causal, jnp.where(is_causal, blocks - step_index, step_index))

    spectrum_sum = accumulate(
        empty_sum, [forward_entry(inputs, 0), backward_item(inputs, 0)], forward_lookup, alternate
    )

    def visit_both(step_index, loop_state):
        total_now, ahead, behind = loop_state
        ahead = pass_forward(ahead)
        behind = passed_along(behind, "seq", -1)
        total_now = accumulate(
            total_now,
            [forward_entry(ahead, step_index), backward_item(behind, step_index)],
            forward_lookup,
            alternate,
        )
        return (total_now, ahead, behind)

    spectrum_sum, ahead, behind = lax.fori_loop(
        1, blocks // 2, visit_both, (spectrum_sum, inputs, inputs)
    )
    ahead = pass_forward(ahead)
    spectrum_sum = accumulate(
        spectrum_sum, [forward_entry(ahead, blocks // 2)], forward_lookup, alternate
    )
    convolved = jnp.dot(
        inv_table, spectrum_sum, precision=lax.Precision.HIGHEST, preferred_element_type=jnp.float32
    )
    gated_mix = gate_values.astype(jnp.float32) * (
        convolved + skip_gain[None, :] * inputs.astype(jnp.float32)
    )
    squares = lax.psum(jnp.sum(gated_mix * gated_mix, axis=1), "ch")
    inv_norm = lax.rsqrt(squares / D + 1e-06)
    return (norm_gain[None, :] * gated_mix * inv_norm[:, None]).astype(jnp.bfloat16)


def solution(mesh):
    placed = (P("seq", "ch"), P("seq", "ch"), P("seq", "ch"), P("seq", "ch"), P("ch"), P("ch"))
    return jax.shard_map(
        on_device, mesh=mesh, in_specs=placed, out_specs=P("seq", "ch"), check_vma=False
    )
```

profile of v0, /device:TPU:1, one launch (start us, length us, event | category | flops | bytes accessed | tf_op | source)
XLA Modules:
  0.0 1137.2 jit_solution(11908115920060747931)
XLA Ops:
  13.1 264.8 %all-gather.3.cloned.1.call-done = bf16[16384,128]{1,0:T(8,128)(2,1)} async-done(((bf16[256,128]{1,0:T(8,128)(2,1)}), bf16[16384,128]{1,0:T(8,128)(2,1)}) %all-gather.3.cloned.1.call-update) | async-done | bytes 4194320 | tf_op jit(solution)/shard_map/all_gather | solution.py:96
  277.9 306.4 %all-gather.5.cloned.1.call-done = bf16[16384,128]{1,0:T(8,128)(2,1)} async-done(((bf16[256,128]{1,0:T(8,128)(2,1)}), bf16[16384,128]{1,0:T(8,128)(2,1)}) %all-gather.5.cloned.1.call-update) | async-done | bytes 4194320 | tf_op jit(solution)/shard_map/all_gather | solution.py:97
  594.1 440.3 %while.20 = (s32[]{:T(128)}, f32[514,128]{1,0:T(8,128)S(1)}, bf16[256,128]{1,0:T(8,128)(2,1)S(1)}, bf16[256,128]{1,0:T(8,128)(2,1)S(1)}, s32[]{:T(128)}, /*index...) while((s32[]{:T(128)}, f32[514,128]{1,0:T(8,128)S(1)}, ...), condition=%wide.region_1.2_spmd, body=%wide.region_0.1_spmd.sunk | while | flops 204020496 | bytes 7761483 | solution.py:142
  624.6 7.6 collective-permute-start.1
  638.8 7.6 collective-permute-start.1
  653.0 7.6 collective-permute-start.1
  738.1 7.6 collective-permute-start.1
  752.3 7.6 collective-permute-start.1
  766.5 7.6 collective-permute-start.1
  780.6 7.6 collective-permute-start.1
  794.8 7.6 collective-permute-start.1
  809.0 7.6 collective-permute-start.1
  823.2 7.6 collective-permute-start.1
  837.4 7.6 collective-permute-start.1
  851.6 7.6 collective-permute-start.1
  865.8 7.6 collective-permute-start.1
  880.0 7.8 collective-permute-start.1
  894.5 7.6 collective-permute-start.1
  908.7 7.6 collective-permute-start.1
  922.9 7.6 collective-permute-start.1
  937.0 7.6 collective-permute-start.1
  951.2 7.6 collective-permute-start.1
  965.4 7.6 collective-permute-start.1
  1045.2 84.4 %psum.7 = f32[256]{0:T(256)S(1)} all-reduce(f32[256]{0:T(256)S(1)} %get-tuple-element.294), channel_id=1, replica_groups=mesh['seq'=64,'ch'=8] {'ch'}, use_global_device_ids=true, to_apply=%region_3.4 | all-reduce | flops 256 | bytes 2048 | tf_op jit(solution)/shard_map/psum | solution.py:155
  (589 shorter events, 311.5 us)
Async XLA Ops:
  6.5 271.4 %all-gather.3.cloned.1.call-start = ((), (), s32[]{:S(2)}) async-start(), calls=%async_computation | async-start | bytes 4259840 | tf_op jit(solution)/shard_map/all_gather | solution.py:96
  7.4 576.9 %all-gather.5.cloned.1.call-start = ((), (), s32[]{:S(2)}) async-start(), calls=%async_computation.1 | async-start | bytes 4259840 | tf_op jit(solution)/shard_map/all_gather | solution.py:97
  594.1 9.7 collective-permute-start
  608.4 9.6 collective-permute-start
  622.6 9.6 collective-permute-start
  636.8 9.6 collective-permute-start
  651.0 9.6 collective-permute-start
  665.2 9.6 collective-permute-start
  764.5 9.6 collective-permute-start
  778.7 9.6 collective-permute-start
  792.9 9.6 collective-permute-start
  807.1 9.6 collective-permute-start
  821.3 9.6 collective-permute-start
  835.5 9.6 collective-permute-start
  849.7 9.6 collective-permute-start
  863.8 9.6 collective-permute-start
  878.0 9.9 collective-permute-start
  880.0 9.8 collective-permute-start.1
  906.7 9.6 collective-permute-start
  920.9 9.6 collective-permute-start
  935.1 9.6 collective-permute-start
  949.3 9.6 collective-permute-start
  963.5 9.6 collective-permute-start
  977.7 9.6 collective-permute-start
  (45 other events, 941.2 us)
Sparse Core Ops, SparseCore 0:
  9.4 268.4 all-gather.2
  280.0 304.2 all-gather.4
where the time goes:
time: 1150 us; the launch traced here: 1140 us
  waiting for transfers between devices  578 us (50%)
  starting transfers between devices  297 us (26%)
  other arithmetic  134 us (12%)
  blocking collectives  84.4 us (7%)
  between operations  13.6 us (1%)
  matrix products  13.4 us (1%)
  local copies, waits for them, and re-layouts  12.6 us (1%)
    all_gather x1, waiting for transfers between devices, on_device(): lax.all_gather(anti_masked, 'seq', axis=0, tiled=True)  306 us
    ppermute x63, starting transfers between devices, passed_along(): return lax.ppermute(block, axis, route)  297 us
    all_gather x1, waiting for transfers between devices, on_device(): lax.all_gather(causal_filter, 'seq', axis=0, tiled=True)  265 us
    while x93, other arithmetic  84.7 us
    psum x1, blocking collectives, on_device(): squares = lax.psum(jnp.sum(gated_mix * gated_mix, axis=1), 'ch')  84.4 us
    concatenate x32, other arithmetic, accumulate(): jnp.concatenate([piece_blk for arrival in arrivals for piece_blk in arriv...  28.4 us
  transfers between devices with their start and end apart: 65, of which 4 were waited for; matrix products, arithmetic and copies ran while one was open for 6% of the time, Pallas kernels for 0%

commit v1 on v0

v1 whole, which is shorter than its diff:
```python
import numpy as np

import jax
import jax.numpy as jnp
from jax import lax
from jax.sharding import PartitionSpec as P

D = 1024
HIGHEST = lax.Precision.HIGHEST


def padded(count, unit=8):
    return -(-count // unit) * unit


def inner_tables(rows_dev):
    freqs = rows_dev + 1
    fp = padded(freqs)
    f = np.arange(freqs)[:, None]
    n = np.arange(rows_dev)[None, :]
    phase = ((f * n) % (2 * rows_dev)) * (np.pi / rows_dev)
    fwd = np.zeros((2 * fp, rows_dev))
    fwd[:freqs] = np.cos(phase)
    fwd[fp : fp + freqs] = -np.sin(phase)
    t = np.arange(rows_dev)[:, None] + rows_dev
    f2 = np.arange(freqs)[None, :]
    phase2 = ((f2 * t) % (2 * rows_dev)) * (np.pi / rows_dev)
    weight = np.where((f2 == 0) | (f2 == rows_dev), 1.0, 2.0) / (2 * rows_dev)
    inv = np.zeros((rows_dev, 2 * fp))
    inv[:, :freqs] = weight * np.cos(phase2)
    inv[:, fp : fp + freqs] = -weight * np.sin(phase2)
    return fp, fwd, inv


def outer_tables(blocks, fp):
    size = 2 * blocks
    j = np.arange(blocks)[:, None]
    m = np.arange(size)[None, :]
    phase = 2 * np.pi * ((j * m) % size) / size
    fwd = np.concatenate([np.cos(phase), np.sin(phase)], axis=1)
    mi = np.arange(size)[:, None]
    i = np.arange(blocks)[None, :]
    phase_i = 2 * np.pi * ((mi * i) % size) / size
    cos_i = np.cos(phase_i) / size
    sin_i = np.sin(phase_i) / size
    inv_re = np.concatenate([cos_i, -sin_i], axis=0)
    inv_im = np.concatenate([sin_i, cos_i], axis=0)
    sign = np.where(np.arange(fp) % 2 == 0, 1.0, -1.0)[:, None]
    step = 2 * np.pi * np.arange(size)[None, :] / size
    shift_re = np.cos(step) + sign
    shift_im = -np.sin(step) + 0.0 * sign
    return fwd, inv_re, inv_im, shift_re, shift_im


def on_device(inputs, gate_values, causal_filter, anti_filter, skip_gain, norm_gain):
    rows_dev, chan_dev = inputs.shape
    blocks = lax.axis_size("seq")
    per = chan_dev // blocks
    size = 2 * blocks
    f32 = jnp.float32
    own_index = lax.axis_index("seq")
    row_ids = lax.broadcasted_iota(jnp.int32, (rows_dev, 1), 0) + own_index * rows_dev
    anti_masked = jnp.where(row_ids > 0, anti_filter, jnp.zeros_like(anti_filter))

    fp, fwd_np, inv_np = inner_tables(rows_dev)
    ofwd_np, oinv_re_np, oinv_im_np, sh_re_np, sh_im_np = outer_tables(blocks, fp)
    fwd = jnp.asarray(fwd_np, jnp.bfloat16)
    inv = jnp.asarray(inv_np, f32)
    ofwd = jnp.asarray(ofwd_np, f32)
    oinv_re = jnp.asarray(oinv_re_np, f32)
    oinv_im = jnp.asarray(oinv_im_np, f32)
    sh_re = jnp.asarray(sh_re_np, f32)
    sh_im = jnp.asarray(sh_im_np, f32)

    stacked = jnp.stack([inputs, causal_filter, anti_masked])
    send = (
        stacked.reshape(3, rows_dev, blocks, per)
        .transpose(2, 0, 3, 1)
        .reshape(blocks, 3 * per * rows_dev)
    )
    recv = lax.all_to_all(send, "seq", 0, 0, tiled=True)
    series = recv.reshape(blocks, 3 * per, rows_dev).transpose(1, 0, 2)

    spec = jnp.einsum("fn,qbn->qfb", fwd, series, preferred_element_type=f32)
    spec = spec.astype(jnp.bfloat16).astype(f32)
    z = jnp.einsum("qfb,bk->qfk", spec, ofwd, precision=HIGHEST, preferred_element_type=f32)
    z_re, z_im = z[:, :fp], z[:, fp:]
    x_re = (z_re[..., :size] + z_im[..., size:]).reshape(3, per, fp, size)
    x_im = (z_im[..., :size] - z_re[..., size:]).reshape(3, per, fp, size)

    c_re = sh_re * x_re[1] - sh_im * x_im[1]
    c_im = sh_re * x_im[1] + sh_im * x_re[1]
    a_re = sh_re * x_re[2] - sh_im * x_im[2]
    a_im = sh_re * x_im[2] + sh_im * x_re[2]
    k_re = c_re + a_re
    k_im = c_im - a_im
    y_re = k_re * x_re[0] - k_im * x_im[0]
    y_im = k_re * x_im[0] + k_im * x_re[0]
    y_cat = jnp.concatenate([y_re, y_im], axis=-1)

    t_re = jnp.einsum("cfk,ki->cfi", y_cat, oinv_re, precision=HIGHEST, preferred_element_type=f32)
    t_im = jnp.einsum("cfk,ki->cfi", y_cat, oinv_im, precision=HIGHEST, preferred_element_type=f32)
    total = jnp.concatenate([t_re, t_im], axis=1)
    conv_t = jnp.einsum("cfi,tf->cit", total, inv, precision=HIGHEST, preferred_element_type=f32)

    back = conv_t.transpose(1, 0, 2).reshape(blocks, per * rows_dev)
    got = lax.all_to_all(back, "seq", 0, 0, tiled=True)
    convolved = got.reshape(blocks * per, rows_dev).T

    gated_mix = gate_values.astype(f32) * (convolved + skip_gain[None, :] * inputs.astype(f32))
    squares = lax.psum(jnp.sum(gated_mix * gated_mix, axis=1), "ch")
    inv_norm = lax.rsqrt(squares / D + 1e-06)
    return (norm_gain[None, :] * gated_mix * inv_norm[:, None]).astype(jnp.bfloat16)


def solution(mesh):
    placed = (P("seq", "ch"), P("seq", "ch"), P("seq", "ch"), P("seq", "ch"), P("ch"), P("ch"))
    return jax.shard_map(
        on_device, mesh=mesh, in_specs=placed, out_specs=P("seq", "ch"), check_vma=False
    )
```

time: 1150 us -> 74.3 us (0.06); the launches traced: 1140 us -> 74 us
  waiting for transfers between devices: 578 us -> 9.63 us
  starting transfers between devices: 297 us -> 5.94 us
  other arithmetic: 134 us -> 5.16 us
  blocking collectives: 84.4 us -> 43.4 us
  between operations: 13.6 us -> 0.29 us
    all_gather x2 -> x0, waiting for transfers between devices: 571 us -> none  [the longest x1 306 us: on_device(): lax.all_gather(anti_masked, 'seq', axis=0, tiled=True)]
    ppermute x63 -> x0, starting transfers between devices: 297 us -> none  [passed_along(): return lax.ppermute(block, axis, route)]
    while x93 -> x0, other arithmetic: 84.7 us -> none
    psum x1, blocking collectives: 84.4 us -> 20.7 us  [on_device(): squares = lax.psum(jnp.sum(gated_mix * gated_mix, axis=1), 'ch')]
    concatenate x34 -> x0, other arithmetic: 28.5 us -> none  [the longest x32 28.4 us: accumulate(): jnp.concatenate([piece_blk for arrival in arrivals for piece_blk in arriv...]
    all_to_all x0 -> x1, blocking collectives: none -> 22.8 us  [on_device(): recv = lax.all_to_all(send, 'seq', 0, 0, tiled=True)]
  transfers between devices with their start and end apart: 65 -> 1, of which waited for: 4 -> 1; matrix products, arithmetic and copies ran while one was open for 6% -> 0% of each run, Pallas kernels for 0% -> 0%
where the time goes in v1:
time: 74.3 us; the launch traced here: 74 us
  blocking collectives  43.4 us (58%)
  waiting for transfers between devices  9.63 us (13%)
  starting transfers between devices  5.94 us (8%)
  local copies, waits for them, and re-layouts  5.73 us (8%)
  other arithmetic  5.16 us (7%)
  matrix products  3.82 us (5%)
    all_to_all x1, blocking collectives, on_device(): recv = lax.all_to_all(send, 'seq', 0, 0, tiled=True)  22.8 us
    psum x1, blocking collectives, on_device(): squares = lax.psum(jnp.sum(gated_mix * gated_mix, axis=1), 'ch')  20.7 us
    all_to_all x1, waiting for transfers between devices, on_device(): got = lax.all_to_all(back, 'seq', 0, 0, tiled=True)  9.63 us
    all_to_all x1, starting transfers between devices, on_device(): got = lax.all_to_all(back, 'seq', 0, 0, tiled=True)  5.94 us
    unnamed x25, local copies, waits for them, and re-layouts  3.02 us
    all_to_all x2, other arithmetic, on_device(): recv = lax.all_to_all(send, 'seq', 0, 0, tiled=True)  2.93 us
    dot_general x1, matrix products, on_device(): jnp.einsum('qfb,bk->qfk', spec, ofwd, precision=HIGHEST, preferred_elemen...  1.49 us
  transfers between devices with their start and end apart: 1, of which 1 were waited for; matrix products, arithmetic and copies ran while one was open for 0% of the time, Pallas kernels for 0%

profile of v1, /device:TPU:1, one launch (start us, length us, event | category | flops | bytes accessed | tf_op | source)
XLA Modules:
  0.0 74.0 jit_solution(5732633215002907503)
XLA Ops:
  0.0 1.0 %copy.23 = bf16[256,128]{0,1:T(8,128)(2,1)S(1)} copy(bf16[256,128]{1,0:T(8,128)(2,1)} %param.13) | data formatting | bytes 131072 | tf_op args[0]
  1.1 0.9 %broadcast_select_fusion = bf16[256,128]{1,0:T(8,128)(2,1)S(1)} fusion(bf16[256,128]{1,0:T(8,128)(2,1)} %param.16, pred[256]{0:T(512)(128)(4,1)S(1)} %add_compare_fusion), kind=kLoop, calls=%fused_computation.22 | loop fusion | flops 32768 | bytes 131328 | tf_op jit(solution)/shard_map/jit(_where)/select_n | solution.py:63
  2.2 0.9 %copy.24 = bf16[256,128]{0,1:T(8,128)(2,1)S(1)} copy(bf16[256,128]{1,0:T(8,128)(2,1)} %param.15) | data formatting | bytes 131072 | tf_op args[2]
  3.1 0.3 maximum_bitcast_fusion
  3.6 0.1 all_to_all.16
  3.8 0.5 broadcast.18
  4.3 1.8 %reduce.2 = bf16[64,1536]{1,0:T(8,128)(2,1)S(1)} reduce(bf16[64,1,1536]{2,1,0:T(2,128)(2,1)S(1)} %all_to_all.16, bf16[]{:T(256)} %broadcast.18), dimensions={1}, to_apply=%all_to_all.16.reduce_sub_computation | reduce | bytes 393218 | tf_op jit(solution)/shard_map/all_to_all | solution.py:81
  6.1 22.8 %all_to_all.20 = bf16[64,2,768]{2,1,0:T(2,128)(2,1)S(1)} all-to-all(bf16[64,2,768]{2,1,0:T(2,128)(2,1)S(1)} %reshape.58), channel_id=1, replica_groups=mesh['seq'=64,'ch'=8] {'seq'}, dimensions={0} | all-to-all | bytes 393216 | tf_op jit(solution)/shard_map/all_to_all | solution.py:81
  28.9 0.1 reshape.59
  29.0 1.1 %reduce = bf16[64,1536]{1,0:T(8,128)(2,1)S(1)} reduce(bf16[64,1,1536]{2,1,0:T(2,128)(2,1)S(1)} %reshape.59, bf16[]{:T(256)} %constant.45), dimensions={1}, to_apply=%all_to_all.13.reduce_sub_computation | reduce | bytes 393218 | tf_op jit(solution)/shard_map/all_to_all | solution.py:81
  30.2 0.3 fusion
  30.6 1.5 %fusion.11 = f32[6,528,256]{2,1,0:T(8,128)S(1)} fusion(bf16[6,528,64]{1,2,0:T(8,128)(2,1)S(1)} %fusion, f32[64,256,1]{1,0,2:T(8,128)S(1)} %copy-done.7), kind=kOutput, calls=%fused_computation.28 | convolution fusion | flops 622854144 | bytes 3715072 | tf_op jit(solution)/shard_map/qfb,bk->qfk/dot_general | solution.py:86
  32.1 0.2 slice_add_fusion
  32.3 0.7 copy-done.2
  33.0 0.2 multiply_subtract_fusion
  33.3 0.7 fusion.2
  34.1 0.7 fusion.1
  34.8 0.5 convolution_bitcast_fusion
  35.5 0.8 %all_to_all.17 = f32[64,1,512]{2,1,0:T(1,128)} reshape(f32[64,2,256]{2,1,0:T(2,128)S(1)} %copy.29) | data formatting | bytes 262144 | tf_op jit(solution)/shard_map/all_to_all | solution.py:107
  36.3 5.9 %all-to-all-start.1 = ((f32[64,1,512]{2,1,0:T(1,128)}), f32[64,1,512]{2,1,0:T(1,128)S(1)}, u32[]{:S(2)}, u32[]{:S(2)}) async-start(f32[64,1,512]{2,1,0:T(1,128)} %all_to_all.17), calls=%async_computation.1 | async-start | bytes 262144 | tf_op jit(solution)/shard_map/all_to_all | solution.py:107
  42.4 9.6 %all-to-all-done.1 = f32[64,1,512]{2,1,0:T(1,128)S(1)} async-done(((f32[64,1,512]{2,1,0:T(1,128)}), f32[64,1,512]{2,1,0:T(1,128)S(1)}, u32[]{:S(2)}, u32[]{:S(2)}) %all-to-all-start.1) | async-done | bytes 131104 | tf_op jit(solution)/shard_map/all_to_all | solution.py:107
  52.0 0.3 reduce.1
  52.5 20.7 %psum.7 = f32[256]{0:T(256)S(1)} all-reduce(f32[256]{0:T(256)S(1)} %multiply_reduce_fusion), channel_id=1, replica_groups=mesh['seq'=64,'ch'=8] {'ch'}, use_global_device_ids=true, to_apply=%region_1.2 | all-reduce | flops 256 | bytes 2048 | tf_op jit(solution)/shard_map/psum | solution.py:111
  73.3 0.7 copy.32
  (33 shorter events, 1.1 us)
Async XLA Ops:
  0.0 30.2 %copy-start.1 = (bf16[528,256,1]{1,0,2:T(8,128)(2,1)S(1)}, bf16[528,256,1]{1,0,2:T(8,128)(2,1)}, u32[]{:S(2)}) copy-start(bf16[528,256,1]{1,0,2:T(8,128)(2,1)} %constant.40) | copy-start | bytes 811012
  0.0 30.6 %copy-start.7 = (f32[64,256,1]{1,0,2:T(8,128)S(1)}, f32[64,256,1]{1,0,2:T(8,128)}, u32[]{:S(2)}) copy-start(f32[64,256,1]{1,0,2:T(8,128)} %constant.41) | copy-start | bytes 196612
  32.1 0.9 %copy-start.2 = (f32[264,128]{1,0:T(8,128)S(1)}, f32[264,128]{1,0:T(8,128)}, u32[]{:S(2)}) copy-start(f32[264,128]{1,0:T(8,128)} %constant.38.clone) | copy-start | bytes 405508
  32.1 1.0 %copy-start.3 = (f32[264,128]{1,0:T(8,128)S(1)}, f32[264,128]{1,0:T(8,128)}, u32[]{:S(2)}) copy-start(f32[264,128]{1,0:T(8,128)} %constant.39.clone) | copy-start | bytes 405508
  32.3 1.1 %copy-start.5 = (f32[256,64,1]{0,1,2:T(8,128)S(1)}, f32[256,64,1]{0,1,2:T(8,128)}, u32[]{:S(2)}) copy-start(f32[256,64,1]{0,1,2:T(8,128)} %constant.42) | copy-start | bytes 196612
  32.3 1.8 %copy-start.4 = (f32[256,64,1]{0,1,2:T(8,128)S(1)}, f32[256,64,1]{0,1,2:T(8,128)}, u32[]{:S(2)}) copy-start(f32[256,64,1]{0,1,2:T(8,128)} %constant.43) | copy-start | bytes 196612
  32.3 2.5 %copy-start = (f32[256,528,1]{0,1,2:T(8,128)S(1)}, f32[256,528,1]{0,1,2:T(8,128)}, u32[]{:S(2)}) copy-start(f32[256,528,1]{0,1,2:T(8,128)} %constant.44) | copy-start | bytes 1622020
  33.0 9.2 %copy-start.6 = (bf16[256,128]{1,0:T(8,128)(2,1)S(1)}, bf16[256,128]{1,0:T(8,128)(2,1)}, u32[]{:S(2)}) copy-start(bf16[256,128]{1,0:T(8,128)(2,1)} %param.14) | copy-start | bytes 196612
  33.2 19.1 %copy-start.8 = (f32[128]{0:T(128)S(1)}, f32[128]{0:T(128)}, u32[]{:S(2)}) copy-start(f32[128]{0:T(128)} %param.17) | copy-start | bytes 1540
  33.2 39.9 %copy-start.9 = (f32[128]{0:T(128)S(1)}, f32[128]{0:T(128)}, u32[]{:S(2)}) copy-start(f32[128]{0:T(128)} %param.18) | copy-start | bytes 1540
  36.3 15.7 %all-to-all-start.1 = ((f32[64,1,512]{2,1,0:T(1,128)}), f32[64,1,512]{2,1,0:T(1,128)S(1)}, u32[]{:S(2)}, u32[]{:S(2)}) async-start(f32[64,1,512]{2,1,0:T(1,128)} %all_to_all.17), calls=%async_computation.1 | async-start | bytes 262144 | tf_op jit(solution)/shard_map/all_to_all | solution.py:107

commit v2 on v1

--- a/solution.py
+++ b/solution.py
@@ -108,7 +108,8 @@
     convolved = got.reshape(blocks * per, rows_dev).T
 
     gated_mix = gate_values.astype(f32) * (convolved + skip_gain[None, :] * inputs.astype(f32))
-    squares = lax.psum(jnp.sum(gated_mix * gated_mix, axis=1), "ch")
+    partial = jnp.sum(gated_mix * gated_mix, axis=1)
+    squares = jnp.sum(lax.all_gather(partial, "ch", axis=0, tiled=False), axis=0)
     inv_norm = lax.rsqrt(squares / D + 1e-06)
     return (norm_gain[None, :] * gated_mix * inv_norm[:, None]).astype(jnp.bfloat16)
 

time: 74.3 us -> 73 us (0.983)
  blocking collectives: 43.4 us -> 42.1 us
    psum x1 -> x0, blocking collectives: 20.7 us -> none  [on_device(): squares = lax.psum(jnp.sum(gated_mix * gated_mix, axis=1), 'ch')]
    all_gather x0 -> x1, blocking collectives: none -> 19.3 us  [on_device(): lax.all_gather(partial, 'ch', axis=0, tiled=False)]
where the time goes in v2:
time: 73 us; the launch traced here: 72.7 us
  blocking collectives  42.1 us (58%)
  waiting for transfers between devices  9.63 us (13%)
  starting transfers between devices  5.94 us (8%)
  local copies, waits for them, and re-layouts  5.73 us (8%)
  other arithmetic  5.19 us (7%)
  matrix products  3.82 us (5%)
    all_to_all x1, blocking collectives, on_device(): recv = lax.all_to_all(send, 'seq', 0, 0, tiled=True)  22.8 us
    all_gather x1, blocking collectives, on_device(): lax.all_gather(partial, 'ch', axis=0, tiled=False)  19.3 us
    all_to_all x1, waiting for transfers between devices, on_device(): got = lax.all_to_all(back, 'seq', 0, 0, tiled=True)  9.63 us
    all_to_all x1, starting transfers between devices, on_device(): got = lax.all_to_all(back, 'seq', 0, 0, tiled=True)  5.94 us
    unnamed x25, local copies, waits for them, and re-layouts  3.02 us
    all_to_all x2, other arithmetic, on_device(): recv = lax.all_to_all(send, 'seq', 0, 0, tiled=True)  2.93 us
    dot_general x1, matrix products, on_device(): jnp.einsum('qfb,bk->qfk', spec, ofwd, precision=HIGHEST, preferred_elemen...  1.49 us
  transfers between devices with their start and end apart: 1, of which 1 were waited for; matrix products, arithmetic and copies ran while one was open for 0% of the time, Pallas kernels for 0%

profile of v2, /device:TPU:1, one launch (start us, length us, event | category | flops | bytes accessed | tf_op | source)
XLA Modules:
  0.0 72.7 jit_solution(17783272990708882191)
XLA Ops:
  0.0 1.0 %copy.23 = bf16[256,128]{0,1:T(8,128)(2,1)S(1)} copy(bf16[256,128]{1,0:T(8,128)(2,1)} %param.13) | data formatting | bytes 131072 | tf_op args[0]
  1.1 0.9 %broadcast_select_fusion = bf16[256,128]{1,0:T(8,128)(2,1)S(1)} fusion(bf16[256,128]{1,0:T(8,128)(2,1)} %param.16, pred[256]{0:T(512)(128)(4,1)S(1)} %add_compare_fusion), kind=kLoop, calls=%fused_computation.22 | loop fusion | flops 32768 | bytes 131328 | tf_op jit(solution)/shard_map/jit(_where)/select_n | solution.py:63
  2.2 0.9 %copy.24 = bf16[256,128]{0,1:T(8,128)(2,1)S(1)} copy(bf16[256,128]{1,0:T(8,128)(2,1)} %param.15) | data formatting | bytes 131072 | tf_op args[2]
  3.1 0.3 maximum_bitcast_fusion
  3.6 0.1 all_to_all.16
  3.8 0.5 broadcast.25
  4.3 1.8 %reduce.3 = bf16[64,1536]{1,0:T(8,128)(2,1)S(1)} reduce(bf16[64,1,1536]{2,1,0:T(2,128)(2,1)S(1)} %all_to_all.16, bf16[]{:T(256)} %broadcast.25), dimensions={1}, to_apply=%all_to_all.16.reduce_sub_computation | reduce | bytes 393218 | tf_op jit(solution)/shard_map/all_to_all | solution.py:81
  6.1 22.8 %all_to_all.20 = bf16[64,2,768]{2,1,0:T(2,128)(2,1)S(1)} all-to-all(bf16[64,2,768]{2,1,0:T(2,128)(2,1)S(1)} %reshape.66), channel_id=1, replica_groups=mesh['seq'=64,'ch'=8] {'seq'}, dimensions={0} | all-to-all | bytes 393216 | tf_op jit(solution)/shard_map/all_to_all | solution.py:81
  28.9 0.1 reshape.67
  29.0 1.1 %reduce.1 = bf16[64,1536]{1,0:T(8,128)(2,1)S(1)} reduce(bf16[64,1,1536]{2,1,0:T(2,128)(2,1)S(1)} %reshape.67, bf16[]{:T(256)} %constant.45), dimensions={1}, to_apply=%all_to_all.13.reduce_sub_computation | reduce | bytes 393218 | tf_op jit(solution)/shard_map/all_to_all | solution.py:81
  30.2 0.3 fusion
  30.6 1.5 %fusion.11 = f32[6,528,256]{2,1,0:T(8,128)S(1)} fusion(bf16[6,528,64]{1,2,0:T(8,128)(2,1)S(1)} %fusion, f32[64,256,1]{1,0,2:T(8,128)S(1)} %copy-done.7), kind=kOutput, calls=%fused_computation.28 | convolution fusion | flops 622854144 | bytes 3715072 | tf_op jit(solution)/shard_map/qfb,bk->qfk/dot_general | solution.py:86
  32.1 0.2 slice_add_fusion
  32.3 0.7 copy-done.2
  33.0 0.2 multiply_subtract_fusion
  33.3 0.7 %fusion.2 = f32[2,264,64]{1,2,0:T(8,128)S(1)} fusion(f32[256,64,1]{0,1,2:T(8,128)S(1)} %copy-done.5, f32[2,264,128]{2,1,0:T(8,128)S(1)} %multiply_add_fusion, f32[2,264,128]{2,1,0:T(8,128)S(1)} %get-tuple-element.5), kind=kOutput, calls=%fused_computation.7 | convolution fusion | flops 103944192 | bytes 741376 | tf_op jit(solution)/shard_map/cfk,ki->cfi/dot_general | solution.py:101
  34.1 0.7 %fusion.1 = f32[2,264,64]{1,2,0:T(8,128)S(1)} fusion(f32[256,64,1]{0,1,2:T(8,128)S(1)} %copy-done.4, f32[2,264,128]{2,1,0:T(8,128)S(1)} %multiply_add_fusion, f32[2,264,128]{2,1,0:T(8,128)S(1)} %get-tuple-element.5), kind=kOutput, calls=%fused_computation.6 | convolution fusion | flops 103944192 | bytes 741376 | tf_op jit(solution)/shard_map/cfk,ki->cfi/dot_general | solution.py:102
  34.8 0.5 convolution_bitcast_fusion
  35.5 0.8 %all_to_all.17 = f32[64,1,512]{2,1,0:T(1,128)} reshape(f32[64,2,256]{2,1,0:T(2,128)S(1)} %copy.29) | data formatting | bytes 262144 | tf_op jit(solution)/shard_map/all_to_all | solution.py:107
  36.3 5.9 %all-to-all-start.1 = ((f32[64,1,512]{2,1,0:T(1,128)}), f32[64,1,512]{2,1,0:T(1,128)S(1)}, u32[]{:S(2)}, u32[]{:S(2)}) async-start(f32[64,1,512]{2,1,0:T(1,128)} %all_to_all.17), calls=%async_computation.1 | async-start | bytes 262144 | tf_op jit(solution)/shard_map/all_to_all | solution.py:107
  42.4 9.6 %all-to-all-done.1 = f32[64,1,512]{2,1,0:T(1,128)S(1)} async-done(((f32[64,1,512]{2,1,0:T(1,128)}), f32[64,1,512]{2,1,0:T(1,128)S(1)}, u32[]{:S(2)}, u32[]{:S(2)}) %all-to-all-start.1) | async-done | bytes 131104 | tf_op jit(solution)/shard_map/all_to_all | solution.py:107
  52.0 0.3 reduce.2
  52.5 19.3 %all-gather.1 = f32[8,1,256]{2,1,0:T(1,128)S(1)} all-gather(f32[1,1,256]{2,1,0:T(1,128)S(1)} %bitcast.40), channel_id=2, replica_groups=mesh['seq'=64,'ch'=8] {'ch'}, dimensions={0}, use_global_device_ids=true | all-gather | bytes 9216 | tf_op jit(solution)/shard_map/all_gather | solution.py:112
  72.0 0.7 %copy.32 = bf16[256,128]{1,0:T(8,128)(2,1)} copy(bf16[256,128]{0,1:T(8,128)(2,1)S(1)} %multiply_convert_fusion) | data formatting | bytes 131072 | tf_op jit(solution)/shard_map/convert_element_type | solution.py:114
  (34 shorter events, 1.1 us)
Async XLA Ops:
  0.0 30.2 %copy-start.1 = (bf16[528,256,1]{1,0,2:T(8,128)(2,1)S(1)}, bf16[528,256,1]{1,0,2:T(8,128)(2,1)}, u32[]{:S(2)}) copy-start(bf16[528,256,1]{1,0,2:T(8,128)(2,1)} %constant.40) | copy-start | bytes 811012
  0.0 30.6 %copy-start.7 = (f32[64,256,1]{1,0,2:T(8,128)S(1)}, f32[64,256,1]{1,0,2:T(8,128)}, u32[]{:S(2)}) copy-start(f32[64,256,1]{1,0,2:T(8,128)} %constant.41) | copy-start | bytes 196612
  32.1 0.9 %copy-start.2 = (f32[264,128]{1,0:T(8,128)S(1)}, f32[264,128]{1,0:T(8,128)}, u32[]{:S(2)}) copy-start(f32[264,128]{1,0:T(8,128)} %constant.38.clone) | copy-start | bytes 405508
  32.1 1.0 %copy-start.3 = (f32[264,128]{1,0:T(8,128)S(1)}, f32[264,128]{1,0:T(8,128)}, u32[]{:S(2)}) copy-start(f32[264,128]{1,0:T(8,128)} %constant.39.clone) | copy-start | bytes 405508
  32.3 1.1 %copy-start.5 = (f32[256,64,1]{0,1,2:T(8,128)S(1)}, f32[256,64,1]{0,1,2:T(8,128)}, u32[]{:S(2)}) copy-start(f32[256,64,1]{0,1,2:T(8,128)} %constant.42) | copy-start | bytes 196612
  32.3 1.8 %copy-start.4 = (f32[256,64,1]{0,1,2:T(8,128)S(1)}, f32[256,64,1]{0,1,2:T(8,128)}, u32[]{:S(2)}) copy-start(f32[256,64,1]{0,1,2:T(8,128)} %constant.43) | copy-start | bytes 196612
  32.3 2.5 %copy-start = (f32[256,528,1]{0,1,2:T(8,128)S(1)}, f32[256,528,1]{0,1,2:T(8,128)}, u32[]{:S(2)}) copy-start(f32[256,528,1]{0,1,2:T(8,128)} %constant.44) | copy-start | bytes 1622020
  33.0 9.2 %copy-start.6 = (bf16[256,128]{1,0:T(8,128)(2,1)S(1)}, bf16[256,128]{1,0:T(8,128)(2,1)}, u32[]{:S(2)}) copy-start(bf16[256,128]{1,0:T(8,128)(2,1)} %param.14) | copy-start | bytes 196612
  33.2 19.1 %copy-start.8 = (f32[128]{0:T(128)S(1)}, f32[128]{0:T(128)}, u32[]{:S(2)}) copy-start(f32[128]{0:T(128)} %param.17) | copy-start | bytes 1540
  33.2 38.6 %copy-start.9 = (f32[128]{0:T(128)S(1)}, f32[128]{0:T(128)}, u32[]{:S(2)}) copy-start(f32[128]{0:T(128)} %param.18) | copy-start | bytes 1540
  36.3 15.7 %all-to-all-start.1 = ((f32[64,1,512]{2,1,0:T(1,128)}), f32[64,1,512]{2,1,0:T(1,128)S(1)}, u32[]{:S(2)}, u32[]{:S(2)}) async-start(f32[64,1,512]{2,1,0:T(1,128)} %all_to_all.17), calls=%async_computation.1 | async-start | bytes 262144 | tf_op jit(solution)/shard_map/all_to_all | solution.py:107

commit v3 on v2

--- a/solution.py
+++ b/solution.py
@@ -59,8 +59,6 @@
     size = 2 * blocks
     f32 = jnp.float32
     own_index = lax.axis_index("seq")
-    row_ids = lax.broadcasted_iota(jnp.int32, (rows_dev, 1), 0) + own_index * rows_dev
-    anti_masked = jnp.where(row_ids > 0, anti_filter, jnp.zeros_like(anti_filter))
 
     fp, fwd_np, inv_np = inner_tables(rows_dev)
     ofwd_np, oinv_re_np, oinv_im_np, sh_re_np, sh_im_np = outer_tables(blocks, fp)
@@ -72,16 +70,23 @@
     sh_re = jnp.asarray(sh_re_np, f32)
     sh_im = jnp.asarray(sh_im_np, f32)
 
-    stacked = jnp.stack([inputs, causal_filter, anti_masked])
+    stacked = jnp.stack([inputs, causal_filter, anti_filter, gate_values])
+    lanes = 128
     send = (
-        stacked.reshape(3, rows_dev, blocks, per)
+        stacked.reshape(4, rows_dev, blocks, per)
         .transpose(2, 0, 3, 1)
-        .reshape(blocks, 3 * per * rows_dev)
+        .reshape(blocks, 4 * per * rows_dev // lanes, lanes)
     )
     recv = lax.all_to_all(send, "seq", 0, 0, tiled=True)
-    series = recv.reshape(blocks, 3 * per, rows_dev).transpose(1, 0, 2)
+    series = recv.reshape(blocks, 4, per, rows_dev)
+    block_ids = lax.broadcasted_iota(jnp.int32, (blocks, 1, rows_dev), 0)
+    tok_ids = lax.broadcasted_iota(jnp.int32, (blocks, 1, rows_dev), 2)
+    first_row = jnp.logical_and(block_ids == 0, tok_ids == 0)
+    anti_rows = jnp.where(first_row, jnp.zeros_like(series[:, 2]), series[:, 2])
+    conv_in = jnp.stack([series[:, 0], series[:, 1], anti_rows], axis=1)
+    conv_in = conv_in.reshape(blocks, 3 * per, rows_dev).transpose(1, 0, 2)
 
-    spec = jnp.einsum("fn,qbn->qfb", fwd, series, preferred_element_type=f32)
+    spec = jnp.einsum("fn,qbn->qfb", fwd, conv_in, preferred_element_type=f32)
     spec = spec.astype(jnp.bfloat16).astype(f32)
     z = jnp.einsum("qfb,bk->qfk", spec, ofwd, precision=HIGHEST, preferred_element_type=f32)
     z_re, z_im = z[:, :fp], z[:, fp:]
@@ -101,13 +106,16 @@
     t_re = jnp.einsum("cfk,ki->cfi", y_cat, oinv_re, precision=HIGHEST, preferred_element_type=f32)
     t_im = jnp.einsum("cfk,ki->cfi", y_cat, oinv_im, precision=HIGHEST, preferred_element_type=f32)
     total = jnp.concatenate([t_re, t_im], axis=1)
-    conv_t = jnp.einsum("cfi,tf->cit", total, inv, precision=HIGHEST, preferred_element_type=f32)
+    conv_t = jnp.einsum("cfi,tf->ict", total, inv, precision=HIGHEST, preferred_element_type=f32)
 
-    back = conv_t.transpose(1, 0, 2).reshape(blocks, per * rows_dev)
+    skip_here = lax.dynamic_slice_in_dim(skip_gain, own_index * per, per)
+    mixed_local = series[:, 3].astype(f32) * (
+        conv_t + skip_here[None, :, None] * series[:, 0].astype(f32)
+    )
+    back = mixed_local.reshape(blocks, per * rows_dev // lanes, lanes)
     got = lax.all_to_all(back, "seq", 0, 0, tiled=True)
-    convolved = got.reshape(blocks * per, rows_dev).T
+    gated_mix = got.reshape(blocks * per, rows_dev).T
 
-    gated_mix = gate_values.astype(f32) * (convolved + skip_gain[None, :] * inputs.astype(f32))
     partial = jnp.sum(gated_mix * gated_mix, axis=1)
     squares = jnp.sum(lax.all_gather(partial, "ch", axis=0, tiled=False), axis=0)
     inv_norm = lax.rsqrt(squares / D + 1e-06)

time: 73 us -> 72.3 us (level)
  blocking collectives: 42.1 us -> 35.1 us
  starting transfers between devices: 5.94 us -> 12.9 us
  other arithmetic: 5.19 us -> 1.61 us
  local copies, waits for them, and re-layouts: 5.73 us -> 7.83 us
    all_to_all x1, blocking collectives: 22.8 us -> 15.8 us  [on_device(): got = lax.all_to_all(back, 'seq', 0, 0, tiled=True)]
    all_to_all x1, starting transfers between devices: 5.94 us -> 12.9 us  [on_device(): recv = lax.all_to_all(send, 'seq', 0, 0, tiled=True)]
    all_to_all x3 -> x0, other arithmetic: 3.24 us -> none  [the longest x2 2.93 us: on_device(): recv = lax.all_to_all(send, 'seq', 0, 0, tiled=True)]
    unnamed x25 -> x20, local copies, waits for them, and re-layouts: 3.02 us -> 4.59 us
    all_to_all x3 -> x0, local copies, waits for them, and re-layouts: 1.49 us -> none  [the longest x1 0.83 us: on_device(): got = lax.all_to_all(back, 'seq', 0, 0, tiled=True)]
    reshape x1 -> x4, local copies, waits for them, and re-layouts: 0.02 us -> 1.23 us  [the longest x1 0.87 us: on_device(): send = stacked.reshape(4, rows_dev, blocks, per).transpose(2, 0, 3, 1).re...]
    select_n x1 -> x0, other arithmetic: 0.94 us -> none  [on_device(): jnp.where(row_ids > 0, anti_filter, jnp.zeros_like(anti_filter))]
    dynamic_slice x0 -> x1, local copies, waits for them, and re-layouts: none -> 0.73 us  [on_device(): skip_here = lax.dynamic_slice_in_dim(skip_gain, own_index * per, per)]
  transfers between devices with their start and end apart: 1 -> 1, of which waited for: 1 -> 1; matrix products, arithmetic and copies ran while one was open for 0% -> 1% of each run, Pallas kernels for 0% -> 0%
where the time goes in v3:
time: 72.3 us; the launch traced here: 71.9 us
  blocking collectives  35.1 us (49%)
  starting transfers between devices  12.9 us (18%)
  waiting for transfers between devices  10.3 us (14%)
  local copies, waits for them, and re-layouts  7.83 us (11%)
  matrix products  3.82 us (5%)
  other arithmetic  1.61 us (2%)
    all_gather x1, blocking collectives, on_device(): lax.all_gather(partial, 'ch', axis=0, tiled=False)  19.4 us
    all_to_all x1, blocking collectives, on_device(): got = lax.all_to_all(back, 'seq', 0, 0, tiled=True)  15.8 us
    all_to_all x1, starting transfers between devices, on_device(): recv = lax.all_to_all(send, 'seq', 0, 0, tiled=True)  12.9 us
    all_to_all x1, waiting for transfers between devices, on_device(): recv = lax.all_to_all(send, 'seq', 0, 0, tiled=True)  10.3 us
    unnamed x20, local copies, waits for them, and re-layouts  4.59 us
    dot_general x1, matrix products, on_device(): jnp.einsum('qfb,bk->qfk', spec, ofwd, precision=HIGHEST, preferred_elemen...  1.49 us
  transfers between devices with their start and end apart: 1, of which 1 were waited for; matrix products, arithmetic and copies ran while one was open for 1% of the time, Pallas kernels for 0%

profile of v3, /device:TPU:1, one launch (start us, length us, event | category | flops | bytes accessed | tf_op | source)
XLA Modules:
  0.0 71.9 jit_solution(18167749390152663706)
XLA Ops:
  0.0 1.0 %copy.33 = bf16[256,128]{0,1:T(8,128)(2,1)S(1)} copy(bf16[256,128]{1,0:T(8,128)(2,1)} %param.13) | data formatting | bytes 131072 | tf_op args[0]
  1.0 0.9 %copy.34 = bf16[256,128]{0,1:T(8,128)(2,1)S(1)} copy(bf16[256,128]{1,0:T(8,128)(2,1)} %param.15) | data formatting | bytes 131072 | tf_op args[2]
  2.0 0.9 %copy.35 = bf16[256,128]{0,1:T(8,128)(2,1)S(1)} copy(bf16[256,128]{1,0:T(8,128)(2,1)} %param.16) | data formatting | bytes 131072 | tf_op args[3]
  3.0 0.9 %copy.36 = bf16[256,128]{0,1:T(8,128)(2,1)S(1)} copy(bf16[256,128]{1,0:T(8,128)(2,1)} %param.14) | data formatting | bytes 131072 | tf_op args[1]
  4.0 0.5 maximum_bitcast_fusion
  4.5 0.2 copy.37
  4.7 0.9 %reshape.71 = bf16[64,16,128]{2,1,0:T(8,128)(2,1)} reshape(bf16[64,4,2,256]{3,2,1,0:T(2,128)(2,1)S(1)} %copy.37) | data formatting | bytes 524288 | tf_op jit(solution)/shard_map/reshape | solution.py:78
  5.5 12.9 %all-to-all-start = ((bf16[64,16,128]{2,1,0:T(8,128)(2,1)}), bf16[64,16,128]{2,1,0:T(8,128)(2,1)S(1)}, u32[]{:S(2)}, u32[]{:S(2)}) async-start(bf16[64,16,128]{2,1,0:T(8,128)(2,1)} %reshape.71), calls=%async_computation | async-start | bytes 524288 | tf_op jit(solution)/shard_map/all_to_all | solution.py:80
  18.5 0.7 %dynamic_slice.3 = f32[2]{0:T(128)S(1)} dynamic-slice(f32[128]{0:T(128)} %param.17, s32[]{:T(128)S(6)} %select_n.9), dynamic_slice_sizes={2} | dynamic-slice | bytes 20 | tf_op jit(solution)/shard_map/dynamic_slice | solution.py:111
  19.3 10.3 %all-to-all-done = bf16[64,16,128]{2,1,0:T(8,128)(2,1)S(1)} async-done(((bf16[64,16,128]{2,1,0:T(8,128)(2,1)}), bf16[64,16,128]{2,1,0:T(8,128)(2,1)S(1)}, u32[]{:S(2)}, u32[]{:S(2)}) %all-to-all-start) | async-done | bytes 262176 | tf_op jit(solution)/shard_map/all_to_all | solution.py:80
  29.6 0.2 reshape.72
  29.9 0.2 fusion.12
  30.1 0.3 pad_maximum_fusion.3
  30.4 0.3 fusion
  30.8 1.5 %fusion.13 = f32[6,528,256]{2,1,0:T(8,128)S(1)} fusion(bf16[6,528,64]{1,2,0:T(8,128)(2,1)S(1)} %fusion, f32[64,256,1]{1,0,2:T(8,128)S(1)} %copy-done.6), kind=kOutput, calls=%fused_computation.34 | convolution fusion | flops 622854144 | bytes 3715072 | tf_op jit(solution)/shard_map/qfb,bk->qfk/dot_general | solution.py:91
  32.3 0.2 slice_add_fusion
  32.5 0.7 copy-done.2
  33.2 0.2 multiply_subtract_fusion
  33.5 0.7 %fusion.4 = f32[2,264,64]{1,2,0:T(8,128)S(1)} fusion(f32[256,64,1]{0,1,2:T(8,128)S(1)} %copy-done.5, f32[2,264,128]{2,1,0:T(8,128)S(1)} %multiply_add_fusion, f32[2,264,128]{2,1,0:T(8,128)S(1)} %get-tuple-element.5), kind=kOutput, calls=%fused_computation.9 | convolution fusion | flops 103944192 | bytes 741376 | tf_op jit(solution)/shard_map/cfk,ki->cfi/dot_general | solution.py:106
  34.3 0.7 %fusion.3 = f32[2,264,64]{1,2,0:T(8,128)S(1)} fusion(f32[256,64,1]{0,1,2:T(8,128)S(1)} %copy-done.4, f32[2,264,128]{2,1,0:T(8,128)S(1)} %multiply_add_fusion, f32[2,264,128]{2,1,0:T(8,128)S(1)} %get-tuple-element.5), kind=kOutput, calls=%fused_computation.8 | convolution fusion | flops 103944192 | bytes 741376 | tf_op jit(solution)/shard_map/cfk,ki->cfi/dot_general | solution.py:107
  35.0 0.5 fusion.2
  35.8 15.8 %all_to_all.10 = f32[64,4,128]{2,1,0:T(4,128)S(1)} all-to-all(f32[64,4,128]{2,1,0:T(4,128)S(1)} %reshape.74), channel_id=1, replica_groups=mesh['seq'=64,'ch'=8] {'seq'}, dimensions={0} | all-to-all | bytes 262144 | tf_op jit(solution)/shard_map/all_to_all | solution.py:116
  51.6 19.4 %all-gather.1 = f32[8,1,256]{2,1,0:T(1,128)S(1)} all-gather(f32[1,1,256]{2,1,0:T(1,128)S(1)} %bitcast.47), channel_id=2, replica_groups=mesh['seq'=64,'ch'=8] {'ch'}, dimensions={0}, use_global_device_ids=true | all-gather | bytes 9216 | tf_op jit(solution)/shard_map/all_gather | solution.py:120
  71.2 0.7 %copy.42 = bf16[256,128]{1,0:T(8,128)(2,1)} copy(bf16[256,128]{0,1:T(8,128)(2,1)S(1)} %fusion.8) | data formatting | bytes 131072 | tf_op jit(solution)/shard_map/convert_element_type | solution.py:122
  (32 shorter events, 1.0 us)
Async XLA Ops:
  0.0 30.4 %copy-start.1 = (bf16[528,256,1]{1,0,2:T(8,128)(2,1)S(1)}, bf16[528,256,1]{1,0,2:T(8,128)(2,1)}, u32[]{:S(2)}) copy-start(bf16[528,256,1]{1,0,2:T(8,128)(2,1)} %constant.43) | copy-start | bytes 811012
  0.0 30.7 %copy-start.6 = (f32[64,256,1]{1,0,2:T(8,128)S(1)}, f32[64,256,1]{1,0,2:T(8,128)}, u32[]{:S(2)}) copy-start(f32[64,256,1]{1,0,2:T(8,128)} %constant.44) | copy-start | bytes 196612
  5.5 24.1 %all-to-all-start = ((bf16[64,16,128]{2,1,0:T(8,128)(2,1)}), bf16[64,16,128]{2,1,0:T(8,128)(2,1)S(1)}, u32[]{:S(2)}, u32[]{:S(2)}) async-start(bf16[64,16,128]{2,1,0:T(8,128)(2,1)} %reshape.71), calls=%async_computation | async-start | bytes 524288 | tf_op jit(solution)/shard_map/all_to_all | solution.py:80
  32.3 0.9 %copy-start.2 = (f32[264,128]{1,0:T(8,128)S(1)}, f32[264,128]{1,0:T(8,128)}, u32[]{:S(2)}) copy-start(f32[264,128]{1,0:T(8,128)} %constant.41.clone) | copy-start | bytes 405508
  32.3 1.0 %copy-start.3 = (f32[264,128]{1,0:T(8,128)S(1)}, f32[264,128]{1,0:T(8,128)}, u32[]{:S(2)}) copy-start(f32[264,128]{1,0:T(8,128)} %constant.42.clone) | copy-start | bytes 405508
  32.4 1.1 %copy-start.5 = (f32[256,64,1]{0,1,2:T(8,128)S(1)}, f32[256,64,1]{0,1,2:T(8,128)}, u32[]{:S(2)}) copy-start(f32[256,64,1]{0,1,2:T(8,128)} %constant.45) | copy-start | bytes 196612
  32.5 1.8 %copy-start.4 = (f32[256,64,1]{0,1,2:T(8,128)S(1)}, f32[256,64,1]{0,1,2:T(8,128)}, u32[]{:S(2)}) copy-start(f32[256,64,1]{0,1,2:T(8,128)} %constant.46) | copy-start | bytes 196612
  32.5 2.5 %copy-start = (f32[256,528,1]{0,1,2:T(8,128)S(1)}, f32[256,528,1]{0,1,2:T(8,128)}, u32[]{:S(2)}) copy-start(f32[256,528,1]{0,1,2:T(8,128)} %constant.47) | copy-start | bytes 1622020
  33.4 37.6 %copy-start.7 = (f32[128]{0:T(128)S(1)}, f32[128]{0:T(128)}, u32[]{:S(2)}) copy-start(f32[128]{0:T(128)} %param.18) | copy-start | bytes 1540

commit v4 on v3

--- a/solution.py
+++ b/solution.py
@@ -72,13 +72,13 @@
 
     stacked = jnp.stack([inputs, causal_filter, anti_filter, gate_values])
     lanes = 128
-    send = (
-        stacked.reshape(4, rows_dev, blocks, per)
-        .transpose(2, 0, 3, 1)
-        .reshape(blocks, 4 * per * rows_dev // lanes, lanes)
-    )
+    eye_ch = jnp.eye(chan_dev, dtype=jnp.bfloat16)
+    by_channel = jnp.einsum(
+        "ck,atk->cat", eye_ch, stacked, preferred_element_type=f32
+    ).astype(jnp.bfloat16)
+    send = by_channel.reshape(blocks, per * 4 * rows_dev // lanes, lanes)
     recv = lax.all_to_all(send, "seq", 0, 0, tiled=True)
-    series = recv.reshape(blocks, 4, per, rows_dev)
+    series = recv.reshape(blocks, per, 4, rows_dev).transpose(0, 2, 1, 3)
     block_ids = lax.broadcasted_iota(jnp.int32, (blocks, 1, rows_dev), 0)
     tok_ids = lax.broadcasted_iota(jnp.int32, (blocks, 1, rows_dev), 2)
     first_row = jnp.logical_and(block_ids == 0, tok_ids == 0)
@@ -114,12 +114,16 @@
     )
     back = mixed_local.reshape(blocks, per * rows_dev // lanes, lanes)
     got = lax.all_to_all(back, "seq", 0, 0, tiled=True)
-    gated_mix = got.reshape(blocks * per, rows_dev).T
+    mix_t = got.reshape(blocks * per, rows_dev)
 
-    partial = jnp.sum(gated_mix * gated_mix, axis=1)
+    partial = jnp.sum(mix_t * mix_t, axis=0)
     squares = jnp.sum(lax.all_gather(partial, "ch", axis=0, tiled=False), axis=0)
     inv_norm = lax.rsqrt(squares / D + 1e-06)
-    return (norm_gain[None, :] * gated_mix * inv_norm[:, None]).astype(jnp.bfloat16)
+    out_t = (norm_gain[:, None] * mix_t * inv_norm[None, :]).astype(jnp.bfloat16)
+    eye_tok = jnp.eye(rows_dev, dtype=jnp.bfloat16)
+    return jnp.einsum("tk,ck->tc", eye_tok, out_t, preferred_element_type=f32).astype(
+        jnp.bfloat16
+    )
 
 
 def solution(mesh):

time: 72.3 us -> 68.4 us (0.946)
  local copies, waits for them, and re-layouts: 7.83 us -> 3.06 us
  matrix products: 3.82 us -> 5.93 us
  other arithmetic: 1.61 us -> 0.62 us
    unnamed x20 -> x16, local copies, waits for them, and re-layouts: 4.59 us -> 0.79 us
    dot_general x0 -> x2, matrix products: none -> 2.11 us  [the longest x1 1.21 us: on_device(): jnp.einsum('ck,atk->cat', eye_ch, stacked, preferred_element_type=f32)]
where the time goes in v4:
time: 68.4 us; the launch traced here: 68.2 us
  blocking collectives  35.1 us (51%)
  starting transfers between devices  12.9 us (19%)
  waiting for transfers between devices  10.3 us (15%)
  matrix products  5.93 us (9%)
  local copies, waits for them, and re-layouts  3.06 us (4%)
    all_gather x1, blocking collectives, on_device(): lax.all_gather(partial, 'ch', axis=0, tiled=False)  19.4 us
    all_to_all x1, blocking collectives, on_device(): got = lax.all_to_all(back, 'seq', 0, 0, tiled=True)  15.7 us
    all_to_all x1, starting transfers between devices, on_device(): recv = lax.all_to_all(send, 'seq', 0, 0, tiled=True)  12.9 us
    all_to_all x1, waiting for transfers between devices, on_device(): recv = lax.all_to_all(send, 'seq', 0, 0, tiled=True)  10.3 us
    dot_general x1, matrix products, on_device(): jnp.einsum('qfb,bk->qfk', spec, ofwd, precision=HIGHEST, preferred_elemen...  1.49 us
  transfers between devices with their start and end apart: 1, of which 1 were waited for; matrix products, arithmetic and copies ran while one was open for 1% of the time, Pallas kernels for 0%

profile of v4, /device:TPU:1, one launch (start us, length us, event | category | flops | bytes accessed | tf_op | source)
XLA Modules:
  0.0 68.2 jit_solution(17379166657644568904)
XLA Ops:
  0.0 1.2 %convolution_convert_fusion.1 = bf16[128,4,256]{2,0,1:T(8,128)(2,1)S(1)} fusion(bf16[1,256,128]{2,1,0:T(8,128)(2,1)} %bitcast.49, bf16[1,256,128]{2,1,0:T(8,128)(2,1)} %bitcast.50, bf16[1,256,128]{2,1,0:T(8,128)(2,1)} %bitcast.51, bf16[1,256,128]{2,1,0:T(8,128)(2,1)} %bitcast.52), kind=kOutput, calls=%fused_computation.2 | convolution fusion | flops 34750464 | bytes 524288 | tf_op jit(solution)/shard_map/ck,atk->cat/dot_general | solution.py:76
  1.2 0.2 copy.17
  1.4 0.8 %reshape.62 = bf16[64,16,128]{2,1,0:T(8,128)(2,1)} reshape(bf16[128,4,256]{2,1,0:T(4,128)(2,1)S(1)} %copy.17) | data formatting | bytes 524288 | tf_op jit(solution)/shard_map/reshape | solution.py:79
  2.2 12.9 %all-to-all-start = ((bf16[64,16,128]{2,1,0:T(8,128)(2,1)}), bf16[64,16,128]{2,1,0:T(8,128)(2,1)S(1)}, u32[]{:S(2)}, u32[]{:S(2)}) async-start(bf16[64,16,128]{2,1,0:T(8,128)(2,1)} %reshape.62), calls=%async_computation | async-start | bytes 524288 | tf_op jit(solution)/shard_map/all_to_all | solution.py:80
  15.2 0.7 %dynamic_slice.3 = f32[2]{0:T(128)S(1)} dynamic-slice(f32[128]{0:T(128)} %param.17, s32[]{:T(128)S(6)} %select_n.9), dynamic_slice_sizes={2} | dynamic-slice | bytes 20 | tf_op jit(solution)/shard_map/dynamic_slice | solution.py:111
  15.9 0.1 broadcast_and_fusion
  16.0 10.3 %all-to-all-done = bf16[64,16,128]{2,1,0:T(8,128)(2,1)S(1)} async-done(((bf16[64,16,128]{2,1,0:T(8,128)(2,1)}), bf16[64,16,128]{2,1,0:T(8,128)(2,1)S(1)}, u32[]{:S(2)}, u32[]{:S(2)}) %all-to-all-start) | async-done | bytes 262176 | tf_op jit(solution)/shard_map/all_to_all | solution.py:80
  26.3 0.2 reshape.63
  26.6 0.3 fusion
  27.0 1.5 %fusion.23 = f32[6,528,256]{2,1,0:T(8,128)S(1)} fusion(bf16[6,528,64]{1,2,0:T(8,128)(2,1)S(1)} %fusion, f32[64,256,1]{1,0,2:T(8,128)S(1)} %copy-done.6), kind=kOutput, calls=%fused_computation.47 | convolution fusion | flops 622854144 | bytes 3715072 | tf_op jit(solution)/shard_map/qfb,bk->qfk/dot_general | solution.py:91
  28.5 0.2 slice_add_fusion
  28.7 0.7 copy-done.2
  29.4 0.1 copy-done.3
  29.5 0.2 multiply_subtract_fusion
  29.7 0.1 multiply_add_fusion
  29.8 0.7 %fusion.4 = f32[2,264,64]{1,2,0:T(8,128)S(1)} fusion(f32[256,64,1]{0,1,2:T(8,128)S(1)} %copy-done.5, f32[2,264,128]{2,1,0:T(8,128)S(1)} %multiply_add_fusion, f32[2,264,128]{2,1,0:T(8,128)S(1)} %get-tuple-element.5), kind=kOutput, calls=%fused_computation.11 | convolution fusion | flops 103944192 | bytes 741376 | tf_op jit(solution)/shard_map/cfk,ki->cfi/dot_general | solution.py:106
  30.5 0.7 %fusion.3 = f32[2,264,64]{1,2,0:T(8,128)S(1)} fusion(f32[256,64,1]{0,1,2:T(8,128)S(1)} %copy-done.4, f32[2,264,128]{2,1,0:T(8,128)S(1)} %multiply_add_fusion, f32[2,264,128]{2,1,0:T(8,128)S(1)} %get-tuple-element.5), kind=kOutput, calls=%fused_computation.10 | convolution fusion | flops 103944192 | bytes 741376 | tf_op jit(solution)/shard_map/cfk,ki->cfi/dot_general | solution.py:107
  31.2 0.5 fusion.2
  31.8 0.1 copy.19
  31.9 0.1 reshape.65
  32.0 15.7 %all_to_all.10 = f32[64,4,128]{2,1,0:T(4,128)S(1)} all-to-all(f32[64,4,128]{2,1,0:T(4,128)S(1)} %reshape.65), channel_id=1, replica_groups=mesh['seq'=64,'ch'=8] {'seq'}, dimensions={0} | all-to-all | bytes 262144 | tf_op jit(solution)/shard_map/all_to_all | solution.py:116
  47.8 0.1 reshape.66
  47.9 19.4 %all-gather.1 = f32[8,1,256]{2,1,0:T(1,128)S(1)} all-gather(f32[1,1,256]{2,1,0:T(1,128)S(1)} %bitcast.48), channel_id=2, replica_groups=mesh['seq'=64,'ch'=8] {'ch'}, dimensions={0}, use_global_device_ids=true | all-gather | bytes 9216 | tf_op jit(solution)/shard_map/all_gather | solution.py:120
  67.3 0.9 %convolution_convert_fusion.2 = bf16[256,128]{1,0:T(8,128)(2,1)} fusion(f32[128,256]{1,0:T(8,128)S(1)} %reshape.66, f32[256]{0:T(256)S(1)} %add_rsqrt_fusion, f32[128]{0:T(128)S(1)} %copy-done.7), kind=kOutput, calls=%fused_computation.6 | convolution fusion | flops 16973824 | bytes 198144 | tf_op jit(solution)/shard_map/tk,ck->tc/dot_general | solution.py:124
  (23 shorter events, 0.2 us)
Async XLA Ops:
  0.0 26.6 %copy-start.1 = (bf16[528,256,1]{1,0,2:T(8,128)(2,1)S(1)}, bf16[528,256,1]{1,0,2:T(8,128)(2,1)}, u32[]{:S(2)}) copy-start(bf16[528,256,1]{1,0,2:T(8,128)(2,1)} %constant.43) | copy-start | bytes 811012
  0.0 27.0 %copy-start.6 = (f32[64,256,1]{1,0,2:T(8,128)S(1)}, f32[64,256,1]{1,0,2:T(8,128)}, u32[]{:S(2)}) copy-start(f32[64,256,1]{1,0,2:T(8,128)} %constant.44) | copy-start | bytes 196612
  2.2 24.1 %all-to-all-start = ((bf16[64,16,128]{2,1,0:T(8,128)(2,1)}), bf16[64,16,128]{2,1,0:T(8,128)(2,1)S(1)}, u32[]{:S(2)}, u32[]{:S(2)}) async-start(bf16[64,16,128]{2,1,0:T(8,128)(2,1)} %reshape.62), calls=%async_computation | async-start | bytes 524288 | tf_op jit(solution)/shard_map/all_to_all | solution.py:80
  28.5 0.9 %copy-start.2 = (f32[264,128]{1,0:T(8,128)S(1)}, f32[264,128]{1,0:T(8,128)}, u32[]{:S(2)}) copy-start(f32[264,128]{1,0:T(8,128)} %constant.41.clone) | copy-start | bytes 405508
  28.5 1.0 %copy-start.3 = (f32[264,128]{1,0:T(8,128)S(1)}, f32[264,128]{1,0:T(8,128)}, u32[]{:S(2)}) copy-start(f32[264,128]{1,0:T(8,128)} %constant.42.clone) | copy-start | bytes 405508
  28.7 1.1 %copy-start.5 = (f32[256,64,1]{0,1,2:T(8,128)S(1)}, f32[256,64,1]{0,1,2:T(8,128)}, u32[]{:S(2)}) copy-start(f32[256,64,1]{0,1,2:T(8,128)} %constant.45) | copy-start | bytes 196612
  28.7 1.8 %copy-start.4 = (f32[256,64,1]{0,1,2:T(8,128)S(1)}, f32[256,64,1]{0,1,2:T(8,128)}, u32[]{:S(2)}) copy-start(f32[256,64,1]{0,1,2:T(8,128)} %constant.46) | copy-start | bytes 196612
  28.7 2.5 %copy-start = (f32[256,528,1]{0,1,2:T(8,128)S(1)}, f32[256,528,1]{0,1,2:T(8,128)}, u32[]{:S(2)}) copy-start(f32[256,528,1]{0,1,2:T(8,128)} %constant.47) | copy-start | bytes 1622020
  29.7 37.6 %copy-start.7 = (f32[128]{0:T(128)S(1)}, f32[128]{0:T(128)}, u32[]{:S(2)}) copy-start(f32[128]{0:T(128)} %param.18) | copy-start | bytes 1540

commit v5 on v4

--- a/solution.py
+++ b/solution.py
@@ -7,6 +7,7 @@
 
 D = 1024
 HIGHEST = lax.Precision.HIGHEST
+HIGH = lax.Precision.HIGH
 
 
 def padded(count, unit=8):
@@ -47,9 +48,7 @@
     inv_im = np.concatenate([sin_i, cos_i], axis=0)
     sign = np.where(np.arange(fp) % 2 == 0, 1.0, -1.0)[:, None]
     step = 2 * np.pi * np.arange(size)[None, :] / size
-    shift_re = np.cos(step) + sign
-    shift_im = -np.sin(step) + 0.0 * sign
-    return fwd, inv_re, inv_im, shift_re, shift_im
+    return fwd, inv_re, inv_im, sign, np.cos(step), -np.sin(step)
 
 
 def on_device(inputs, gate_values, causal_filter, anti_filter, skip_gain, norm_gain):
@@ -61,14 +60,14 @@
     own_index = lax.axis_index("seq")
 
     fp, fwd_np, inv_np = inner_tables(rows_dev)
-    ofwd_np, oinv_re_np, oinv_im_np, sh_re_np, sh_im_np = outer_tables(blocks, fp)
+    ofwd_np, oinv_re_np, oinv_im_np, sign_np, cos_np, msin_np = outer_tables(blocks, fp)
     fwd = jnp.asarray(fwd_np, jnp.bfloat16)
     inv = jnp.asarray(inv_np, f32)
     ofwd = jnp.asarray(ofwd_np, f32)
     oinv_re = jnp.asarray(oinv_re_np, f32)
     oinv_im = jnp.asarray(oinv_im_np, f32)
-    sh_re = jnp.asarray(sh_re_np, f32)
-    sh_im = jnp.asarray(sh_im_np, f32)
+    sh_re = jnp.asarray(sign_np, f32) + jnp.asarray(cos_np, f32)
+    sh_im = jnp.asarray(msin_np, f32)
 
     stacked = jnp.stack([inputs, causal_filter, anti_filter, gate_values])
     lanes = 128
@@ -88,7 +87,7 @@
 
     spec = jnp.einsum("fn,qbn->qfb", fwd, conv_in, preferred_element_type=f32)
     spec = spec.astype(jnp.bfloat16).astype(f32)
-    z = jnp.einsum("qfb,bk->qfk", spec, ofwd, precision=HIGHEST, preferred_element_type=f32)
+    z = jnp.einsum("qfb,bk->qfk", spec, ofwd, precision=HIGH, preferred_element_type=f32)
     z_re, z_im = z[:, :fp], z[:, fp:]
     x_re = (z_re[..., :size] + z_im[..., size:]).reshape(3, per, fp, size)
     x_im = (z_im[..., :size] - z_re[..., size:]).reshape(3, per, fp, size)
@@ -103,10 +102,10 @@
     y_im = k_re * x_im[0] + k_im * x_re[0]
     y_cat = jnp.concatenate([y_re, y_im], axis=-1)
 
-    t_re = jnp.einsum("cfk,ki->cfi", y_cat, oinv_re, precision=HIGHEST, preferred_element_type=f32)
-    t_im = jnp.einsum("cfk,ki->cfi", y_cat, oinv_im, precision=HIGHEST, preferred_element_type=f32)
+    t_re = jnp.einsum("cfk,ki->cfi", y_cat, oinv_re, precision=HIGH, preferred_element_type=f32)
+    t_im = jnp.einsum("cfk,ki->cfi", y_cat, oinv_im, precision=HIGH, preferred_element_type=f32)
     total = jnp.concatenate([t_re, t_im], axis=1)
-    conv_t = jnp.einsum("cfi,tf->ict", total, inv, precision=HIGHEST, preferred_element_type=f32)
+    conv_t = jnp.einsum("cfi,tf->ict", total, inv, precision=HIGH, preferred_element_type=f32)
 
     skip_here = lax.dynamic_slice_in_dim(skip_gain, own_index * per, per)
     mixed_local = series[:, 3].astype(f32) * (

time: 68.4 us -> 67 us (0.980)
  matrix products: 5.93 us -> 4.77 us
  waiting for transfers between devices: 10.3 us -> 9.5 us
  other arithmetic: 0.62 us -> 1.4 us
    dot_general x4, matrix products: 3.47 us -> 2.32 us  [the longest x1 1.06 us: on_device(): jnp.einsum('qfb,bk->qfk', spec, ofwd, precision=HIGH, preferred_element_t...]
    all_to_all x1, waiting for transfers between devices: 10.3 us -> 9.5 us  [on_device(): recv = lax.all_to_all(send, 'seq', 0, 0, tiled=True)]
    add x0 -> x1, other arithmetic: none -> 0.8 us  [on_device(): sh_re = jnp.asarray(sign_np, f32) + jnp.asarray(cos_np, f32)]
  transfers between devices with their start and end apart: 1 -> 1, of which waited for: 1 -> 1; matrix products, arithmetic and copies ran while one was open for 1% -> 2% of each run, Pallas kernels for 0% -> 0%
where the time goes in v5:
time: 67 us; the launch traced here: 66.7 us
  blocking collectives  35.1 us (52%)
  starting transfers between devices  12.9 us (19%)
  waiting for transfers between devices  9.5 us (14%)
  matrix products  4.77 us (7%)
  local copies, waits for them, and re-layouts  2.75 us (4%)
  other arithmetic  1.4 us (2%)
    all_gather x1, blocking collectives, on_device(): lax.all_gather(partial, 'ch', axis=0, tiled=False)  19.4 us
    all_to_all x1, blocking collectives, on_device(): got = lax.all_to_all(back, 'seq', 0, 0, tiled=True)  15.8 us
    all_to_all x1, starting transfers between devices, on_device(): recv = lax.all_to_all(send, 'seq', 0, 0, tiled=True)  12.9 us
    all_to_all x1, waiting for transfers between devices, on_device(): recv = lax.all_to_all(send, 'seq', 0, 0, tiled=True)  9.5 us
  transfers between devices with their start and end apart: 1, of which 1 were waited for; matrix products, arithmetic and copies ran while one was open for 2% of the time, Pallas kernels for 0%

profile of v5, /device:TPU:1, one launch (start us, length us, event | category | flops | bytes accessed | tf_op | source)
XLA Modules:
  0.0 66.7 jit_solution(2334870474814574393)
XLA Ops:
  0.0 1.2 %convolution_convert_fusion.1 = bf16[128,4,256]{2,0,1:T(8,128)(2,1)S(1)} fusion(bf16[1,256,128]{2,1,0:T(8,128)(2,1)} %bitcast.49, bf16[1,256,128]{2,1,0:T(8,128)(2,1)} %bitcast.50, bf16[1,256,128]{2,1,0:T(8,128)(2,1)} %bitcast.51, bf16[1,256,128]{2,1,0:T(8,128)(2,1)} %bitcast.52), kind=kOutput, calls=%fused_computation.2 | convolution fusion | flops 34750464 | bytes 524288 | tf_op jit(solution)/shard_map/ck,atk->cat/dot_general | solution.py:75
  1.2 0.2 copy.18
  1.4 0.8 %reshape.91 = bf16[64,16,128]{2,1,0:T(8,128)(2,1)} reshape(bf16[128,4,256]{2,1,0:T(4,128)(2,1)S(1)} %copy.18) | data formatting | bytes 524288 | tf_op jit(solution)/shard_map/reshape | solution.py:78
  2.2 12.9 %all-to-all-start = ((bf16[64,16,128]{2,1,0:T(8,128)(2,1)}), bf16[64,16,128]{2,1,0:T(8,128)(2,1)S(1)}, u32[]{:S(2)}, u32[]{:S(2)}) async-start(bf16[64,16,128]{2,1,0:T(8,128)(2,1)} %reshape.91), calls=%async_computation | async-start | bytes 524288 | tf_op jit(solution)/shard_map/all_to_all | solution.py:79
  15.2 0.7 %dynamic_slice.3 = f32[2]{0:T(128)S(1)} dynamic-slice(f32[128]{0:T(128)} %param.18, s32[]{:T(128)S(6)} %select_n.9), dynamic_slice_sizes={2} | dynamic-slice | bytes 20 | tf_op jit(solution)/shard_map/dynamic_slice | solution.py:110
  15.9 0.1 broadcast_and_fusion
  16.0 0.8 %broadcast_add_fusion = f32[264,128]{1,0:T(8,128)S(1)} fusion(f32[128]{0:T(128)} %constant.47, f32[264]{0:T(512)} %constant.46), kind=kLoop, calls=%fused_computation.32 | loop fusion | flops 33792 | bytes 136736 | tf_op jit(solution)/shard_map/add | solution.py:69
  16.8 9.5 %all-to-all-done = bf16[64,16,128]{2,1,0:T(8,128)(2,1)S(1)} async-done(((bf16[64,16,128]{2,1,0:T(8,128)(2,1)}), bf16[64,16,128]{2,1,0:T(8,128)(2,1)S(1)}, u32[]{:S(2)}, u32[]{:S(2)}) %all-to-all-start) | async-done | bytes 262176 | tf_op jit(solution)/shard_map/all_to_all | solution.py:79
  26.3 0.2 reshape.92
  26.6 0.3 fusion
  27.0 1.1 %fusion.23 = f32[6,528,256]{2,1,0:T(8,128)S(1)} fusion(bf16[6,528,64]{1,2,0:T(8,128)(2,1)S(1)} %fusion, f32[64,256,1]{1,0,2:T(8,128)S(1)} %copy-done.4), kind=kOutput, calls=%fused_computation.48 | convolution fusion | flops 311427072 | bytes 3715072 | tf_op jit(solution)/shard_map/qfb,bk->qfk/dot_general | solution.py:90
  28.1 0.2 slice_add_fusion
  28.3 0.4 copy-done.6
  28.7 0.2 multiply_subtract_fusion
  28.9 0.1 multiply_add_fusion
  29.0 0.4 fusion.4
  29.4 0.4 fusion.3
  29.9 0.4 fusion.2
  30.3 0.1 copy.20
  30.4 0.1 reshape.94
  30.5 15.8 %all_to_all.10 = f32[64,4,128]{2,1,0:T(4,128)S(1)} all-to-all(f32[64,4,128]{2,1,0:T(4,128)S(1)} %reshape.94), channel_id=1, replica_groups=mesh['seq'=64,'ch'=8] {'seq'}, dimensions={0} | all-to-all | bytes 262144 | tf_op jit(solution)/shard_map/all_to_all | solution.py:115
  46.3 0.1 reshape.95
  46.4 19.4 %all-gather.1 = f32[8,1,256]{2,1,0:T(1,128)S(1)} all-gather(f32[1,1,256]{2,1,0:T(1,128)S(1)} %bitcast.48), channel_id=2, replica_groups=mesh['seq'=64,'ch'=8] {'ch'}, dimensions={0}, use_global_device_ids=true | all-gather | bytes 9216 | tf_op jit(solution)/shard_map/all_gather | solution.py:119
  65.8 0.9 %convolution_convert_fusion.2 = bf16[256,128]{1,0:T(8,128)(2,1)} fusion(f32[128,256]{1,0:T(8,128)S(1)} %reshape.95, f32[256]{0:T(256)S(1)} %add_rsqrt_fusion, f32[128]{0:T(128)S(1)} %copy-done.5), kind=kOutput, calls=%fused_computation.6 | convolution fusion | flops 16973824 | bytes 198144 | tf_op jit(solution)/shard_map/tk,ck->tc/dot_general | solution.py:123
  (22 shorter events, 0.2 us)
Async XLA Ops:
  0.0 26.6 %copy-start.1 = (bf16[528,256,1]{1,0,2:T(8,128)(2,1)S(1)}, bf16[528,256,1]{1,0,2:T(8,128)(2,1)}, u32[]{:S(2)}) copy-start(bf16[528,256,1]{1,0,2:T(8,128)(2,1)} %constant.49) | copy-start | bytes 811012
  0.0 27.0 %copy-start.4 = (f32[64,256,1]{1,0,2:T(8,128)S(1)}, f32[64,256,1]{1,0,2:T(8,128)}, u32[]{:S(2)}) copy-start(f32[64,256,1]{1,0,2:T(8,128)} %constant.50) | copy-start | bytes 196612
  2.2 24.1 %all-to-all-start = ((bf16[64,16,128]{2,1,0:T(8,128)(2,1)}), bf16[64,16,128]{2,1,0:T(8,128)(2,1)S(1)}, u32[]{:S(2)}, u32[]{:S(2)}) async-start(bf16[64,16,128]{2,1,0:T(8,128)(2,1)} %reshape.91), calls=%async_computation | async-start | bytes 524288 | tf_op jit(solution)/shard_map/all_to_all | solution.py:79
  28.0 0.7 copy-start.6
  28.1 0.9 %copy-start.3 = (f32[256,64,1]{0,1,2:T(8,128)S(1)}, f32[256,64,1]{0,1,2:T(8,128)}, u32[]{:S(2)}) copy-start(f32[256,64,1]{0,1,2:T(8,128)} %constant.51) | copy-start | bytes 196612
  28.2 1.2 %copy-start.2 = (f32[256,64,1]{0,1,2:T(8,128)S(1)}, f32[256,64,1]{0,1,2:T(8,128)}, u32[]{:S(2)}) copy-start(f32[256,64,1]{0,1,2:T(8,128)} %constant.52) | copy-start | bytes 196612
  28.3 1.6 %copy-start = (f32[256,528,1]{0,1,2:T(8,128)S(1)}, f32[256,528,1]{0,1,2:T(8,128)}, u32[]{:S(2)}) copy-start(f32[256,528,1]{0,1,2:T(8,128)} %constant.53) | copy-start | bytes 1622020
  28.9 36.9 %copy-start.5 = (f32[128]{0:T(128)S(1)}, f32[128]{0:T(128)}, u32[]{:S(2)}) copy-start(f32[128]{0:T(128)} %param.19) | copy-start | bytes 1540

commit v6 on v5

--- a/solution.py
+++ b/solution.py
@@ -111,9 +111,9 @@
     mixed_local = series[:, 3].astype(f32) * (
         conv_t + skip_here[None, :, None] * series[:, 0].astype(f32)
     )
-    back = mixed_local.reshape(blocks, per * rows_dev // lanes, lanes)
+    back = mixed_local.astype(jnp.bfloat16).reshape(blocks, per * rows_dev // lanes, lanes)
     got = lax.all_to_all(back, "seq", 0, 0, tiled=True)
-    mix_t = got.reshape(blocks * per, rows_dev)
+    mix_t = got.reshape(blocks * per, rows_dev).astype(f32)
 
     partial = jnp.sum(mix_t * mix_t, axis=0)
     squares = jnp.sum(lax.all_gather(partial, "ch", axis=0, tiled=False), axis=0)

time: 67 us -> 66.5 us (level)
  no operation moved by 1% of the time
where the time goes in v6:
time: 66.5 us; the launch traced here: 66.2 us
  blocking collectives  34.8 us (52%)
  starting transfers between devices  12.9 us (19%)
  waiting for transfers between devices  9.5 us (14%)
  matrix products  4.77 us (7%)
  local copies, waits for them, and re-layouts  2.6 us (4%)
  other arithmetic  1.4 us (2%)
    all_gather x1, blocking collectives, on_device(): lax.all_gather(partial, 'ch', axis=0, tiled=False)  19.3 us
    all_to_all x1, blocking collectives, on_device(): got = lax.all_to_all(back, 'seq', 0, 0, tiled=True)  15.4 us
    all_to_all x1, starting transfers between devices, on_device(): recv = lax.all_to_all(send, 'seq', 0, 0, tiled=True)  12.9 us
    all_to_all x1, waiting for transfers between devices, on_device(): recv = lax.all_to_all(send, 'seq', 0, 0, tiled=True)  9.5 us
  transfers between devices with their start and end apart: 1, of which 1 were waited for; matrix products, arithmetic and copies ran while one was open for 2% of the time, Pallas kernels for 0%

profile of v6, /device:TPU:1, one launch (start us, length us, event | category | flops | bytes accessed | tf_op | source)
XLA Modules:
  0.0 66.2 jit_solution(14198978629439123381)
XLA Ops:
  0.0 1.2 %convolution_convert_fusion.1 = bf16[128,4,256]{2,0,1:T(8,128)(2,1)S(1)} fusion(bf16[1,256,128]{2,1,0:T(8,128)(2,1)} %bitcast.51, bf16[1,256,128]{2,1,0:T(8,128)(2,1)} %bitcast.52, bf16[1,256,128]{2,1,0:T(8,128)(2,1)} %bitcast.53, bf16[1,256,128]{2,1,0:T(8,128)(2,1)} %bitcast.54), kind=kOutput, calls=%fused_computation.2 | convolution fusion | flops 34750464 | bytes 524288 | tf_op jit(solution)/shard_map/ck,atk->cat/dot_general | solution.py:75
  1.2 0.2 copy.18
  1.4 0.8 %reshape.91 = bf16[64,16,128]{2,1,0:T(8,128)(2,1)} reshape(bf16[128,4,256]{2,1,0:T(4,128)(2,1)S(1)} %copy.18) | data formatting | bytes 524288 | tf_op jit(solution)/shard_map/reshape | solution.py:78
  2.2 12.9 %all-to-all-start = ((bf16[64,16,128]{2,1,0:T(8,128)(2,1)}), bf16[64,16,128]{2,1,0:T(8,128)(2,1)S(1)}, u32[]{:S(2)}, u32[]{:S(2)}) async-start(bf16[64,16,128]{2,1,0:T(8,128)(2,1)} %reshape.91), calls=%async_computation | async-start | bytes 524288 | tf_op jit(solution)/shard_map/all_to_all | solution.py:79
  15.2 0.7 %dynamic_slice.3 = f32[2]{0:T(128)S(1)} dynamic-slice(f32[128]{0:T(128)} %param.18, s32[]{:T(128)S(6)} %select_n.9), dynamic_slice_sizes={2} | dynamic-slice | bytes 20 | tf_op jit(solution)/shard_map/dynamic_slice | solution.py:110
  15.9 0.1 broadcast_and_fusion
  16.0 0.8 %broadcast_add_fusion = f32[264,128]{1,0:T(8,128)S(1)} fusion(f32[128]{0:T(128)} %constant.47, f32[264]{0:T(512)} %constant.46), kind=kLoop, calls=%fused_computation.33 | loop fusion | flops 33792 | bytes 136736 | tf_op jit(solution)/shard_map/add | solution.py:69
  16.8 9.5 %all-to-all-done = bf16[64,16,128]{2,1,0:T(8,128)(2,1)S(1)} async-done(((bf16[64,16,128]{2,1,0:T(8,128)(2,1)}), bf16[64,16,128]{2,1,0:T(8,128)(2,1)S(1)}, u32[]{:S(2)}, u32[]{:S(2)}) %all-to-all-start) | async-done | bytes 262176 | tf_op jit(solution)/shard_map/all_to_all | solution.py:79
  26.3 0.2 reshape.92
  26.6 0.3 fusion
  27.0 1.1 %fusion.24 = f32[6,528,256]{2,1,0:T(8,128)S(1)} fusion(bf16[6,528,64]{1,2,0:T(8,128)(2,1)S(1)} %fusion, f32[64,256,1]{1,0,2:T(8,128)S(1)} %copy-done.4), kind=kOutput, calls=%fused_computation.49 | convolution fusion | flops 311427072 | bytes 3715072 | tf_op jit(solution)/shard_map/qfb,bk->qfk/dot_general | solution.py:90
  28.0 0.0 copy-start.6
  28.1 0.2 slice_add_fusion
  28.2 0.0 copy-start.2
  28.3 0.4 copy-done.6
  28.7 0.2 multiply_subtract_fusion
  28.9 0.1 multiply_add_fusion
  29.0 0.4 fusion.5
  29.4 0.4 fusion.4
  29.9 0.4 fusion.3
  30.3 0.1 copy.20
  30.4 15.4 %all_to_all.10 = bf16[64,4,128]{2,1,0:T(4,128)(2,1)S(1)} all-to-all(bf16[64,4,128]{2,1,0:T(4,128)(2,1)S(1)} %reshape.94), channel_id=1, replica_groups=mesh['seq'=64,'ch'=8] {'seq'}, dimensions={0} | all-to-all | bytes 131072 | tf_op jit(solution)/shard_map/all_to_all | solution.py:115
  45.9 19.3 %all-gather.1 = f32[8,1,256]{2,1,0:T(1,128)S(1)} all-gather(f32[1,1,256]{2,1,0:T(1,128)S(1)} %bitcast.50), channel_id=2, replica_groups=mesh['seq'=64,'ch'=8] {'ch'}, dimensions={0}, use_global_device_ids=true | all-gather | bytes 9216 | tf_op jit(solution)/shard_map/all_gather | solution.py:119
  65.3 0.9 %convolution_convert_fusion.2 = bf16[256,128]{1,0:T(8,128)(2,1)} fusion(f32[128,256]{1,0:T(8,128)S(1)} %reshape.97, f32[256]{0:T(256)S(1)} %add_rsqrt_fusion, f32[128]{0:T(128)S(1)} %copy-done.5), kind=kOutput, calls=%fused_computation.7 | convolution fusion | flops 16973824 | bytes 198144 | tf_op jit(solution)/shard_map/tk,ck->tc/dot_general | solution.py:123
  (22 shorter events, 0.3 us)
Async XLA Ops:
  0.0 26.6 %copy-start.1 = (bf16[528,256,1]{1,0,2:T(8,128)(2,1)S(1)}, bf16[528,256,1]{1,0,2:T(8,128)(2,1)}, u32[]{:S(2)}) copy-start(bf16[528,256,1]{1,0,2:T(8,128)(2,1)} %constant.49) | copy-start | bytes 811012
  0.0 27.0 %copy-start.4 = (f32[64,256,1]{1,0,2:T(8,128)S(1)}, f32[64,256,1]{1,0,2:T(8,128)}, u32[]{:S(2)}) copy-start(f32[64,256,1]{1,0,2:T(8,128)} %constant.50) | copy-start | bytes 196612
  2.2 24.1 %all-to-all-start = ((bf16[64,16,128]{2,1,0:T(8,128)(2,1)}), bf16[64,16,128]{2,1,0:T(8,128)(2,1)S(1)}, u32[]{:S(2)}, u32[]{:S(2)}) async-start(bf16[64,16,128]{2,1,0:T(8,128)(2,1)} %reshape.91), calls=%async_computation | async-start | bytes 524288 | tf_op jit(solution)/shard_map/all_to_all | solution.py:79
  28.0 0.7 copy-start.6
  28.1 0.9 %copy-start.3 = (f32[256,64,1]{0,1,2:T(8,128)S(1)}, f32[256,64,1]{0,1,2:T(8,128)}, u32[]{:S(2)}) copy-start(f32[256,64,1]{0,1,2:T(8,128)} %constant.51) | copy-start | bytes 196612
  28.2 1.2 %copy-start.2 = (f32[256,64,1]{0,1,2:T(8,128)S(1)}, f32[256,64,1]{0,1,2:T(8,128)}, u32[]{:S(2)}) copy-start(f32[256,64,1]{0,1,2:T(8,128)} %constant.52) | copy-start | bytes 196612
  28.3 1.6 %copy-start = (f32[256,528,1]{0,1,2:T(8,128)S(1)}, f32[256,528,1]{0,1,2:T(8,128)}, u32[]{:S(2)}) copy-start(f32[256,528,1]{0,1,2:T(8,128)} %constant.53) | copy-start | bytes 1622020
  28.7 36.6 %copy-start.5 = (f32[128]{0:T(128)S(1)}, f32[128]{0:T(128)}, u32[]{:S(2)}) copy-start(f32[128]{0:T(128)} %param.19) | copy-start | bytes 1540

commit v7 on v6

--- a/solution.py
+++ b/solution.py
@@ -69,15 +69,15 @@
     sh_re = jnp.asarray(sign_np, f32) + jnp.asarray(cos_np, f32)
     sh_im = jnp.asarray(msin_np, f32)
 
-    stacked = jnp.stack([inputs, causal_filter, anti_filter, gate_values])
+    stacked = jnp.stack([inputs, causal_filter, anti_filter])
     lanes = 128
     eye_ch = jnp.eye(chan_dev, dtype=jnp.bfloat16)
     by_channel = jnp.einsum(
         "ck,atk->cat", eye_ch, stacked, preferred_element_type=f32
     ).astype(jnp.bfloat16)
-    send = by_channel.reshape(blocks, per * 4 * rows_dev // lanes, lanes)
+    send = by_channel.reshape(blocks, per * 3 * rows_dev // lanes, lanes)
     recv = lax.all_to_all(send, "seq", 0, 0, tiled=True)
-    series = recv.reshape(blocks, per, 4, rows_dev).transpose(0, 2, 1, 3)
+    series = recv.reshape(blocks, per, 3, rows_dev).transpose(0, 2, 1, 3)
     block_ids = lax.broadcasted_iota(jnp.int32, (blocks, 1, rows_dev), 0)
     tok_ids = lax.broadcasted_iota(jnp.int32, (blocks, 1, rows_dev), 2)
     first_row = jnp.logical_and(block_ids == 0, tok_ids == 0)
@@ -107,13 +107,13 @@
     total = jnp.concatenate([t_re, t_im], axis=1)
     conv_t = jnp.einsum("cfi,tf->ict", total, inv, precision=HIGH, preferred_element_type=f32)
 
-    skip_here = lax.dynamic_slice_in_dim(skip_gain, own_index * per, per)
-    mixed_local = series[:, 3].astype(f32) * (
-        conv_t + skip_here[None, :, None] * series[:, 0].astype(f32)
-    )
-    back = mixed_local.astype(jnp.bfloat16).reshape(blocks, per * rows_dev // lanes, lanes)
+    back = conv_t.reshape(blocks, per * rows_dev // lanes, lanes)
     got = lax.all_to_all(back, "seq", 0, 0, tiled=True)
-    mix_t = got.reshape(blocks * per, rows_dev).astype(f32)
+    conv_tc = got.reshape(blocks * per, rows_dev)
+    eye_ch_f = jnp.eye(chan_dev, dtype=f32)
+    gate_t = jnp.einsum("ck,tk->ct", eye_ch, gate_values, preferred_element_type=f32)
+    inputs_t = jnp.einsum("ck,tk->ct", eye_ch, inputs, preferred_element_type=f32)
+    mix_t = gate_t * (conv_tc + skip_gain[:, None] * inputs_t)
 
     partial = jnp.sum(mix_t * mix_t, axis=0)
     squares = jnp.sum(lax.all_gather(partial, "ch", axis=0, tiled=False), axis=0)

time: 66.5 us -> 68.6 us (1.032)
  blocking collectives: 34.8 us -> 19.4 us
  waiting for transfers between devices: 9.5 us -> 19.8 us
  starting transfers between devices: 12.9 us -> 19.1 us
    all_to_all x1 -> x0, blocking collectives: 15.4 us -> none  [on_device(): got = lax.all_to_all(back, 'seq', 0, 0, tiled=True)]
    all_to_all x0 -> x1, waiting for transfers between devices: none -> 9.58 us  [on_device(): got = lax.all_to_all(back, 'seq', 0, 0, tiled=True)]
    all_to_all x0 -> x1, starting transfers between devices: none -> 6.2 us  [on_device(): got = lax.all_to_all(back, 'seq', 0, 0, tiled=True)]
    reshape x4, local copies, waits for them, and re-layouts: 1.07 us -> 1.88 us  [the longest x1 0.88 us: on_device(): send = by_channel.reshape(blocks, per * 3 * rows_dev // lanes, lanes)]
    all_to_all x1, waiting for transfers between devices: 9.5 us -> 10.2 us  [on_device(): recv = lax.all_to_all(send, 'seq', 0, 0, tiled=True)]
    dynamic_slice x1 -> x0, local copies, waits for them, and re-layouts: 0.73 us -> none  [on_device(): skip_here = lax.dynamic_slice_in_dim(skip_gain, own_index * per, per)]
  transfers between devices with their start and end apart: 1 -> 2, of which waited for: 1 -> 2; matrix products, arithmetic and copies ran while one was open for 2% -> 2% of each run, Pallas kernels for 0% -> 0%
where the time goes in v7:
time: 68.6 us; the launch traced here: 68.4 us
  waiting for transfers between devices  19.8 us (29%)
  blocking collectives  19.4 us (28%)
  starting transfers between devices  19.1 us (28%)
  matrix products  5.08 us (7%)
  local copies, waits for them, and re-layouts  2.79 us (4%)
  other arithmetic  1.88 us (3%)
    all_gather x1, blocking collectives, on_device(): lax.all_gather(partial, 'ch', axis=0, tiled=False)  19.4 us
    all_to_all x1, starting transfers between devices, on_device(): recv = lax.all_to_all(send, 'seq', 0, 0, tiled=True)  12.9 us
    all_to_all x1, waiting for transfers between devices, on_device(): recv = lax.all_to_all(send, 'seq', 0, 0, tiled=True)  10.2 us
    all_to_all x1, waiting for transfers between devices, on_device(): got = lax.all_to_all(back, 'seq', 0, 0, tiled=True)  9.58 us
    all_to_all x1, starting transfers between devices, on_device(): got = lax.all_to_all(back, 'seq', 0, 0, tiled=True)  6.2 us
  transfers between devices with their start and end apart: 2, of which 2 were waited for; matrix products, arithmetic and copies ran while one was open for 2% of the time, Pallas kernels for 0%

profile of v7, /device:TPU:1, one launch (start us, length us, event | category | flops | bytes accessed | tf_op | source)
XLA Modules:
  0.0 68.4 jit_solution(14054782846662495753)
XLA Ops:
  0.0 1.2 %convolution_convert_fusion.1 = bf16[128,3,256]{2,0,1:T(8,128)(2,1)S(1)} fusion(bf16[1,256,128]{2,1,0:T(8,128)(2,1)} %bitcast.34, bf16[1,256,128]{2,1,0:T(8,128)(2,1)} %bitcast.35, bf16[1,256,128]{2,1,0:T(8,128)(2,1)} %bitcast.32), kind=kOutput, calls=%fused_computation.2 | convolution fusion | flops 25870336 | bytes 393216 | tf_op jit(solution)/shard_map/ck,atk->cat/dot_general | solution.py:75
  1.2 0.2 copy.18
  1.4 0.9 %reshape.87 = bf16[64,12,128]{2,1,0:T(8,128)(2,1)} reshape(bf16[128,3,256]{2,1,0:T(4,128)(2,1)S(1)} %copy.18) | data formatting | bytes 393216 | tf_op jit(solution)/shard_map/reshape | solution.py:78
  2.3 12.9 %all-to-all-start = ((bf16[64,12,128]{2,1,0:T(8,128)(2,1)}), bf16[64,12,128]{2,1,0:T(8,128)(2,1)S(1)}, u32[]{:S(2)}, u32[]{:S(2)}) async-start(bf16[64,12,128]{2,1,0:T(8,128)(2,1)} %reshape.87), calls=%async_computation | async-start | bytes 524288 | tf_op jit(solution)/shard_map/all_to_all | solution.py:79
  15.3 0.8 %broadcast_add_fusion = f32[264,128]{1,0:T(8,128)S(1)} fusion(f32[128]{0:T(128)} %constant.36, f32[264]{0:T(512)} %constant.35), kind=kLoop, calls=%fused_computation.30 | loop fusion | flops 33792 | bytes 136736 | tf_op jit(solution)/shard_map/add | solution.py:69
  16.1 10.2 %all-to-all-done = bf16[64,12,128]{2,1,0:T(8,128)(2,1)S(1)} async-done(((bf16[64,12,128]{2,1,0:T(8,128)(2,1)}), bf16[64,12,128]{2,1,0:T(8,128)(2,1)S(1)}, u32[]{:S(2)}, u32[]{:S(2)}) %all-to-all-start) | async-done | bytes 196640 | tf_op jit(solution)/shard_map/all_to_all | solution.py:79
  26.3 0.2 reshape.88
  26.6 0.3 broadcast_select_fusion
  26.9 0.3 pad_maximum_fusion.3
  27.2 0.3 fusion
  27.6 1.1 %fusion.22 = f32[6,528,256]{2,1,0:T(8,128)S(1)} fusion(bf16[6,528,64]{1,2,0:T(8,128)(2,1)S(1)} %fusion, f32[64,256,1]{1,0,2:T(8,128)S(1)} %copy-done.6), kind=kOutput, calls=%fused_computation.44 | convolution fusion | flops 311427072 | bytes 3715072 | tf_op jit(solution)/shard_map/qfb,bk->qfk/dot_general | solution.py:90
  28.7 0.2 slice_add_fusion
  28.9 0.4 copy-done.9
  29.3 0.2 multiply_subtract_fusion
  29.6 0.4 fusion.4
  30.1 0.4 fusion.3
  30.5 0.4 convolution_bitcast_fusion
  31.0 0.8 %reshape.90 = f32[64,4,128]{2,1,0:T(4,128)} reshape(f32[64,2,256]{2,1,0:T(2,128)S(1)} %copy.20) | data formatting | bytes 262144 | tf_op jit(solution)/shard_map/reshape | solution.py:110
  31.8 6.2 %all-to-all-start.1 = ((f32[64,4,128]{2,1,0:T(4,128)}), f32[64,4,128]{2,1,0:T(4,128)S(1)}, u32[]{:S(2)}, u32[]{:S(2)}) async-start(f32[64,4,128]{2,1,0:T(4,128)} %reshape.90), calls=%async_computation.1 | async-start | bytes 262144 | tf_op jit(solution)/shard_map/all_to_all | solution.py:111
  38.0 0.2 fusion.15
  38.2 9.6 %all-to-all-done.1 = f32[64,4,128]{2,1,0:T(4,128)S(1)} async-done(((f32[64,4,128]{2,1,0:T(4,128)}), f32[64,4,128]{2,1,0:T(4,128)S(1)}, u32[]{:S(2)}, u32[]{:S(2)}) %all-to-all-start.1) | async-done | bytes 131104 | tf_op jit(solution)/shard_map/all_to_all | solution.py:111
  47.8 0.2 multiply_reduce_fusion
  48.0 19.4 %all-gather.1 = f32[8,1,256]{2,1,0:T(1,128)S(1)} all-gather(f32[1,1,256]{2,1,0:T(1,128)S(1)} %bitcast.33), channel_id=2, replica_groups=mesh['seq'=64,'ch'=8] {'ch'}, dimensions={0}, use_global_device_ids=true | all-gather | bytes 9216 | tf_op jit(solution)/shard_map/all_gather | solution.py:119
  67.5 0.9 %convolution_convert_fusion.2 = bf16[256,128]{1,0:T(8,128)(2,1)} fusion(f32[128,256]{1,0:T(8,128)S(1)} %get-tuple-element.11, f32[256]{0:T(256)S(1)} %add_rsqrt_fusion, f32[128]{0:T(128)S(1)} %copy-done.7), kind=kOutput, calls=%fused_computation.7 | convolution fusion | flops 16973824 | bytes 198144 | tf_op jit(solution)/shard_map/tk,ck->tc/dot_general | solution.py:123
  (29 shorter events, 0.6 us)
Async XLA Ops:
  0.0 38.0 %copy-start = (bf16[256,128]{1,0:T(8,128)(2,1)S(1)}, bf16[256,128]{1,0:T(8,128)(2,1)}, u32[]{:S(2)}) copy-start(bf16[256,128]{1,0:T(8,128)(2,1)} %param.15) | copy-start | bytes 196612
  0.0 27.2 %copy-start.2 = (bf16[528,256,1]{1,0,2:T(8,128)(2,1)S(1)}, bf16[528,256,1]{1,0,2:T(8,128)(2,1)}, u32[]{:S(2)}) copy-start(bf16[528,256,1]{1,0,2:T(8,128)(2,1)} %constant.38) | copy-start | bytes 811012
  0.0 27.6 %copy-start.6 = (f32[64,256,1]{1,0,2:T(8,128)S(1)}, f32[64,256,1]{1,0,2:T(8,128)}, u32[]{:S(2)}) copy-start(f32[64,256,1]{1,0,2:T(8,128)} %constant.39) | copy-start | bytes 196612
  2.3 24.1 %all-to-all-start = ((bf16[64,12,128]{2,1,0:T(8,128)(2,1)}), bf16[64,12,128]{2,1,0:T(8,128)(2,1)S(1)}, u32[]{:S(2)}, u32[]{:S(2)}) async-start(bf16[64,12,128]{2,1,0:T(8,128)(2,1)} %reshape.87), calls=%async_computation | async-start | bytes 524288 | tf_op jit(solution)/shard_map/all_to_all | solution.py:79
  28.6 0.7 copy-start.9
  28.7 0.9 %copy-start.4 = (f32[256,64,1]{0,1,2:T(8,128)S(1)}, f32[256,64,1]{0,1,2:T(8,128)}, u32[]{:S(2)}) copy-start(f32[256,64,1]{0,1,2:T(8,128)} %constant.40) | copy-start | bytes 196612
  28.8 1.2 %copy-start.3 = (f32[256,64,1]{0,1,2:T(8,128)S(1)}, f32[256,64,1]{0,1,2:T(8,128)}, u32[]{:S(2)}) copy-start(f32[256,64,1]{0,1,2:T(8,128)} %constant.41) | copy-start | bytes 196612
  28.9 1.6 %copy-start.1 = (f32[256,528,1]{0,1,2:T(8,128)S(1)}, f32[256,528,1]{0,1,2:T(8,128)}, u32[]{:S(2)}) copy-start(f32[256,528,1]{0,1,2:T(8,128)} %constant.42) | copy-start | bytes 1622020
  29.5 18.3 %copy-start.5 = (bf16[256,128]{1,0:T(8,128)(2,1)S(1)}, bf16[256,128]{1,0:T(8,128)(2,1)}, u32[]{:S(2)}) copy-start(bf16[256,128]{1,0:T(8,128)(2,1)} %param.14) | copy-start | bytes 196612
  29.5 18.3 %copy-start.8 = (f32[128]{0:T(128)S(1)}, f32[128]{0:T(128)}, u32[]{:S(2)}) copy-start(f32[128]{0:T(128)} %param.18) | copy-start | bytes 1540
  29.5 37.9 %copy-start.7 = (f32[128]{0:T(128)S(1)}, f32[128]{0:T(128)}, u32[]{:S(2)}) copy-start(f32[128]{0:T(128)} %param.19) | copy-start | bytes 1540
  31.8 16.0 %all-to-all-start.1 = ((f32[64,4,128]{2,1,0:T(4,128)}), f32[64,4,128]{2,1,0:T(4,128)S(1)}, u32[]{:S(2)}, u32[]{:S(2)}) async-start(f32[64,4,128]{2,1,0:T(4,128)} %reshape.90), calls=%async_computation.1 | async-start | bytes 262144 | tf_op jit(solution)/shard_map/all_to_all | solution.py:111

commit v8 on v5

--- a/solution.py
+++ b/solution.py
@@ -69,15 +69,22 @@
     sh_re = jnp.asarray(sign_np, f32) + jnp.asarray(cos_np, f32)
     sh_im = jnp.asarray(msin_np, f32)
 
-    stacked = jnp.stack([inputs, causal_filter, anti_filter, gate_values])
     lanes = 128
-    eye_ch = jnp.eye(chan_dev, dtype=jnp.bfloat16)
-    by_channel = jnp.einsum(
-        "ck,atk->cat", eye_ch, stacked, preferred_element_type=f32
-    ).astype(jnp.bfloat16)
-    send = by_channel.reshape(blocks, per * 4 * rows_dev // lanes, lanes)
+    arrays = 4
+    joined = jnp.concatenate([inputs, causal_filter, anti_filter, gate_values], axis=1)
+    dest = np.arange(blocks)[:, None, None]
+    kind = np.arange(arrays)[None, :, None]
+    chan = np.arange(per)[None, None, :]
+    source = (kind * chan_dev + dest * per + chan).reshape(-1)
+    perm_np = np.zeros((arrays * chan_dev, arrays * chan_dev))
+    perm_np[np.arange(arrays * chan_dev), source] = 1.0
+    perm = jnp.asarray(perm_np, jnp.bfloat16)
+    by_dest = jnp.einsum("rk,tk->rt", perm, joined, preferred_element_type=f32).astype(
+        jnp.bfloat16
+    )
+    send = by_dest.reshape(blocks, arrays * per, rows_dev)
     recv = lax.all_to_all(send, "seq", 0, 0, tiled=True)
-    series = recv.reshape(blocks, per, 4, rows_dev).transpose(0, 2, 1, 3)
+    series = recv.reshape(blocks, arrays, per, rows_dev)
     block_ids = lax.broadcasted_iota(jnp.int32, (blocks, 1, rows_dev), 0)
     tok_ids = lax.broadcasted_iota(jnp.int32, (blocks, 1, rows_dev), 2)
     first_row = jnp.logical_and(block_ids == 0, tok_ids == 0)

time: 67 us -> 69.8 us (1.042)
  matrix products: 4.77 us -> 7.91 us
  waiting for transfers between devices: 9.5 us -> 10.8 us
  local copies, waits for them, and re-layouts: 2.75 us -> 1.73 us
  other arithmetic: 1.4 us -> 0.7 us
    dot_general x1 -> x4, matrix products: 1.21 us -> 4.35 us  [on_device(): jnp.einsum('rk,tk->rt', perm, joined, preferred_element_type=f32)]
    all_to_all x1, waiting for transfers between devices: 9.5 us -> 10.8 us  [on_device(): recv = lax.all_to_all(send, 'seq', 0, 0, tiled=True)]
    reshape x3 -> x0, local copies, waits for them, and re-layouts: 1.02 us -> none  [the longest x1 0.8 us: on_device(): send = by_channel.reshape(blocks, per * 4 * rows_dev // lanes, lanes)]
    unnamed x14 -> x26, local copies, waits for them, and re-layouts: 0.48 us -> 1.29 us
    add x1, other arithmetic: 0.8 us -> 0.1 us  [on_device(): sh_re = jnp.asarray(sign_np, f32) + jnp.asarray(cos_np, f32)]
  transfers between devices with their start and end apart: 1 -> 1, of which waited for: 1 -> 1; matrix products, arithmetic and copies ran while one was open for 2% -> 0% of each run, Pallas kernels for 0% -> 0%
where the time goes in v8:
time: 69.8 us; the launch traced here: 69.6 us
  blocking collectives  35.1 us (50%)
  starting transfers between devices  12.9 us (18%)
  waiting for transfers between devices  10.8 us (15%)
  matrix products  7.91 us (11%)
  local copies, waits for them, and re-layouts  1.73 us (2%)
  other arithmetic  0.7 us (1%)
    all_gather x1, blocking collectives, on_device(): lax.all_gather(partial, 'ch', axis=0, tiled=False)  19.4 us
    all_to_all x1, blocking collectives, on_device(): got = lax.all_to_all(back, 'seq', 0, 0, tiled=True)  15.8 us
    all_to_all x1, starting transfers between devices, on_device(): recv = lax.all_to_all(send, 'seq', 0, 0, tiled=True)  12.9 us
    all_to_all x1, waiting for transfers between devices, on_device(): recv = lax.all_to_all(send, 'seq', 0, 0, tiled=True)  10.8 us
    dot_general x4, matrix products, on_device(): jnp.einsum('rk,tk->rt', perm, joined, preferred_element_type=f32)  4.35 us
  transfers between devices with their start and end apart: 1, of which 1 were waited for; matrix products, arithmetic and copies ran while one was open for 0% of the time, Pallas kernels for 0%

profile of v8, /device:TPU:1, one launch (start us, length us, event | category | flops | bytes accessed | tf_op | source)
XLA Modules:
  0.0 69.6 jit_solution(15222560790167748936)
XLA Ops:
  0.1 0.8 %copy-done = bf16[256,128]{1,0:T(8,128)(2,1)S(1)} copy-done((bf16[256,128]{1,0:T(8,128)(2,1)S(1)}, bf16[256,128]{1,0:T(8,128)(2,1)}, u32[]{:S(2)}) %copy-start) | copy-done | bytes 65560
  0.8 1.1 %fusion.15 = f32[512,256]{1,0:T(8,128)S(1)} fusion(bf16[512,128]{1,0:T(8,128)(2,1)} %constant.49, bf16[256,128]{1,0:T(8,128)(2,1)S(1)} %copy-done), kind=kOutput, calls=%fused_computation.41 | convolution fusion | flops 33554432 | bytes 720896 | tf_op jit(solution)/shard_map/rk,tk->rt/dot_general | solution.py:82
  2.0 1.2 %convolution_add_fusion.2 = f32[512,256]{1,0:T(8,128)S(1)} fusion(f32[512,256]{1,0:T(8,128)S(1)} %fusion.15, bf16[512,128]{1,0:T(8,128)(2,1)} %constant.50, bf16[256,128]{1,0:T(8,128)(2,1)} %param.17), kind=kOutput, calls=%fused_computation.3 | convolution fusion | flops 33685504 | bytes 1245184 | tf_op jit(solution)/shard_map/rk,tk->rt/dot_general | solution.py:82
  3.2 1.1 %convolution_add_fusion.1 = f32[512,256]{1,0:T(8,128)S(1)} fusion(f32[512,256]{1,0:T(8,128)S(1)} %convolution_add_fusion.2, bf16[512,128]{1,0:T(8,128)(2,1)} %constant.51, bf16[256,128]{1,0:T(8,128)(2,1)} %param.18), kind=kOutput, calls=%fused_computation.2 | convolution fusion | flops 33685504 | bytes 1245184 | tf_op jit(solution)/shard_map/rk,tk->rt/dot_general | solution.py:82
  4.3 0.9 %fusion.2 = bf16[64,8,256]{2,1,0:T(8,128)(2,1)} fusion(f32[512,256]{1,0:T(8,128)S(1)} %convolution_add_fusion.1, bf16[512,128]{1,0:T(8,128)(2,1)S(1)} %copy-done.3, bf16[256,128]{1,0:T(8,128)(2,1)S(1)} %copy-done.6), kind=kOutput, calls=%fused_computation.6 | convolution fusion | flops 33816576 | bytes 983040 | tf_op jit(solution)/shard_map/rk,tk->rt/dot_general | solution.py:82
  5.3 12.9 %all-to-all-start = ((bf16[64,8,256]{2,1,0:T(8,128)(2,1)}), bf16[64,8,256]{2,1,0:T(8,128)(2,1)S(1)}, u32[]{:S(2)}, u32[]{:S(2)}) async-start(bf16[64,8,256]{2,1,0:T(8,128)(2,1)} %fusion.2), calls=%async_computation | async-start | bytes 524288 | tf_op jit(solution)/shard_map/all_to_all | solution.py:86
  18.2 0.1 dynamic_slice.3
  18.3 0.1 broadcast_and_fusion
  18.4 0.1 broadcast_add_fusion
  18.5 10.8 %all-to-all-done = bf16[64,8,256]{2,1,0:T(8,128)(2,1)S(1)} async-done(((bf16[64,8,256]{2,1,0:T(8,128)(2,1)}), bf16[64,8,256]{2,1,0:T(8,128)(2,1)S(1)}, u32[]{:S(2)}, u32[]{:S(2)}) %all-to-all-start) | async-done | bytes 262176 | tf_op jit(solution)/shard_map/all_to_all | solution.py:86
  29.5 0.3 fusion
  29.8 1.1 %fusion.16 = f32[6,528,256]{2,1,0:T(8,128)S(1)} fusion(bf16[6,528,64]{1,2,0:T(8,128)(2,1)S(1)} %fusion, f32[64,256,1]{1,0,2:T(8,128)S(1)} %copy-done.7), kind=kOutput, calls=%fused_computation.42 | convolution fusion | flops 311427072 | bytes 3715072 | tf_op jit(solution)/shard_map/qfb,bk->qfk/dot_general | solution.py:97
  30.9 0.2 slice_add_fusion
  31.1 0.4 copy-done.11
  31.5 0.2 multiply_subtract_fusion
  31.7 0.1 multiply_add_fusion
  31.8 0.4 fusion.6
  32.3 0.4 fusion.5
  32.7 0.4 fusion.4
  33.1 0.1 copy.20
  33.2 0.1 reshape.94
  33.4 15.8 %all_to_all.10 = f32[64,4,128]{2,1,0:T(4,128)S(1)} all-to-all(f32[64,4,128]{2,1,0:T(4,128)S(1)} %reshape.94), channel_id=1, replica_groups=mesh['seq'=64,'ch'=8] {'seq'}, dimensions={0} | all-to-all | bytes 262144 | tf_op jit(solution)/shard_map/all_to_all | solution.py:122
  49.2 19.4 %all-gather.1 = f32[8,1,256]{2,1,0:T(1,128)S(1)} all-gather(f32[1,1,256]{2,1,0:T(1,128)S(1)} %bitcast.49), channel_id=2, replica_groups=mesh['seq'=64,'ch'=8] {'ch'}, dimensions={0}, use_global_device_ids=true | all-gather | bytes 9216 | tf_op jit(solution)/shard_map/all_gather | solution.py:126
  68.7 0.9 %convolution_convert_fusion.1 = bf16[256,128]{1,0:T(8,128)(2,1)} fusion(f32[128,256]{1,0:T(8,128)S(1)} %reshape.95, f32[256]{0:T(256)S(1)} %add_rsqrt_fusion, f32[128]{0:T(128)S(1)} %copy-done.9), kind=kOutput, calls=%fused_computation.10 | convolution fusion | flops 16973824 | bytes 198144 | tf_op jit(solution)/shard_map/tk,ck->tc/dot_general | solution.py:130
  (34 shorter events, 0.3 us)
Async XLA Ops:
  0.0 0.8 %copy-start = (bf16[256,128]{1,0:T(8,128)(2,1)S(1)}, bf16[256,128]{1,0:T(8,128)(2,1)}, u32[]{:S(2)}) copy-start(bf16[256,128]{1,0:T(8,128)(2,1)} %param.15) | copy-start | bytes 196612
  0.0 4.3 %copy-start.3 = (bf16[512,128]{1,0:T(8,128)(2,1)S(1)}, bf16[512,128]{1,0:T(8,128)(2,1)}, u32[]{:S(2)}) copy-start(bf16[512,128]{1,0:T(8,128)(2,1)} %constant.52) | copy-start | bytes 393220
  0.0 18.4 %copy-start.8 = (f32[264]{0:T(512)S(1)}, f32[264]{0:T(512)}, u32[]{:S(2)}) copy-start(f32[264]{0:T(512)} %constant.53) | copy-start | bytes 3172
  0.0 18.4 %copy-start.10 = (f32[128]{0:T(128)S(1)}, f32[128]{0:T(128)}, u32[]{:S(2)}) copy-start(f32[128]{0:T(128)} %constant.54) | copy-start | bytes 1540
  0.0 29.4 %copy-start.2 = (bf16[528,256,1]{1,0,2:T(8,128)(2,1)S(1)}, bf16[528,256,1]{1,0,2:T(8,128)(2,1)}, u32[]{:S(2)}) copy-start(bf16[528,256,1]{1,0,2:T(8,128)(2,1)} %constant.56) | copy-start | bytes 811012
  0.0 4.3 %copy-start.6 = (bf16[256,128]{1,0:T(8,128)(2,1)S(1)}, bf16[256,128]{1,0:T(8,128)(2,1)}, u32[]{:S(2)}) copy-start(bf16[256,128]{1,0:T(8,128)(2,1)} %param.16) | copy-start | bytes 196612
  0.0 18.2 %copy-start.12 = (f32[128]{0:T(128)S(1)}, f32[128]{0:T(128)}, u32[]{:S(2)}) copy-start(f32[128]{0:T(128)} %param.19) | copy-start | bytes 1540
  2.0 27.8 %copy-start.7 = (f32[64,256,1]{1,0,2:T(8,128)S(1)}, f32[64,256,1]{1,0,2:T(8,128)}, u32[]{:S(2)}) copy-start(f32[64,256,1]{1,0,2:T(8,128)} %constant.57) | copy-start | bytes 196612
  5.3 24.1 %all-to-all-start = ((bf16[64,8,256]{2,1,0:T(8,128)(2,1)}), bf16[64,8,256]{2,1,0:T(8,128)(2,1)S(1)}, u32[]{:S(2)}, u32[]{:S(2)}) async-start(bf16[64,8,256]{2,1,0:T(8,128)(2,1)} %fusion.2), calls=%async_computation | async-start | bytes 524288 | tf_op jit(solution)/shard_map/all_to_all | solution.py:86
  30.9 0.7 copy-start.11
  30.9 0.9 %copy-start.5 = (f32[256,64,1]{0,1,2:T(8,128)S(1)}, f32[256,64,1]{0,1,2:T(8,128)}, u32[]{:S(2)}) copy-start(f32[256,64,1]{0,1,2:T(8,128)} %constant.58) | copy-start | bytes 196612
  31.1 1.2 %copy-start.4 = (f32[256,64,1]{0,1,2:T(8,128)S(1)}, f32[256,64,1]{0,1,2:T(8,128)}, u32[]{:S(2)}) copy-start(f32[256,64,1]{0,1,2:T(8,128)} %constant.59) | copy-start | bytes 196612
  31.1 1.6 %copy-start.1 = (f32[256,528,1]{0,1,2:T(8,128)S(1)}, f32[256,528,1]{0,1,2:T(8,128)}, u32[]{:S(2)}) copy-start(f32[256,528,1]{0,1,2:T(8,128)} %constant.60) | copy-start | bytes 1622020
  31.7 36.9 %copy-start.9 = (f32[128]{0:T(128)S(1)}, f32[128]{0:T(128)}, u32[]{:S(2)}) copy-start(f32[128]{0:T(128)} %param.20) | copy-start | bytes 1540

commit v9 on v5

--- a/solution.py
+++ b/solution.py
@@ -63,11 +63,15 @@
     ofwd_np, oinv_re_np, oinv_im_np, sign_np, cos_np, msin_np = outer_tables(blocks, fp)
     fwd = jnp.asarray(fwd_np, jnp.bfloat16)
     inv = jnp.asarray(inv_np, f32)
-    ofwd = jnp.asarray(ofwd_np, f32)
+    ofwd_hi = ofwd_np.astype(np.float32).astype(jnp.bfloat16)
+    ofwd_lo = (ofwd_np - ofwd_hi.astype(np.float64)).astype(np.float32).astype(jnp.bfloat16)
+    ofwd_split = jnp.asarray(np.concatenate([ofwd_hi, ofwd_lo], axis=1), jnp.bfloat16)
     oinv_re = jnp.asarray(oinv_re_np, f32)
     oinv_im = jnp.asarray(oinv_im_np, f32)
-    sh_re = jnp.asarray(sign_np, f32) + jnp.asarray(cos_np, f32)
-    sh_im = jnp.asarray(msin_np, f32)
+    step = lax.broadcasted_iota(f32, (1, size), 1) * f32(2 * np.pi / size)
+    step = step + f32(0.0) * own_index.astype(f32)
+    sh_re = jnp.asarray(sign_np, f32) + jnp.cos(step)
+    sh_im = -jnp.sin(step)
 
     stacked = jnp.stack([inputs, causal_filter, anti_filter, gate_values])
     lanes = 128
@@ -86,8 +90,9 @@
     conv_in = conv_in.reshape(blocks, 3 * per, rows_dev).transpose(1, 0, 2)
 
     spec = jnp.einsum("fn,qbn->qfb", fwd, conv_in, preferred_element_type=f32)
-    spec = spec.astype(jnp.bfloat16).astype(f32)
-    z = jnp.einsum("qfb,bk->qfk", spec, ofwd, precision=HIGH, preferred_element_type=f32)
+    spec = spec.astype(jnp.bfloat16)
+    z_split = jnp.einsum("qfb,bk->qfk", spec, ofwd_split, preferred_element_type=f32)
+    z = z_split[..., : 2 * size] + z_split[..., 2 * size :]
     z_re, z_im = z[:, :fp], z[:, fp:]
     x_re = (z_re[..., :size] + z_im[..., size:]).reshape(3, per, fp, size)
     x_im = (z_im[..., :size] - z_re[..., size:]).reshape(3, per, fp, size)

time: 67 us -> 72.8 us (1.087)
  other arithmetic: 1.4 us -> 4.76 us
  matrix products: 4.77 us -> 7.35 us
    add x1 -> x2, other arithmetic: 0.8 us -> 4.1 us  [the longest x1 3.32 us: on_device(): z = z_split[..., :2 * size] + z_split[..., 2 * size:]]
    dot_general x2 -> x1, matrix products: 1.4 us -> 3.98 us  [on_device(): jnp.einsum('qfb,bk->qfk', spec, ofwd_split, preferred_element_type=f32)]
where the time goes in v9:
time: 72.8 us; the launch traced here: 72.5 us
  blocking collectives  35.1 us (48%)
  starting transfers between devices  12.9 us (18%)
  waiting for transfers between devices  9.46 us (13%)
  matrix products  7.35 us (10%)
  other arithmetic  4.76 us (7%)
  local copies, waits for them, and re-layouts  2.66 us (4%)
    all_gather x1, blocking collectives, on_device(): lax.all_gather(partial, 'ch', axis=0, tiled=False)  19.4 us
    all_to_all x1, blocking collectives, on_device(): got = lax.all_to_all(back, 'seq', 0, 0, tiled=True)  15.8 us
    all_to_all x1, starting transfers between devices, on_device(): recv = lax.all_to_all(send, 'seq', 0, 0, tiled=True)  12.9 us
    all_to_all x1, waiting for transfers between devices, on_device(): recv = lax.all_to_all(send, 'seq', 0, 0, tiled=True)  9.46 us
    dot_general x1, matrix products, on_device(): jnp.einsum('qfb,bk->qfk', spec, ofwd_split, preferred_element_type=f32)  3.98 us
    add x1, other arithmetic, on_device(): z = z_split[..., :2 * size] + z_split[..., 2 * size:]  3.32 us
  transfers between devices with their start and end apart: 1, of which 1 were waited for; matrix products, arithmetic and copies ran while one was open for 2% of the time, Pallas kernels for 0%

profile of v9, /device:TPU:1, one launch (start us, length us, event | category | flops | bytes accessed | tf_op | source)
XLA Modules:
  0.0 72.5 jit_solution(12587767538482008830)
XLA Ops:
  0.0 1.2 %convolution_convert_fusion.1 = bf16[128,4,256]{2,0,1:T(8,128)(2,1)S(1)} fusion(bf16[1,256,128]{2,1,0:T(8,128)(2,1)} %bitcast.50, bf16[1,256,128]{2,1,0:T(8,128)(2,1)} %bitcast.51, bf16[1,256,128]{2,1,0:T(8,128)(2,1)} %bitcast.52, bf16[1,256,128]{2,1,0:T(8,128)(2,1)} %bitcast.53), kind=kOutput, calls=%fused_computation.4 | convolution fusion | flops 34750464 | bytes 524288 | tf_op jit(solution)/shard_map/ck,atk->cat/dot_general | solution.py:79
  1.2 0.2 copy.16
  1.4 0.8 %reshape.106 = bf16[64,16,128]{2,1,0:T(8,128)(2,1)} reshape(bf16[128,4,256]{2,1,0:T(4,128)(2,1)S(1)} %copy.16) | data formatting | bytes 524288 | tf_op jit(solution)/shard_map/reshape | solution.py:82
  2.2 12.9 %all-to-all-start = ((bf16[64,16,128]{2,1,0:T(8,128)(2,1)}), bf16[64,16,128]{2,1,0:T(8,128)(2,1)S(1)}, u32[]{:S(2)}, u32[]{:S(2)}) async-start(bf16[64,16,128]{2,1,0:T(8,128)(2,1)} %reshape.106), calls=%async_computation | async-start | bytes 524288 | tf_op jit(solution)/shard_map/all_to_all | solution.py:83
  15.2 0.7 %dynamic_slice.3 = f32[2]{0:T(128)S(1)} dynamic-slice(f32[128]{0:T(128)} %param.16, s32[]{:T(128)S(6)} %select_n.9), dynamic_slice_sizes={2} | dynamic-slice | bytes 20 | tf_op jit(solution)/shard_map/dynamic_slice | solution.py:115
  16.0 0.1 broadcast_and_fusion
  16.1 0.8 %broadcast_add_fusion = f32[264,128]{1,0:T(8,128)S(1)} fusion(f32[128]{0:T(128)S(1)} %get-tuple-element.11, f32[264]{0:T(512)} %constant.42), kind=kLoop, calls=%fused_computation.34 | loop fusion | flops 33792 | bytes 136736 | tf_op jit(solution)/shard_map/add | solution.py:73
  16.9 9.5 %all-to-all-done = bf16[64,16,128]{2,1,0:T(8,128)(2,1)S(1)} async-done(((bf16[64,16,128]{2,1,0:T(8,128)(2,1)}), bf16[64,16,128]{2,1,0:T(8,128)(2,1)S(1)}, u32[]{:S(2)}, u32[]{:S(2)}) %all-to-all-start) | async-done | bytes 262176 | tf_op jit(solution)/shard_map/all_to_all | solution.py:83
  26.3 0.2 reshape.107
  26.6 4.0 %fusion.1 = f32[6,528,512]{2,1,0:T(8,128)} fusion(bf16[64,512,1]{1,0,2:T(8,128)(2,1)S(1)} %copy-done.2, bf16[6,64,256]{2,1,0:T(8,128)(2,1)S(1)} %bitcast.48, bf16[528,256,1]{1,0,2:T(8,128)(2,1)S(1)} %copy-done.1), kind=kOutput, calls=%fused_computation.3 | convolution fusion | flops 311629824 | bytes 7020544 | tf_op jit(solution)/shard_map/qfb,bk->qfk/dot_general | solution.py:94
  30.6 3.3 %slice_add_fusion = f32[6,528,256]{2,1,0:T(8,128)S(1)} fusion(f32[6,528,512]{2,1,0:T(8,128)} %fusion.1), kind=kLoop, calls=%fused_computation | loop fusion | flops 811008 | bytes 9732096 | tf_op jit(solution)/shard_map/add | solution.py:95
  34.0 0.2 slice_add_fusion.1
  34.1 0.2 multiply_subtract_fusion
  34.3 0.1 multiply_add_fusion
  34.4 0.4 copy-done.4
  34.8 0.4 fusion.5
  35.2 0.4 fusion.4
  35.7 0.4 fusion.3
  36.1 0.1 copy.18
  36.2 0.1 reshape.109
  36.3 15.8 %all_to_all.10 = f32[64,4,128]{2,1,0:T(4,128)S(1)} all-to-all(f32[64,4,128]{2,1,0:T(4,128)S(1)} %reshape.109), channel_id=1, replica_groups=mesh['seq'=64,'ch'=8] {'seq'}, dimensions={0} | all-to-all | bytes 262144 | tf_op jit(solution)/shard_map/all_to_all | solution.py:120
  52.1 0.1 reshape.110
  52.2 19.4 %all-gather.1 = f32[8,1,256]{2,1,0:T(1,128)S(1)} all-gather(f32[1,1,256]{2,1,0:T(1,128)S(1)} %bitcast.49), channel_id=2, replica_groups=mesh['seq'=64,'ch'=8] {'ch'}, dimensions={0}, use_global_device_ids=true | all-gather | bytes 9216 | tf_op jit(solution)/shard_map/all_gather | solution.py:124
  71.6 0.9 %convolution_convert_fusion.2 = bf16[256,128]{1,0:T(8,128)(2,1)} fusion(f32[128,256]{1,0:T(8,128)S(1)} %reshape.110, f32[256]{0:T(256)S(1)} %add_rsqrt_fusion, f32[128]{0:T(128)S(1)} %copy-done.5), kind=kOutput, calls=%fused_computation.8 | convolution fusion | flops 16973824 | bytes 198144 | tf_op jit(solution)/shard_map/tk,ck->tc/dot_general | solution.py:128
  (21 shorter events, 0.3 us)
Async XLA Ops:
  0.0 26.6 %copy-start.1 = (bf16[528,256,1]{1,0,2:T(8,128)(2,1)S(1)}, bf16[528,256,1]{1,0,2:T(8,128)(2,1)}, u32[]{:S(2)}) copy-start(bf16[528,256,1]{1,0,2:T(8,128)(2,1)} %constant.43) | copy-start | bytes 811012
  0.0 26.6 %copy-start.2 = (bf16[64,512,1]{1,0,2:T(8,128)(2,1)S(1)}, bf16[64,512,1]{1,0,2:T(8,128)(2,1)}, u32[]{:S(2)}) copy-start(bf16[64,512,1]{1,0,2:T(8,128)(2,1)} %constant.44) | copy-start | bytes 196612
  2.2 24.1 %all-to-all-start = ((bf16[64,16,128]{2,1,0:T(8,128)(2,1)}), bf16[64,16,128]{2,1,0:T(8,128)(2,1)S(1)}, u32[]{:S(2)}, u32[]{:S(2)}) async-start(bf16[64,16,128]{2,1,0:T(8,128)(2,1)} %reshape.106), calls=%async_computation | async-start | bytes 524288 | tf_op jit(solution)/shard_map/all_to_all | solution.py:83
  33.9 0.8 %copy-start.4 = (f32[256,64,1]{0,1,2:T(8,128)S(1)}, f32[256,64,1]{0,1,2:T(8,128)}, u32[]{:S(2)}) copy-start(f32[256,64,1]{0,1,2:T(8,128)} %constant.45) | copy-start | bytes 196612
  34.1 1.1 %copy-start.3 = (f32[256,64,1]{0,1,2:T(8,128)S(1)}, f32[256,64,1]{0,1,2:T(8,128)}, u32[]{:S(2)}) copy-start(f32[256,64,1]{0,1,2:T(8,128)} %constant.46) | copy-start | bytes 196612
  34.1 1.5 %copy-start = (f32[256,528,1]{0,1,2:T(8,128)S(1)}, f32[256,528,1]{0,1,2:T(8,128)}, u32[]{:S(2)}) copy-start(f32[256,528,1]{0,1,2:T(8,128)} %constant.47) | copy-start | bytes 1622020
  34.3 37.3 %copy-start.5 = (f32[128]{0:T(128)S(1)}, f32[128]{0:T(128)}, u32[]{:S(2)}) copy-start(f32[128]{0:T(128)} %param.17) | copy-start | bytes 1540

commit v10 on v5

--- a/solution.py
+++ b/solution.py
@@ -63,9 +63,8 @@
     ofwd_np, oinv_re_np, oinv_im_np, sign_np, cos_np, msin_np = outer_tables(blocks, fp)
     fwd = jnp.asarray(fwd_np, jnp.bfloat16)
     inv = jnp.asarray(inv_np, f32)
-    ofwd = jnp.asarray(ofwd_np, f32)
-    oinv_re = jnp.asarray(oinv_re_np, f32)
-    oinv_im = jnp.asarray(oinv_im_np, f32)
+    ofwd = jnp.asarray(ofwd_np, jnp.bfloat16)
+    oinv = jnp.asarray(np.concatenate([oinv_re_np, oinv_im_np], axis=1), f32)
     sh_re = jnp.asarray(sign_np, f32) + jnp.asarray(cos_np, f32)
     sh_im = jnp.asarray(msin_np, f32)
 
@@ -86,8 +85,8 @@
     conv_in = conv_in.reshape(blocks, 3 * per, rows_dev).transpose(1, 0, 2)
 
     spec = jnp.einsum("fn,qbn->qfb", fwd, conv_in, preferred_element_type=f32)
-    spec = spec.astype(jnp.bfloat16).astype(f32)
-    z = jnp.einsum("qfb,bk->qfk", spec, ofwd, precision=HIGH, preferred_element_type=f32)
+    spec = spec.astype(jnp.bfloat16)
+    z = jnp.einsum("qfb,bk->qfk", spec, ofwd, preferred_element_type=f32)
     z_re, z_im = z[:, :fp], z[:, fp:]
     x_re = (z_re[..., :size] + z_im[..., size:]).reshape(3, per, fp, size)
     x_im = (z_im[..., :size] - z_re[..., size:]).reshape(3, per, fp, size)
@@ -102,9 +101,8 @@
     y_im = k_re * x_im[0] + k_im * x_re[0]
     y_cat = jnp.concatenate([y_re, y_im], axis=-1)
 
-    t_re = jnp.einsum("cfk,ki->cfi", y_cat, oinv_re, precision=HIGH, preferred_element_type=f32)
-    t_im = jnp.einsum("cfk,ki->cfi", y_cat, oinv_im, precision=HIGH, preferred_element_type=f32)
-    total = jnp.concatenate([t_re, t_im], axis=1)
+    t_both = jnp.einsum("cfk,ki->cfi", y_cat, oinv, precision=HIGH, preferred_element_type=f32)
+    total = jnp.concatenate([t_both[..., :blocks], t_both[..., blocks:]], axis=1)
     conv_t = jnp.einsum("cfi,tf->ict", total, inv, precision=HIGH, preferred_element_type=f32)
 
     skip_here = lax.dynamic_slice_in_dim(skip_gain, own_index * per, per)

time: 67 us -> 68.4 us (1.021)
  other arithmetic: 1.4 us -> 2.73 us
    dot_general x4 -> x2, matrix products: 2.27 us -> 2.38 us  [the longest x1 2 us: on_device(): z = jnp.einsum('qfb,bk->qfk', spec, ofwd, preferred_element_type=f32)]
  transfers between devices with their start and end apart: 1 -> 1, of which waited for: 1 -> 1; matrix products, arithmetic and copies ran while one was open for 2% -> 3% of each run, Pallas kernels for 0% -> 0%
where the time goes in v10:
time: 68.4 us; the launch traced here: 68.1 us
  blocking collectives  35.1 us (51%)
  starting transfers between devices  12.9 us (19%)
  waiting for transfers between devices  8.84 us (13%)
  matrix products  5.12 us (7%)
  local copies, waits for them, and re-layouts  3.12 us (5%)
  other arithmetic  2.73 us (4%)
    all_gather x1, blocking collectives, on_device(): lax.all_gather(partial, 'ch', axis=0, tiled=False)  19.4 us
    all_to_all x1, blocking collectives, on_device(): got = lax.all_to_all(back, 'seq', 0, 0, tiled=True)  15.7 us
    all_to_all x1, starting transfers between devices, on_device(): recv = lax.all_to_all(send, 'seq', 0, 0, tiled=True)  12.9 us
    all_to_all x1, waiting for transfers between devices, on_device(): recv = lax.all_to_all(send, 'seq', 0, 0, tiled=True)  8.84 us
    dot_general x1, matrix products, on_device(): z = jnp.einsum('qfb,bk->qfk', spec, ofwd, preferred_element_type=f32)  2 us
    add x1, other arithmetic, on_device(): sh_re = jnp.asarray(sign_np, f32) + jnp.asarray(cos_np, f32)  1.46 us
  transfers between devices with their start and end apart: 1, of which 1 were waited for; matrix products, arithmetic and copies ran while one was open for 3% of the time, Pallas kernels for 0%

profile of v10, /device:TPU:1, one launch (start us, length us, event | category | flops | bytes accessed | tf_op | source)
XLA Modules:
  0.0 68.1 jit_solution(9300632591467025696)
XLA Ops:
  0.0 1.2 %convolution_convert_fusion.1 = bf16[128,4,256]{2,0,1:T(8,128)(2,1)S(1)} fusion(bf16[1,256,128]{2,1,0:T(8,128)(2,1)} %bitcast.48, bf16[1,256,128]{2,1,0:T(8,128)(2,1)} %bitcast.49, bf16[1,256,128]{2,1,0:T(8,128)(2,1)} %bitcast.50, bf16[1,256,128]{2,1,0:T(8,128)(2,1)} %bitcast.51), kind=kOutput, calls=%fused_computation.3 | convolution fusion | flops 34750464 | bytes 524288 | tf_op jit(solution)/shard_map/ck,atk->cat/dot_general | solution.py:74
  1.2 0.2 copy.19
  1.4 0.8 %reshape.91 = bf16[64,16,128]{2,1,0:T(8,128)(2,1)} reshape(bf16[128,4,256]{2,1,0:T(4,128)(2,1)S(1)} %copy.19) | data formatting | bytes 524288 | tf_op jit(solution)/shard_map/reshape | solution.py:77
  2.2 12.9 %all-to-all-start = ((bf16[64,16,128]{2,1,0:T(8,128)(2,1)}), bf16[64,16,128]{2,1,0:T(8,128)(2,1)S(1)}, u32[]{:S(2)}, u32[]{:S(2)}) async-start(bf16[64,16,128]{2,1,0:T(8,128)(2,1)} %reshape.91), calls=%async_computation | async-start | bytes 524288 | tf_op jit(solution)/shard_map/all_to_all | solution.py:78
  15.1 0.7 %dynamic_slice.3 = f32[2]{0:T(128)S(1)} dynamic-slice(f32[128]{0:T(128)} %param.17, s32[]{:T(128)S(6)} %select_n.9), dynamic_slice_sizes={2} | dynamic-slice | bytes 20 | tf_op jit(solution)/shard_map/dynamic_slice | solution.py:108
  15.9 0.1 broadcast_and_fusion
  16.0 1.5 %broadcast_add_fusion = f32[264,128]{1,0:T(8,128)} fusion(f32[128]{0:T(128)} %constant.44, f32[264]{0:T(512)} %constant.43), kind=kLoop, calls=%fused_computation.34 | loop fusion | flops 33792 | bytes 136736 | tf_op jit(solution)/shard_map/add | solution.py:68
  17.4 8.8 %all-to-all-done = bf16[64,16,128]{2,1,0:T(8,128)(2,1)S(1)} async-done(((bf16[64,16,128]{2,1,0:T(8,128)(2,1)}), bf16[64,16,128]{2,1,0:T(8,128)(2,1)S(1)}, u32[]{:S(2)}, u32[]{:S(2)}) %all-to-all-start) | async-done | bytes 262176 | tf_op jit(solution)/shard_map/all_to_all | solution.py:78
  26.3 0.2 reshape.92
  26.5 0.7 %pad_maximum_fusion = bf16[64,3,2,256]{3,0,2,1:T(8,128)(2,1)} fusion(bf16[64,1,2,256]{3,0,2,1:T(8,128)(2,1)S(1)} %slice_select_fusion, bf16[64,2,2,256]{3,0,2,1:T(8,128)(2,1)S(1)} %slice.85), kind=kLoop, calls=%fused_computation.30 | loop fusion | flops 98304 | bytes 393216 | tf_op jit(solution)/shard_map/stack | solution.py:84
  27.2 2.0 %fusion.1 = f32[6,528,256]{2,1,0:T(8,128)S(1)} fusion(bf16[64,256,1]{1,0,2:T(8,128)(2,1)S(1)} %copy-done.3, bf16[6,64,256]{2,1,0:T(8,128)(2,1)} %bitcast.46, bf16[528,256,1]{1,0,2:T(8,128)(2,1)} %constant.46), kind=kOutput, calls=%fused_computation.2 | convolution fusion | flops 207820800 | bytes 3743744 | tf_op jit(solution)/shard_map/qfb,bk->qfk/dot_general | solution.py:89
  29.3 0.2 slice_add_fusion
  29.5 0.7 %copy-done = f32[264,128]{1,0:T(8,128)S(1)} copy-done((f32[264,128]{1,0:T(8,128)S(1)}, f32[264,128]{1,0:T(8,128)}, u32[]{:S(2)}) %copy-start) | copy-done | bytes 135192
  30.1 0.2 multiply_subtract_fusion
  30.3 0.1 multiply_add_fusion
  30.4 0.4 fusion.4
  30.8 0.1 fusion.25
  31.0 0.7 fusion.3
  31.6 0.1 copy.22
  31.7 0.1 reshape.94
  31.9 15.7 %all_to_all.10 = f32[64,4,128]{2,1,0:T(4,128)S(1)} all-to-all(f32[64,4,128]{2,1,0:T(4,128)S(1)} %reshape.94), channel_id=1, replica_groups=mesh['seq'=64,'ch'=8] {'seq'}, dimensions={0} | all-to-all | bytes 262144 | tf_op jit(solution)/shard_map/all_to_all | solution.py:113
  47.6 0.1 reshape.95
  47.7 19.4 %all-gather.1 = f32[8,1,256]{2,1,0:T(1,128)S(1)} all-gather(f32[1,1,256]{2,1,0:T(1,128)S(1)} %bitcast.47), channel_id=2, replica_groups=mesh['seq'=64,'ch'=8] {'ch'}, dimensions={0}, use_global_device_ids=true | all-gather | bytes 9216 | tf_op jit(solution)/shard_map/all_gather | solution.py:117
  67.2 0.9 %convolution_convert_fusion.2 = bf16[256,128]{1,0:T(8,128)(2,1)} fusion(f32[128,256]{1,0:T(8,128)S(1)} %reshape.95, f32[256]{0:T(256)S(1)} %add_rsqrt_fusion, f32[128]{0:T(128)S(1)} %copy-done.4), kind=kOutput, calls=%fused_computation.7 | convolution fusion | flops 16973824 | bytes 198144 | tf_op jit(solution)/shard_map/tk,ck->tc/dot_general | solution.py:121
  (19 shorter events, 0.2 us)
Async XLA Ops:
  0.0 27.2 %copy-start.3 = (bf16[64,256,1]{1,0,2:T(8,128)(2,1)S(1)}, bf16[64,256,1]{1,0,2:T(8,128)(2,1)}, u32[]{:S(2)}) copy-start(bf16[64,256,1]{1,0,2:T(8,128)(2,1)} %constant.47) | copy-start | bytes 98308
  2.2 24.1 %all-to-all-start = ((bf16[64,16,128]{2,1,0:T(8,128)(2,1)}), bf16[64,16,128]{2,1,0:T(8,128)(2,1)S(1)}, u32[]{:S(2)}, u32[]{:S(2)}) async-start(bf16[64,16,128]{2,1,0:T(8,128)(2,1)} %reshape.91), calls=%async_computation | async-start | bytes 524288 | tf_op jit(solution)/shard_map/all_to_all | solution.py:78
  29.2 0.9 %copy-start = (f32[264,128]{1,0:T(8,128)S(1)}, f32[264,128]{1,0:T(8,128)}, u32[]{:S(2)}) copy-start(f32[264,128]{1,0:T(8,128)} %broadcast_add_fusion) | copy-start | bytes 405508
  29.2 0.9 %copy-start.5 = (f32[128]{0:T(128)S(1)}, f32[128]{0:T(128)}, u32[]{:S(2)}) copy-start(f32[128]{0:T(128)} %constant.45) | copy-start | bytes 1540
  29.3 1.2 %copy-start.2 = (f32[256,128,1]{1,0,2:T(8,128)S(1)}, f32[256,128,1]{1,0,2:T(8,128)}, u32[]{:S(2)}) copy-start(f32[256,128,1]{1,0,2:T(8,128)} %constant.48) | copy-start | bytes 393220
  29.4 1.5 %copy-start.1 = (f32[256,528,1]{0,1,2:T(8,128)S(1)}, f32[256,528,1]{0,1,2:T(8,128)}, u32[]{:S(2)}) copy-start(f32[256,528,1]{0,1,2:T(8,128)} %constant.49) | copy-start | bytes 1622020
  30.3 36.8 %copy-start.4 = (f32[128]{0:T(128)S(1)}, f32[128]{0:T(128)}, u32[]{:S(2)}) copy-start(f32[128]{0:T(128)} %param.18) | copy-start | bytes 1540

commit v11 on v5

--- a/solution.py
+++ b/solution.py
@@ -87,7 +87,7 @@
 
     spec = jnp.einsum("fn,qbn->qfb", fwd, conv_in, preferred_element_type=f32)
     spec = spec.astype(jnp.bfloat16).astype(f32)
-    z = jnp.einsum("qfb,bk->qfk", spec, ofwd, precision=HIGH, preferred_element_type=f32)
+    z = jnp.einsum("qfb,bk->qfk", spec, ofwd, precision=HIGHEST, preferred_element_type=f32)
     z_re, z_im = z[:, :fp], z[:, fp:]
     x_re = (z_re[..., :size] + z_im[..., size:]).reshape(3, per, fp, size)
     x_im = (z_im[..., :size] - z_re[..., size:]).reshape(3, per, fp, size)
@@ -102,8 +102,8 @@
     y_im = k_re * x_im[0] + k_im * x_re[0]
     y_cat = jnp.concatenate([y_re, y_im], axis=-1)
 
-    t_re = jnp.einsum("cfk,ki->cfi", y_cat, oinv_re, precision=HIGH, preferred_element_type=f32)
-    t_im = jnp.einsum("cfk,ki->cfi", y_cat, oinv_im, precision=HIGH, preferred_element_type=f32)
+    t_re = jnp.einsum("cfk,ki->cfi", y_cat, oinv_re, precision=HIGHEST, preferred_element_type=f32)
+    t_im = jnp.einsum("cfk,ki->cfi", y_cat, oinv_im, precision=HIGHEST, preferred_element_type=f32)
     total = jnp.concatenate([t_re, t_im], axis=1)
     conv_t = jnp.einsum("cfi,tf->ict", total, inv, precision=HIGH, preferred_element_type=f32)
 

time: 67 us -> 68 us (1.015)
  matrix products: 4.77 us -> 5.81 us
    dot_general x3, matrix products: 1.92 us -> 2.96 us  [the longest x1 1.49 us: on_device(): jnp.einsum('qfb,bk->qfk', spec, ofwd, precision=HIGHEST, preferred_elemen...]
where the time goes in v11:
time: 68 us; the launch traced here: 67.7 us
  blocking collectives  35.1 us (52%)
  starting transfers between devices  12.9 us (19%)
  waiting for transfers between devices  9.5 us (14%)
  matrix products  5.81 us (9%)
  local copies, waits for them, and re-layouts  2.75 us (4%)
  other arithmetic  1.4 us (2%)
    all_gather x1, blocking collectives, on_device(): lax.all_gather(partial, 'ch', axis=0, tiled=False)  19.4 us
    all_to_all x1, blocking collectives, on_device(): got = lax.all_to_all(back, 'seq', 0, 0, tiled=True)  15.8 us
    all_to_all x1, starting transfers between devices, on_device(): recv = lax.all_to_all(send, 'seq', 0, 0, tiled=True)  12.9 us
    all_to_all x1, waiting for transfers between devices, on_device(): recv = lax.all_to_all(send, 'seq', 0, 0, tiled=True)  9.5 us
    dot_general x1, matrix products, on_device(): jnp.einsum('qfb,bk->qfk', spec, ofwd, precision=HIGHEST, preferred_elemen...  1.49 us
  transfers between devices with their start and end apart: 1, of which 1 were waited for; matrix products, arithmetic and copies ran while one was open for 2% of the time, Pallas kernels for 0%

profile of v11, /device:TPU:1, one launch (start us, length us, event | category | flops | bytes accessed | tf_op | source)
XLA Modules:
  0.0 67.7 jit_solution(8099662524051274147)
XLA Ops:
  0.0 1.2 %convolution_convert_fusion.1 = bf16[128,4,256]{2,0,1:T(8,128)(2,1)S(1)} fusion(bf16[1,256,128]{2,1,0:T(8,128)(2,1)} %bitcast.49, bf16[1,256,128]{2,1,0:T(8,128)(2,1)} %bitcast.50, bf16[1,256,128]{2,1,0:T(8,128)(2,1)} %bitcast.51, bf16[1,256,128]{2,1,0:T(8,128)(2,1)} %bitcast.52), kind=kOutput, calls=%fused_computation.2 | convolution fusion | flops 34750464 | bytes 524288 | tf_op jit(solution)/shard_map/ck,atk->cat/dot_general | solution.py:75
  1.2 0.2 copy.18
  1.4 0.8 %reshape.91 = bf16[64,16,128]{2,1,0:T(8,128)(2,1)} reshape(bf16[128,4,256]{2,1,0:T(4,128)(2,1)S(1)} %copy.18) | data formatting | bytes 524288 | tf_op jit(solution)/shard_map/reshape | solution.py:78
  2.2 12.9 %all-to-all-start = ((bf16[64,16,128]{2,1,0:T(8,128)(2,1)}), bf16[64,16,128]{2,1,0:T(8,128)(2,1)S(1)}, u32[]{:S(2)}, u32[]{:S(2)}) async-start(bf16[64,16,128]{2,1,0:T(8,128)(2,1)} %reshape.91), calls=%async_computation | async-start | bytes 524288 | tf_op jit(solution)/shard_map/all_to_all | solution.py:79
  15.2 0.7 %dynamic_slice.3 = f32[2]{0:T(128)S(1)} dynamic-slice(f32[128]{0:T(128)} %param.18, s32[]{:T(128)S(6)} %select_n.9), dynamic_slice_sizes={2} | dynamic-slice | bytes 20 | tf_op jit(solution)/shard_map/dynamic_slice | solution.py:110
  15.9 0.1 broadcast_and_fusion
  16.0 0.8 %broadcast_add_fusion = f32[264,128]{1,0:T(8,128)S(1)} fusion(f32[128]{0:T(128)} %constant.47, f32[264]{0:T(512)} %constant.46), kind=kLoop, calls=%fused_computation.32 | loop fusion | flops 33792 | bytes 136736 | tf_op jit(solution)/shard_map/add | solution.py:69
  16.8 9.5 %all-to-all-done = bf16[64,16,128]{2,1,0:T(8,128)(2,1)S(1)} async-done(((bf16[64,16,128]{2,1,0:T(8,128)(2,1)}), bf16[64,16,128]{2,1,0:T(8,128)(2,1)S(1)}, u32[]{:S(2)}, u32[]{:S(2)}) %all-to-all-start) | async-done | bytes 262176 | tf_op jit(solution)/shard_map/all_to_all | solution.py:79
  26.3 0.2 reshape.92
  26.6 0.3 fusion
  27.0 1.5 %fusion.23 = f32[6,528,256]{2,1,0:T(8,128)S(1)} fusion(bf16[6,528,64]{1,2,0:T(8,128)(2,1)S(1)} %fusion, f32[64,256,1]{1,0,2:T(8,128)S(1)} %copy-done.4), kind=kOutput, calls=%fused_computation.48 | convolution fusion | flops 622854144 | bytes 3715072 | tf_op jit(solution)/shard_map/qfb,bk->qfk/dot_general | solution.py:90
  28.5 0.2 slice_add_fusion
  28.7 0.4 copy-done.6
  29.1 0.2 multiply_subtract_fusion
  29.3 0.1 multiply_add_fusion
  29.4 0.7 %fusion.4 = f32[2,264,64]{1,2,0:T(8,128)S(1)} fusion(f32[256,64,1]{0,1,2:T(8,128)S(1)} %copy-done.3, f32[2,264,128]{2,1,0:T(8,128)S(1)} %multiply_add_fusion, f32[2,264,128]{2,1,0:T(8,128)S(1)} %get-tuple-element.5), kind=kOutput, calls=%fused_computation.11 | convolution fusion | flops 103944192 | bytes 741376 | tf_op jit(solution)/shard_map/cfk,ki->cfi/dot_general | solution.py:105
  30.2 0.7 %fusion.3 = f32[2,264,64]{1,2,0:T(8,128)S(1)} fusion(f32[256,64,1]{0,1,2:T(8,128)S(1)} %copy-done.2, f32[2,264,128]{2,1,0:T(8,128)S(1)} %multiply_add_fusion, f32[2,264,128]{2,1,0:T(8,128)S(1)} %get-tuple-element.5), kind=kOutput, calls=%fused_computation.10 | convolution fusion | flops 103944192 | bytes 741376 | tf_op jit(solution)/shard_map/cfk,ki->cfi/dot_general | solution.py:106
  30.9 0.4 fusion.2
  31.3 0.1 copy.20
  31.4 0.1 reshape.94
  31.6 15.8 %all_to_all.10 = f32[64,4,128]{2,1,0:T(4,128)S(1)} all-to-all(f32[64,4,128]{2,1,0:T(4,128)S(1)} %reshape.94), channel_id=1, replica_groups=mesh['seq'=64,'ch'=8] {'seq'}, dimensions={0} | all-to-all | bytes 262144 | tf_op jit(solution)/shard_map/all_to_all | solution.py:115
  47.3 0.1 reshape.95
  47.4 19.4 %all-gather.1 = f32[8,1,256]{2,1,0:T(1,128)S(1)} all-gather(f32[1,1,256]{2,1,0:T(1,128)S(1)} %bitcast.48), channel_id=2, replica_groups=mesh['seq'=64,'ch'=8] {'ch'}, dimensions={0}, use_global_device_ids=true | all-gather | bytes 9216 | tf_op jit(solution)/shard_map/all_gather | solution.py:119
  66.8 0.9 %convolution_convert_fusion.2 = bf16[256,128]{1,0:T(8,128)(2,1)} fusion(f32[128,256]{1,0:T(8,128)S(1)} %reshape.95, f32[256]{0:T(256)S(1)} %add_rsqrt_fusion, f32[128]{0:T(128)S(1)} %copy-done.5), kind=kOutput, calls=%fused_computation.6 | convolution fusion | flops 16973824 | bytes 198144 | tf_op jit(solution)/shard_map/tk,ck->tc/dot_general | solution.py:123
  (22 shorter events, 0.2 us)
Async XLA Ops:
  0.0 26.6 %copy-start.1 = (bf16[528,256,1]{1,0,2:T(8,128)(2,1)S(1)}, bf16[528,256,1]{1,0,2:T(8,128)(2,1)}, u32[]{:S(2)}) copy-start(bf16[528,256,1]{1,0,2:T(8,128)(2,1)} %constant.49) | copy-start | bytes 811012
  0.0 27.0 %copy-start.4 = (f32[64,256,1]{1,0,2:T(8,128)S(1)}, f32[64,256,1]{1,0,2:T(8,128)}, u32[]{:S(2)}) copy-start(f32[64,256,1]{1,0,2:T(8,128)} %constant.50) | copy-start | bytes 196612
  2.2 24.1 %all-to-all-start = ((bf16[64,16,128]{2,1,0:T(8,128)(2,1)}), bf16[64,16,128]{2,1,0:T(8,128)(2,1)S(1)}, u32[]{:S(2)}, u32[]{:S(2)}) async-start(bf16[64,16,128]{2,1,0:T(8,128)(2,1)} %reshape.91), calls=%async_computation | async-start | bytes 524288 | tf_op jit(solution)/shard_map/all_to_all | solution.py:79
  28.5 0.7 copy-start.6
  28.5 0.9 %copy-start.3 = (f32[256,64,1]{0,1,2:T(8,128)S(1)}, f32[256,64,1]{0,1,2:T(8,128)}, u32[]{:S(2)}) copy-start(f32[256,64,1]{0,1,2:T(8,128)} %constant.51) | copy-start | bytes 196612
  28.7 1.5 %copy-start.2 = (f32[256,64,1]{0,1,2:T(8,128)S(1)}, f32[256,64,1]{0,1,2:T(8,128)}, u32[]{:S(2)}) copy-start(f32[256,64,1]{0,1,2:T(8,128)} %constant.52) | copy-start | bytes 196612
  28.7 2.2 %copy-start = (f32[256,528,1]{0,1,2:T(8,128)S(1)}, f32[256,528,1]{0,1,2:T(8,128)}, u32[]{:S(2)}) copy-start(f32[256,528,1]{0,1,2:T(8,128)} %constant.53) | copy-start | bytes 1622020
  29.3 37.5 %copy-start.5 = (f32[128]{0:T(128)S(1)}, f32[128]{0:T(128)}, u32[]{:S(2)}) copy-start(f32[128]{0:T(128)} %param.19) | copy-start | bytes 1540

commit v12 on v11

--- a/solution.py
+++ b/solution.py
@@ -63,7 +63,11 @@
     ofwd_np, oinv_re_np, oinv_im_np, sign_np, cos_np, msin_np = outer_tables(blocks, fp)
     fwd = jnp.asarray(fwd_np, jnp.bfloat16)
     inv = jnp.asarray(inv_np, f32)
-    ofwd = jnp.asarray(ofwd_np, f32)
+    part_hi = ofwd_np.astype(np.float32).astype(jnp.bfloat16)
+    rest = ofwd_np - part_hi.astype(np.float64)
+    part_mid = rest.astype(np.float32).astype(jnp.bfloat16)
+    part_lo = (rest - part_mid.astype(np.float64)).astype(np.float32).astype(jnp.bfloat16)
+    ofwd_parts = [jnp.asarray(p, jnp.bfloat16) for p in (part_hi, part_mid, part_lo)]
     oinv_re = jnp.asarray(oinv_re_np, f32)
     oinv_im = jnp.asarray(oinv_im_np, f32)
     sh_re = jnp.asarray(sign_np, f32) + jnp.asarray(cos_np, f32)
@@ -86,8 +90,11 @@
     conv_in = conv_in.reshape(blocks, 3 * per, rows_dev).transpose(1, 0, 2)
 
     spec = jnp.einsum("fn,qbn->qfb", fwd, conv_in, preferred_element_type=f32)
-    spec = spec.astype(jnp.bfloat16).astype(f32)
-    z = jnp.einsum("qfb,bk->qfk", spec, ofwd, precision=HIGHEST, preferred_element_type=f32)
+    spec = spec.astype(jnp.bfloat16)
+    z_parts = [
+        jnp.einsum("qfb,bk->qfk", spec, part, preferred_element_type=f32) for part in ofwd_parts
+    ]
+    z = z_parts[2] + z_parts[1] + z_parts[0]
     z_re, z_im = z[:, :fp], z[:, fp:]
     x_re = (z_re[..., :size] + z_im[..., size:]).reshape(3, per, fp, size)
     x_im = (z_im[..., :size] - z_re[..., size:]).reshape(3, per, fp, size)

time: 68 us -> 68.4 us (level)
    dot_general x1 -> x3, matrix products: 1.49 us -> 1.85 us  [on_device(): jnp.einsum('qfb,bk->qfk', spec, part, preferred_element_type=f32)]
where the time goes in v12:
time: 68.4 us; the launch traced here: 68.1 us
  blocking collectives  35.1 us (51%)
  starting transfers between devices  12.9 us (19%)
  waiting for transfers between devices  9.48 us (14%)
  matrix products  6.17 us (9%)
  local copies, waits for them, and re-layouts  2.76 us (4%)
  other arithmetic  1.4 us (2%)
    all_gather x1, blocking collectives, on_device(): lax.all_gather(partial, 'ch', axis=0, tiled=False)  19.4 us
    all_to_all x1, blocking collectives, on_device(): got = lax.all_to_all(back, 'seq', 0, 0, tiled=True)  15.7 us
    all_to_all x1, starting transfers between devices, on_device(): recv = lax.all_to_all(send, 'seq', 0, 0, tiled=True)  12.9 us
    all_to_all x1, waiting for transfers between devices, on_device(): recv = lax.all_to_all(send, 'seq', 0, 0, tiled=True)  9.48 us
    dot_general x3, matrix products, on_device(): jnp.einsum('qfb,bk->qfk', spec, part, preferred_element_type=f32)  1.85 us
  transfers between devices with their start and end apart: 1, of which 1 were waited for; matrix products, arithmetic and copies ran while one was open for 2% of the time, Pallas kernels for 0%

profile of v12, /device:TPU:1, one launch (start us, length us, event | category | flops | bytes accessed | tf_op | source)
XLA Modules:
  0.0 68.1 jit_solution(10454322726630106207)
XLA Ops:
  0.0 1.2 %convolution_convert_fusion.1 = bf16[128,4,256]{2,0,1:T(8,128)(2,1)S(1)} fusion(bf16[1,256,128]{2,1,0:T(8,128)(2,1)} %bitcast.55, bf16[1,256,128]{2,1,0:T(8,128)(2,1)} %bitcast.56, bf16[1,256,128]{2,1,0:T(8,128)(2,1)} %bitcast.57, bf16[1,256,128]{2,1,0:T(8,128)(2,1)} %bitcast.58), kind=kOutput, calls=%fused_computation.3 | convolution fusion | flops 34750464 | bytes 524288 | tf_op jit(solution)/shard_map/ck,atk->cat/dot_general | solution.py:79
  1.2 0.2 copy.20
  1.4 0.8 %reshape.91 = bf16[64,16,128]{2,1,0:T(8,128)(2,1)} reshape(bf16[128,4,256]{2,1,0:T(4,128)(2,1)S(1)} %copy.20) | data formatting | bytes 524288 | tf_op jit(solution)/shard_map/reshape | solution.py:82
  2.2 12.9 %all-to-all-start = ((bf16[64,16,128]{2,1,0:T(8,128)(2,1)}), bf16[64,16,128]{2,1,0:T(8,128)(2,1)S(1)}, u32[]{:S(2)}, u32[]{:S(2)}) async-start(bf16[64,16,128]{2,1,0:T(8,128)(2,1)} %reshape.91), calls=%async_computation | async-start | bytes 524288 | tf_op jit(solution)/shard_map/all_to_all | solution.py:83
  15.2 0.7 %dynamic_slice.3 = f32[2]{0:T(128)S(1)} dynamic-slice(f32[128]{0:T(128)} %param.20, s32[]{:T(128)S(6)} %select_n.9), dynamic_slice_sizes={2} | dynamic-slice | bytes 20 | tf_op jit(solution)/shard_map/dynamic_slice | solution.py:117
  15.9 0.1 broadcast_and_fusion
  16.0 0.8 %broadcast_add_fusion = f32[264,128]{1,0:T(8,128)S(1)} fusion(f32[128]{0:T(128)} %constant.53, f32[264]{0:T(512)} %constant.52), kind=kLoop, calls=%fused_computation.33 | loop fusion | flops 33792 | bytes 136736 | tf_op jit(solution)/shard_map/add | solution.py:73
  16.8 9.5 %all-to-all-done = bf16[64,16,128]{2,1,0:T(8,128)(2,1)S(1)} async-done(((bf16[64,16,128]{2,1,0:T(8,128)(2,1)}), bf16[64,16,128]{2,1,0:T(8,128)(2,1)S(1)}, u32[]{:S(2)}, u32[]{:S(2)}) %all-to-all-start) | async-done | bytes 262176 | tf_op jit(solution)/shard_map/all_to_all | solution.py:83
  26.3 0.2 reshape.92
  26.6 0.3 fusion
  27.0 0.6 fusion.23
  27.6 0.6 fusion.24
  28.3 0.6 add_add_fusion
  28.9 0.2 slice_add_fusion
  29.1 0.4 copy-done.8
  29.5 0.2 multiply_subtract_fusion
  29.8 0.7 %fusion.4 = f32[2,264,64]{1,2,0:T(8,128)S(1)} fusion(f32[256,64,1]{0,1,2:T(8,128)S(1)} %copy-done.3, f32[2,264,128]{2,1,0:T(8,128)S(1)} %multiply_add_fusion, f32[2,264,128]{2,1,0:T(8,128)S(1)} %get-tuple-element.5), kind=kOutput, calls=%fused_computation.12 | convolution fusion | flops 103944192 | bytes 741376 | tf_op jit(solution)/shard_map/cfk,ki->cfi/dot_general | solution.py:112
  30.6 0.7 %fusion.3 = f32[2,264,64]{1,2,0:T(8,128)S(1)} fusion(f32[256,64,1]{0,1,2:T(8,128)S(1)} %copy-done.2, f32[2,264,128]{2,1,0:T(8,128)S(1)} %multiply_add_fusion, f32[2,264,128]{2,1,0:T(8,128)S(1)} %get-tuple-element.5), kind=kOutput, calls=%fused_computation.11 | convolution fusion | flops 103944192 | bytes 741376 | tf_op jit(solution)/shard_map/cfk,ki->cfi/dot_general | solution.py:113
  31.3 0.4 fusion.2
  31.7 0.1 copy.22
  31.8 0.1 reshape.94
  32.0 15.7 %all_to_all.10 = f32[64,4,128]{2,1,0:T(4,128)S(1)} all-to-all(f32[64,4,128]{2,1,0:T(4,128)S(1)} %reshape.94), channel_id=1, replica_groups=mesh['seq'=64,'ch'=8] {'seq'}, dimensions={0} | all-to-all | bytes 262144 | tf_op jit(solution)/shard_map/all_to_all | solution.py:122
  47.8 19.4 %all-gather.1 = f32[8,1,256]{2,1,0:T(1,128)S(1)} all-gather(f32[1,1,256]{2,1,0:T(1,128)S(1)} %bitcast.54), channel_id=2, replica_groups=mesh['seq'=64,'ch'=8] {'ch'}, dimensions={0}, use_global_device_ids=true | all-gather | bytes 9216 | tf_op jit(solution)/shard_map/all_gather | solution.py:126
  67.2 0.9 %convolution_convert_fusion.2 = bf16[256,128]{1,0:T(8,128)(2,1)} fusion(f32[128,256]{1,0:T(8,128)S(1)} %reshape.95, f32[256]{0:T(256)S(1)} %add_rsqrt_fusion, f32[128]{0:T(128)S(1)} %copy-done.7), kind=kOutput, calls=%fused_computation.7 | convolution fusion | flops 16973824 | bytes 198144 | tf_op jit(solution)/shard_map/tk,ck->tc/dot_general | solution.py:130
  (28 shorter events, 0.4 us)
Async XLA Ops:
  0.0 26.6 %copy-start.1 = (bf16[528,256,1]{1,0,2:T(8,128)(2,1)S(1)}, bf16[528,256,1]{1,0,2:T(8,128)(2,1)}, u32[]{:S(2)}) copy-start(bf16[528,256,1]{1,0,2:T(8,128)(2,1)} %constant.55) | copy-start | bytes 811012
  0.0 27.0 %copy-start.6 = (bf16[64,256,1]{1,0,2:T(8,128)(2,1)S(1)}, bf16[64,256,1]{1,0,2:T(8,128)(2,1)}, u32[]{:S(2)}) copy-start(bf16[64,256,1]{1,0,2:T(8,128)(2,1)} %constant.56) | copy-start | bytes 98308
  2.2 24.1 %all-to-all-start = ((bf16[64,16,128]{2,1,0:T(8,128)(2,1)}), bf16[64,16,128]{2,1,0:T(8,128)(2,1)S(1)}, u32[]{:S(2)}, u32[]{:S(2)}) async-start(bf16[64,16,128]{2,1,0:T(8,128)(2,1)} %reshape.91), calls=%async_computation | async-start | bytes 524288 | tf_op jit(solution)/shard_map/all_to_all | solution.py:83
  16.8 10.8 %copy-start.5 = (bf16[64,256,1]{1,0,2:T(8,128)(2,1)S(1)}, bf16[64,256,1]{1,0,2:T(8,128)(2,1)}, u32[]{:S(2)}) copy-start(bf16[64,256,1]{1,0,2:T(8,128)(2,1)} %constant.57) | copy-start | bytes 98308
  27.0 1.3 %copy-start.4 = (bf16[64,256,1]{1,0,2:T(8,128)(2,1)S(1)}, bf16[64,256,1]{1,0,2:T(8,128)(2,1)}, u32[]{:S(2)}) copy-start(bf16[64,256,1]{1,0,2:T(8,128)(2,1)} %constant.58) | copy-start | bytes 98308
  28.9 0.7 copy-start.8
  28.9 0.9 %copy-start.3 = (f32[256,64,1]{0,1,2:T(8,128)S(1)}, f32[256,64,1]{0,1,2:T(8,128)}, u32[]{:S(2)}) copy-start(f32[256,64,1]{0,1,2:T(8,128)} %constant.59) | copy-start | bytes 196612
  29.1 1.5 %copy-start.2 = (f32[256,64,1]{0,1,2:T(8,128)S(1)}, f32[256,64,1]{0,1,2:T(8,128)}, u32[]{:S(2)}) copy-start(f32[256,64,1]{0,1,2:T(8,128)} %constant.60) | copy-start | bytes 196612
  29.1 2.2 %copy-start = (f32[256,528,1]{0,1,2:T(8,128)S(1)}, f32[256,528,1]{0,1,2:T(8,128)}, u32[]{:S(2)}) copy-start(f32[256,528,1]{0,1,2:T(8,128)} %constant.61) | copy-start | bytes 1622020
  29.7 37.5 %copy-start.7 = (f32[128]{0:T(128)S(1)}, f32[128]{0:T(128)}, u32[]{:S(2)}) copy-start(f32[128]{0:T(128)} %param.21) | copy-start | bytes 1540

commit v13 on v11

--- a/solution.py
+++ b/solution.py
@@ -64,8 +64,7 @@
     fwd = jnp.asarray(fwd_np, jnp.bfloat16)
     inv = jnp.asarray(inv_np, f32)
     ofwd = jnp.asarray(ofwd_np, f32)
-    oinv_re = jnp.asarray(oinv_re_np, f32)
-    oinv_im = jnp.asarray(oinv_im_np, f32)
+    oinv = jnp.asarray(np.concatenate([oinv_re_np, oinv_im_np], axis=1), f32)
     sh_re = jnp.asarray(sign_np, f32) + jnp.asarray(cos_np, f32)
     sh_im = jnp.asarray(msin_np, f32)
 
@@ -102,9 +101,8 @@
     y_im = k_re * x_im[0] + k_im * x_re[0]
     y_cat = jnp.concatenate([y_re, y_im], axis=-1)
 
-    t_re = jnp.einsum("cfk,ki->cfi", y_cat, oinv_re, precision=HIGHEST, preferred_element_type=f32)
-    t_im = jnp.einsum("cfk,ki->cfi", y_cat, oinv_im, precision=HIGHEST, preferred_element_type=f32)
-    total = jnp.concatenate([t_re, t_im], axis=1)
+    t_both = jnp.einsum("cfk,ki->cfi", y_cat, oinv, precision=HIGHEST, preferred_element_type=f32)
+    total = jnp.concatenate([t_both[..., :blocks], t_both[..., blocks:]], axis=1)
     conv_t = jnp.einsum("cfi,tf->ict", total, inv, precision=HIGH, preferred_element_type=f32)
 
     skip_here = lax.dynamic_slice_in_dim(skip_gain, own_index * per, per)

time: 68 us -> 67.5 us (level)
    dot_general x2 -> x1, matrix products: 1.47 us -> 0.59 us  [on_device(): jnp.einsum('cfk,ki->cfi', y_cat, oinv, precision=HIGHEST, preferred_eleme...]
where the time goes in v13:
time: 67.5 us; the launch traced here: 67.3 us
  blocking collectives  35.1 us (52%)
  starting transfers between devices  12.9 us (19%)
  waiting for transfers between devices  9.5 us (14%)
  matrix products  5.21 us (8%)
  local copies, waits for them, and re-layouts  2.88 us (4%)
  other arithmetic  1.4 us (2%)
    all_gather x1, blocking collectives, on_device(): lax.all_gather(partial, 'ch', axis=0, tiled=False)  19.4 us
    all_to_all x1, blocking collectives, on_device(): got = lax.all_to_all(back, 'seq', 0, 0, tiled=True)  15.8 us
    all_to_all x1, starting transfers between devices, on_device(): recv = lax.all_to_all(send, 'seq', 0, 0, tiled=True)  12.9 us
    all_to_all x1, waiting for transfers between devices, on_device(): recv = lax.all_to_all(send, 'seq', 0, 0, tiled=True)  9.5 us
    dot_general x1, matrix products, on_device(): jnp.einsum('qfb,bk->qfk', spec, ofwd, precision=HIGHEST, preferred_elemen...  1.49 us
  transfers between devices with their start and end apart: 1, of which 1 were waited for; matrix products, arithmetic and copies ran while one was open for 2% of the time, Pallas kernels for 0%

profile of v13, /device:TPU:1, one launch (start us, length us, event | category | flops | bytes accessed | tf_op | source)
XLA Modules:
  0.0 67.3 jit_solution(10627164528224713251)
XLA Ops:
  0.0 1.2 %convolution_convert_fusion.1 = bf16[128,4,256]{2,0,1:T(8,128)(2,1)S(1)} fusion(bf16[1,256,128]{2,1,0:T(8,128)(2,1)} %bitcast.47, bf16[1,256,128]{2,1,0:T(8,128)(2,1)} %bitcast.48, bf16[1,256,128]{2,1,0:T(8,128)(2,1)} %bitcast.49, bf16[1,256,128]{2,1,0:T(8,128)(2,1)} %bitcast.50), kind=kOutput, calls=%fused_computation.2 | convolution fusion | flops 34750464 | bytes 524288 | tf_op jit(solution)/shard_map/ck,atk->cat/dot_general | solution.py:74
  1.2 0.2 copy.19
  1.4 0.8 %reshape.91 = bf16[64,16,128]{2,1,0:T(8,128)(2,1)} reshape(bf16[128,4,256]{2,1,0:T(4,128)(2,1)S(1)} %copy.19) | data formatting | bytes 524288 | tf_op jit(solution)/shard_map/reshape | solution.py:77
  2.2 12.9 %all-to-all-start = ((bf16[64,16,128]{2,1,0:T(8,128)(2,1)}), bf16[64,16,128]{2,1,0:T(8,128)(2,1)S(1)}, u32[]{:S(2)}, u32[]{:S(2)}) async-start(bf16[64,16,128]{2,1,0:T(8,128)(2,1)} %reshape.91), calls=%async_computation | async-start | bytes 524288 | tf_op jit(solution)/shard_map/all_to_all | solution.py:78
  15.2 0.7 %dynamic_slice.3 = f32[2]{0:T(128)S(1)} dynamic-slice(f32[128]{0:T(128)} %param.17, s32[]{:T(128)S(6)} %select_n.9), dynamic_slice_sizes={2} | dynamic-slice | bytes 20 | tf_op jit(solution)/shard_map/dynamic_slice | solution.py:108
  15.9 0.1 broadcast_and_fusion
  16.0 0.8 %broadcast_add_fusion = f32[264,128]{1,0:T(8,128)S(1)} fusion(f32[128]{0:T(128)} %constant.44, f32[264]{0:T(512)} %constant.43), kind=kLoop, calls=%fused_computation.33 | loop fusion | flops 33792 | bytes 136736 | tf_op jit(solution)/shard_map/add | solution.py:68
  16.8 9.5 %all-to-all-done = bf16[64,16,128]{2,1,0:T(8,128)(2,1)S(1)} async-done(((bf16[64,16,128]{2,1,0:T(8,128)(2,1)}), bf16[64,16,128]{2,1,0:T(8,128)(2,1)S(1)}, u32[]{:S(2)}, u32[]{:S(2)}) %all-to-all-start) | async-done | bytes 262176 | tf_op jit(solution)/shard_map/all_to_all | solution.py:78
  26.3 0.2 reshape.92
  26.6 0.3 fusion
  27.0 1.5 %fusion.25 = f32[6,528,256]{2,1,0:T(8,128)S(1)} fusion(bf16[6,528,64]{1,2,0:T(8,128)(2,1)S(1)} %fusion, f32[64,256,1]{1,0,2:T(8,128)S(1)} %copy-done.3), kind=kOutput, calls=%fused_computation.49 | convolution fusion | flops 622854144 | bytes 3715072 | tf_op jit(solution)/shard_map/qfb,bk->qfk/dot_general | solution.py:89
  28.5 0.2 slice_add_fusion
  28.7 0.5 copy-done.5
  29.1 0.2 multiply_subtract_fusion
  29.3 0.1 multiply_add_fusion
  29.4 0.6 fusion.3
  30.0 0.1 fusion.24
  30.2 0.7 %fusion.2 = f32[64,2,256]{2,0,1:T(8,128)S(1)} fusion(f32[256,528,1]{0,1,2:T(8,128)S(1)} %copy-done, f32[2,264,64]{2,1,0:T(8,128)S(1)} %get-tuple-element.11, f32[2,264,64]{2,1,0:T(8,128)S(1)} %get-tuple-element.10, bf16[64,4,2,256]{3,0,2,1:T(8,128)(2,1)S(1)} %bitcast.44, f32[2]{0:T(128)S(1)} %dynamic_slice.3), kind=kOutput, calls=%fused_computation.5 | convolution fusion | flops 104040448 | bytes 1073160 | tf_op jit(solution)/shard_map/cfi,tf->ict/dot_general | solution.py:106
  30.8 0.1 copy.22
  31.0 0.1 reshape.94
  31.1 15.8 %all_to_all.10 = f32[64,4,128]{2,1,0:T(4,128)S(1)} all-to-all(f32[64,4,128]{2,1,0:T(4,128)S(1)} %reshape.94), channel_id=1, replica_groups=mesh['seq'=64,'ch'=8] {'seq'}, dimensions={0} | all-to-all | bytes 262144 | tf_op jit(solution)/shard_map/all_to_all | solution.py:113
  46.9 0.1 reshape.95
  47.0 19.4 %all-gather.1 = f32[8,1,256]{2,1,0:T(1,128)S(1)} all-gather(f32[1,1,256]{2,1,0:T(1,128)S(1)} %bitcast.46), channel_id=2, replica_groups=mesh['seq'=64,'ch'=8] {'ch'}, dimensions={0}, use_global_device_ids=true | all-gather | bytes 9216 | tf_op jit(solution)/shard_map/all_gather | solution.py:117
  66.4 0.9 %convolution_convert_fusion.2 = bf16[256,128]{1,0:T(8,128)(2,1)} fusion(f32[128,256]{1,0:T(8,128)S(1)} %reshape.95, f32[256]{0:T(256)S(1)} %add_rsqrt_fusion, f32[128]{0:T(128)S(1)} %copy-done.4), kind=kOutput, calls=%fused_computation.6 | convolution fusion | flops 16973824 | bytes 198144 | tf_op jit(solution)/shard_map/tk,ck->tc/dot_general | solution.py:121
  (20 shorter events, 0.2 us)
Async XLA Ops:
  0.0 26.6 %copy-start.1 = (bf16[528,256,1]{1,0,2:T(8,128)(2,1)S(1)}, bf16[528,256,1]{1,0,2:T(8,128)(2,1)}, u32[]{:S(2)}) copy-start(bf16[528,256,1]{1,0,2:T(8,128)(2,1)} %constant.46) | copy-start | bytes 811012
  0.0 27.0 %copy-start.3 = (f32[64,256,1]{1,0,2:T(8,128)S(1)}, f32[64,256,1]{1,0,2:T(8,128)}, u32[]{:S(2)}) copy-start(f32[64,256,1]{1,0,2:T(8,128)} %constant.47) | copy-start | bytes 196612
  2.2 24.1 %all-to-all-start = ((bf16[64,16,128]{2,1,0:T(8,128)(2,1)}), bf16[64,16,128]{2,1,0:T(8,128)(2,1)S(1)}, u32[]{:S(2)}, u32[]{:S(2)}) async-start(bf16[64,16,128]{2,1,0:T(8,128)(2,1)} %reshape.91), calls=%async_computation | async-start | bytes 524288 | tf_op jit(solution)/shard_map/all_to_all | solution.py:78
  28.5 0.7 copy-start.5
  28.5 0.9 %copy-start.2 = (f32[256,128,1]{1,0,2:T(8,128)S(1)}, f32[256,128,1]{1,0,2:T(8,128)}, u32[]{:S(2)}) copy-start(f32[256,128,1]{1,0,2:T(8,128)} %constant.48) | copy-start | bytes 393220
  28.7 1.5 %copy-start = (f32[256,528,1]{0,1,2:T(8,128)S(1)}, f32[256,528,1]{0,1,2:T(8,128)}, u32[]{:S(2)}) copy-start(f32[256,528,1]{0,1,2:T(8,128)} %constant.49) | copy-start | bytes 1622020
  29.3 37.1 %copy-start.4 = (f32[128]{0:T(128)S(1)}, f32[128]{0:T(128)}, u32[]{:S(2)}) copy-start(f32[128]{0:T(128)} %param.18) | copy-start | bytes 1540

commit v14 on v13

--- a/solution.py
+++ b/solution.py
@@ -39,6 +39,8 @@
     m = np.arange(size)[None, :]
     phase = 2 * np.pi * ((j * m) % size) / size
     fwd = np.concatenate([np.cos(phase), np.sin(phase)], axis=1)
+    phase1 = 2 * np.pi * (((j + 1) * m) % size) / size
+    fwd_shift = np.concatenate([np.cos(phase1), np.sin(phase1)], axis=1)
     mi = np.arange(size)[:, None]
     i = np.arange(blocks)[None, :]
     phase_i = 2 * np.pi * ((mi * i) % size) / size
@@ -48,7 +50,7 @@
     inv_im = np.concatenate([sin_i, cos_i], axis=0)
     sign = np.where(np.arange(fp) % 2 == 0, 1.0, -1.0)[:, None]
     step = 2 * np.pi * np.arange(size)[None, :] / size
-    return fwd, inv_re, inv_im, sign, np.cos(step), -np.sin(step)
+    return fwd, fwd_shift, inv_re, inv_im
 
 
 def on_device(inputs, gate_values, causal_filter, anti_filter, skip_gain, norm_gain):
@@ -60,13 +62,12 @@
     own_index = lax.axis_index("seq")
 
     fp, fwd_np, inv_np = inner_tables(rows_dev)
-    ofwd_np, oinv_re_np, oinv_im_np, sign_np, cos_np, msin_np = outer_tables(blocks, fp)
+    ofwd_np, oshift_np, oinv_re_np, oinv_im_np = outer_tables(blocks, fp)
     fwd = jnp.asarray(fwd_np, jnp.bfloat16)
     inv = jnp.asarray(inv_np, f32)
     ofwd = jnp.asarray(ofwd_np, f32)
+    oseg = jnp.asarray(np.concatenate([oshift_np, ofwd_np], axis=0), f32)
     oinv = jnp.asarray(np.concatenate([oinv_re_np, oinv_im_np], axis=1), f32)
-    sh_re = jnp.asarray(sign_np, f32) + jnp.asarray(cos_np, f32)
-    sh_im = jnp.asarray(msin_np, f32)
 
     stacked = jnp.stack([inputs, causal_filter, anti_filter, gate_values])
     lanes = 128
@@ -86,19 +87,24 @@
 
     spec = jnp.einsum("fn,qbn->qfb", fwd, conv_in, preferred_element_type=f32)
     spec = spec.astype(jnp.bfloat16).astype(f32)
-    z = jnp.einsum("qfb,bk->qfk", spec, ofwd, precision=HIGHEST, preferred_element_type=f32)
-    z_re, z_im = z[:, :fp], z[:, fp:]
-    x_re = (z_re[..., :size] + z_im[..., size:]).reshape(3, per, fp, size)
-    x_im = (z_im[..., :size] - z_re[..., size:]).reshape(3, per, fp, size)
+    spec = spec.reshape(3, per, 2 * fp, blocks)
+    row_ids = lax.broadcasted_iota(jnp.int32, (2 * fp, 1), 0)
+    sign = (1 - 2 * (row_ids % 2)).astype(f32)
+    filt = spec[1:]
+    seg_in = jnp.concatenate([filt, sign * filt], axis=-1)
+    z_x = jnp.einsum("cfb,bk->cfk", spec[0], ofwd, precision=HIGHEST, preferred_element_type=f32)
+    z_s = jnp.einsum("acfb,bk->acfk", seg_in, oseg, precision=HIGHEST, preferred_element_type=f32)
 
-    c_re = sh_re * x_re[1] - sh_im * x_im[1]
-    c_im = sh_re * x_im[1] + sh_im * x_re[1]
-    a_re = sh_re * x_re[2] - sh_im * x_im[2]
-    a_im = sh_re * x_im[2] + sh_im * x_re[2]
-    k_re = c_re + a_re
-    k_im = c_im - a_im
-    y_re = k_re * x_re[0] - k_im * x_im[0]
-    y_im = k_re * x_im[0] + k_im * x_re[0]
+    def halves(z):
+        z_re, z_im = z[..., :fp, :], z[..., fp:, :]
+        return z_re[..., :size] + z_im[..., size:], z_im[..., :size] - z_re[..., size:]
+
+    x_re, x_im = halves(z_x)
+    s_re, s_im = halves(z_s)
+    k_re = s_re[0] + s_re[1]
+    k_im = s_im[0] - s_im[1]
+    y_re = k_re * x_re - k_im * x_im
+    y_im = k_re * x_im + k_im * x_re
     y_cat = jnp.concatenate([y_re, y_im], axis=-1)
 
     t_both = jnp.einsum("cfk,ki->cfi", y_cat, oinv, precision=HIGHEST, preferred_element_type=f32)

time: 67.5 us -> 70.8 us (1.049)
  waiting for transfers between devices: 9.5 us -> 11 us
  matrix products: 5.21 us -> 6.57 us
  local copies, waits for them, and re-layouts: 2.88 us -> 3.99 us
  other arithmetic: 1.4 us -> 0.56 us
    unnamed x12 -> x14, local copies, waits for them, and re-layouts: 0.49 us -> 2.22 us
    all_to_all x1, waiting for transfers between devices: 9.5 us -> 11 us  [on_device(): recv = lax.all_to_all(send, 'seq', 0, 0, tiled=True)]
    dot_general x1 -> x2, matrix products: 1.49 us -> 2.89 us  [the longest x1 2.25 us: on_device(): jnp.einsum('acfb,bk->acfk', seg_in, oseg, precision=HIGHEST, preferred_el...]
    add x3 -> x0, other arithmetic: 1.04 us -> none  [the longest x1 0.8 us: on_device(): sh_re = jnp.asarray(sign_np, f32) + jnp.asarray(cos_np, f32)]
  transfers between devices with their start and end apart: 1 -> 1, of which waited for: 1 -> 1; matrix products, arithmetic and copies ran while one was open for 2% -> 0% of each run, Pallas kernels for 0% -> 0%
where the time goes in v14:
time: 70.8 us; the launch traced here: 70.5 us
  blocking collectives  35.1 us (50%)
  starting transfers between devices  13.1 us (19%)
  waiting for transfers between devices  11 us (16%)
  matrix products  6.57 us (9%)
  local copies, waits for them, and re-layouts  3.99 us (6%)
    all_gather x1, blocking collectives, on_device(): lax.all_gather(partial, 'ch', axis=0, tiled=False)  19.4 us
    all_to_all x1, blocking collectives, on_device(): got = lax.all_to_all(back, 'seq', 0, 0, tiled=True)  15.8 us
    all_to_all x1, starting transfers between devices, on_device(): recv = lax.all_to_all(send, 'seq', 0, 0, tiled=True)  13.1 us
    all_to_all x1, waiting for transfers between devices, on_device(): recv = lax.all_to_all(send, 'seq', 0, 0, tiled=True)  11 us
    dot_general x1, matrix products, on_device(): jnp.einsum('acfb,bk->acfk', seg_in, oseg, precision=HIGHEST, preferred_el...  2.25 us
    unnamed x14, local copies, waits for them, and re-layouts  2.22 us
  transfers between devices with their start and end apart: 1, of which 1 were waited for; matrix products, arithmetic and copies ran while one was open for 0% of the time, Pallas kernels for 0%

profile of v14, /device:TPU:1, one launch (start us, length us, event | category | flops | bytes accessed | tf_op | source)
XLA Modules:
  0.0 70.5 jit_solution(11966158720901667939)
XLA Ops:
  0.0 1.2 %convolution_convert_fusion.1 = bf16[128,4,256]{2,0,1:T(8,128)(2,1)S(1)} fusion(bf16[1,256,128]{2,1,0:T(8,128)(2,1)} %bitcast.67, bf16[1,256,128]{2,1,0:T(8,128)(2,1)} %bitcast.68, bf16[1,256,128]{2,1,0:T(8,128)(2,1)} %bitcast.69, bf16[1,256,128]{2,1,0:T(8,128)(2,1)} %bitcast.70), kind=kOutput, calls=%fused_computation.6 | convolution fusion | flops 34750464 | bytes 524288 | tf_op jit(solution)/shard_map/ck,atk->cat/dot_general | solution.py:75
  1.2 0.2 copy.27
  1.4 0.8 %reshape.75 = bf16[64,16,128]{2,1,0:T(8,128)(2,1)} reshape(bf16[128,4,256]{2,1,0:T(4,128)(2,1)S(1)} %copy.27) | data formatting | bytes 524288 | tf_op jit(solution)/shard_map/reshape | solution.py:78
  2.2 13.1 %all-to-all-start = ((bf16[64,16,128]{2,1,0:T(8,128)(2,1)}), bf16[64,16,128]{2,1,0:T(8,128)(2,1)S(1)}, u32[]{:S(2)}, u32[]{:S(2)}) async-start(bf16[64,16,128]{2,1,0:T(8,128)(2,1)} %reshape.75), calls=%async_computation | async-start | bytes 524288 | tf_op jit(solution)/shard_map/all_to_all | solution.py:79
  15.3 0.1 dynamic_slice.3
  15.4 0.1 broadcast_and_fusion
  15.5 11.0 %all-to-all-done = bf16[64,16,128]{2,1,0:T(8,128)(2,1)S(1)} async-done(((bf16[64,16,128]{2,1,0:T(8,128)(2,1)}), bf16[64,16,128]{2,1,0:T(8,128)(2,1)S(1)}, u32[]{:S(2)}, u32[]{:S(2)}) %all-to-all-start) | async-done | bytes 262176 | tf_op jit(solution)/shard_map/all_to_all | solution.py:79
  26.4 0.2 reshape.76
  26.7 0.3 fusion.4
  27.2 0.7 %copy-done.2 = f32[128,256,1,1]{1,0,3,2:T(8,128)S(1)} copy-done((f32[128,256,1,1]{1,0,3,2:T(8,128)S(1)}, f32[128,256,1,1]{1,0,3,2:T(8,128)}, u32[]{:S(2)}) %copy-start.2) | copy-done | bytes 131096
  28.0 2.3 %fusion = f32[2,2,528,256]{3,2,1,0:T(8,128)S(1)} fusion(f32[128,256,1,1]{1,0,3,2:T(8,128)S(1)} %copy-done.2, f32[2,2,528,64]{2,3,1,0:T(8,128)S(1)} %broadcast_multiply_fusion, f32[2,2,528,64]{2,3,1,0:T(8,128)S(1)} %convert.4), kind=kOutput, calls=%fused_computation | convolution fusion | flops 830742528 | bytes 3375104 | tf_op jit(solution)/shard_map/acfb,bk->acfk/dot_general | solution.py:96
  30.2 0.1 slice_subtract_fusion
  30.4 0.7 %copy-done.4 = f32[64,256,1]{1,0,2:T(8,128)S(1)} copy-done((f32[64,256,1]{1,0,2:T(8,128)S(1)}, f32[64,256,1]{1,0,2:T(8,128)}, u32[]{:S(2)}) %copy-start.4) | copy-done | bytes 65560
  31.1 0.6 fusion.38
  31.7 0.2 multiply_subtract_fusion
  31.9 0.7 %copy-done.3 = f32[256,128,1]{1,0,2:T(8,128)S(1)} copy-done((f32[256,128,1]{1,0,2:T(8,128)S(1)}, f32[256,128,1]{1,0,2:T(8,128)}, u32[]{:S(2)}) %copy-start.3) | copy-done | bytes 131096
  32.6 0.6 fusion.7
  33.2 0.1 fusion.37
  33.4 0.7 fusion.6
  34.1 0.1 copy.31
  34.2 0.1 reshape.78
  34.3 15.8 %all_to_all.10 = f32[64,4,128]{2,1,0:T(4,128)S(1)} all-to-all(f32[64,4,128]{2,1,0:T(4,128)S(1)} %reshape.78), channel_id=1, replica_groups=mesh['seq'=64,'ch'=8] {'seq'}, dimensions={0} | all-to-all | bytes 262144 | tf_op jit(solution)/shard_map/all_to_all | solution.py:119
  50.2 19.4 %all-gather.1 = f32[8,1,256]{2,1,0:T(1,128)S(1)} all-gather(f32[1,1,256]{2,1,0:T(1,128)S(1)} %bitcast.66), channel_id=2, replica_groups=mesh['seq'=64,'ch'=8] {'ch'}, dimensions={0}, use_global_device_ids=true | all-gather | bytes 9216 | tf_op jit(solution)/shard_map/all_gather | solution.py:123
  69.6 0.9 %convolution_convert_fusion.2 = bf16[256,128]{1,0:T(8,128)(2,1)} fusion(f32[128,256]{1,0:T(8,128)S(1)} %reshape.79, f32[256]{0:T(256)S(1)} %add_rsqrt_fusion, f32[128]{0:T(128)S(1)} %copy-done.5), kind=kOutput, calls=%fused_computation.10 | convolution fusion | flops 16973824 | bytes 198144 | tf_op jit(solution)/shard_map/tk,ck->tc/dot_general | solution.py:127
  (25 shorter events, 0.4 us)
Async XLA Ops:
  0.0 15.3 %copy-start.6 = (f32[128]{0:T(128)S(1)}, f32[128]{0:T(128)}, u32[]{:S(2)}) copy-start(f32[128]{0:T(128)} %param.15) | copy-start | bytes 1540
  2.2 24.5 %copy-start.1 = (bf16[528,256,1]{1,0,2:T(8,128)(2,1)S(1)}, bf16[528,256,1]{1,0,2:T(8,128)(2,1)}, u32[]{:S(2)}) copy-start(bf16[528,256,1]{1,0,2:T(8,128)(2,1)} %constant.52) | copy-start | bytes 811012
  2.2 24.2 %all-to-all-start = ((bf16[64,16,128]{2,1,0:T(8,128)(2,1)}), bf16[64,16,128]{2,1,0:T(8,128)(2,1)S(1)}, u32[]{:S(2)}, u32[]{:S(2)}) async-start(bf16[64,16,128]{2,1,0:T(8,128)(2,1)} %reshape.75), calls=%async_computation | async-start | bytes 524288 | tf_op jit(solution)/shard_map/all_to_all | solution.py:79
  27.1 0.9 %copy-start.2 = (f32[128,256,1,1]{1,0,3,2:T(8,128)S(1)}, f32[128,256,1,1]{1,0,3,2:T(8,128)}, u32[]{:S(2)}) copy-start(f32[128,256,1,1]{1,0,3,2:T(8,128)} %constant.53) | copy-start | bytes 393220
  30.2 0.8 %copy-start.4 = (f32[64,256,1]{1,0,2:T(8,128)S(1)}, f32[64,256,1]{1,0,2:T(8,128)}, u32[]{:S(2)}) copy-start(f32[64,256,1]{1,0,2:T(8,128)} %constant.54) | copy-start | bytes 196612
  31.7 0.9 %copy-start.3 = (f32[256,128,1]{1,0,2:T(8,128)S(1)}, f32[256,128,1]{1,0,2:T(8,128)}, u32[]{:S(2)}) copy-start(f32[256,128,1]{1,0,2:T(8,128)} %constant.55) | copy-start | bytes 393220
  31.9 1.5 %copy-start = (f32[256,528,1]{0,1,2:T(8,128)S(1)}, f32[256,528,1]{0,1,2:T(8,128)}, u32[]{:S(2)}) copy-start(f32[256,528,1]{0,1,2:T(8,128)} %constant.56) | copy-start | bytes 1622020
  33.4 36.2 %copy-start.5 = (f32[128]{0:T(128)S(1)}, f32[128]{0:T(128)}, u32[]{:S(2)}) copy-start(f32[128]{0:T(128)} %param.16) | copy-start | bytes 1540

commit v15 on v13

--- a/solution.py
+++ b/solution.py
@@ -68,7 +68,9 @@
     sh_re = jnp.asarray(sign_np, f32) + jnp.asarray(cos_np, f32)
     sh_im = jnp.asarray(msin_np, f32)
 
-    stacked = jnp.stack([inputs, causal_filter, anti_filter, gate_values])
+    row_ids = lax.broadcasted_iota(jnp.int32, (rows_dev, 1), 0) + own_index * rows_dev
+    anti_masked = jnp.where(row_ids > 0, anti_filter, jnp.zeros_like(anti_filter))
+    stacked = jnp.stack([inputs, causal_filter, anti_masked, gate_values])
     lanes = 128
     eye_ch = jnp.eye(chan_dev, dtype=jnp.bfloat16)
     by_channel = jnp.einsum(
@@ -77,12 +79,7 @@
     send = by_channel.reshape(blocks, per * 4 * rows_dev // lanes, lanes)
     recv = lax.all_to_all(send, "seq", 0, 0, tiled=True)
     series = recv.reshape(blocks, per, 4, rows_dev).transpose(0, 2, 1, 3)
-    block_ids = lax.broadcasted_iota(jnp.int32, (blocks, 1, rows_dev), 0)
-    tok_ids = lax.broadcasted_iota(jnp.int32, (blocks, 1, rows_dev), 2)
-    first_row = jnp.logical_and(block_ids == 0, tok_ids == 0)
-    anti_rows = jnp.where(first_row, jnp.zeros_like(series[:, 2]), series[:, 2])
-    conv_in = jnp.stack([series[:, 0], series[:, 1], anti_rows], axis=1)
-    conv_in = conv_in.reshape(blocks, 3 * per, rows_dev).transpose(1, 0, 2)
+    conv_in = series[:, :3].reshape(blocks, 3 * per, rows_dev).transpose(1, 0, 2)
 
     spec = jnp.einsum("fn,qbn->qfb", fwd, conv_in, preferred_element_type=f32)
     spec = spec.astype(jnp.bfloat16).astype(f32)

time: 67.5 us -> 68.5 us (1.015)
  other arithmetic: 1.4 us -> 2.27 us
    another operation x1, other arithmetic: 0.02 us -> 0.99 us  [on_device(): stacked = jnp.stack([inputs, causal_filter, anti_masked, gate_values])]
where the time goes in v15:
time: 68.5 us; the launch traced here: 68.2 us
  blocking collectives  35.1 us (51%)
  starting transfers between devices  12.9 us (19%)
  waiting for transfers between devices  9.61 us (14%)
  matrix products  5.13 us (7%)
  local copies, waits for them, and re-layouts  2.89 us (4%)
  other arithmetic  2.27 us (3%)
    all_gather x1, blocking collectives, on_device(): lax.all_gather(partial, 'ch', axis=0, tiled=False)  19.4 us
    all_to_all x1, blocking collectives, on_device(): got = lax.all_to_all(back, 'seq', 0, 0, tiled=True)  15.8 us
    all_to_all x1, starting transfers between devices, on_device(): recv = lax.all_to_all(send, 'seq', 0, 0, tiled=True)  12.9 us
    all_to_all x1, waiting for transfers between devices, on_device(): recv = lax.all_to_all(send, 'seq', 0, 0, tiled=True)  9.61 us
    dot_general x1, matrix products, on_device(): jnp.einsum('qfb,bk->qfk', spec, ofwd, precision=HIGHEST, preferred_elemen...  1.49 us
  transfers between devices with their start and end apart: 1, of which 1 were waited for; matrix products, arithmetic and copies ran while one was open for 2% of the time, Pallas kernels for 0%

profile of v15, /device:TPU:1, one launch (start us, length us, event | category | flops | bytes accessed | tf_op | source)
XLA Modules:
  0.0 68.2 jit_solution(9275611886983770100)
XLA Ops:
  0.0 1.0 %select_bitcast_fusion = bf16[1,256,128]{2,1,0:T(8,128)(2,1)S(1)} fusion(bf16[256,128]{1,0:T(8,128)(2,1)} %param.16, pred[256]{0:T(512)(128)(4,1)S(1)} %add_compare_fusion), kind=kLoop, calls=%fused_computation.36 | loop fusion | flops 32768 | bytes 131328 | tf_op jit(solution)/shard_map/stack | solution.py:73
  1.0 1.1 %convolution_convert_fusion.1 = bf16[128,4,256]{2,0,1:T(8,128)(2,1)S(1)} fusion(bf16[1,256,128]{2,1,0:T(8,128)(2,1)} %bitcast.47, bf16[1,256,128]{2,1,0:T(8,128)(2,1)S(1)} %select_bitcast_fusion, bf16[1,256,128]{2,1,0:T(8,128)(2,1)} %bitcast.48, bf16[1,256,128]{2,1,0:T(8,128)(2,1)} %bitcast.49), kind=kOutput, calls=%fused_computation.2 | convolution fusion | flops 34750464 | bytes 524288 | tf_op jit(solution)/shard_map/ck,atk->cat/dot_general | solution.py:76
  2.2 0.2 copy.19
  2.4 0.8 %reshape.78 = bf16[64,16,128]{2,1,0:T(8,128)(2,1)} reshape(bf16[128,4,256]{2,1,0:T(4,128)(2,1)S(1)} %copy.19) | data formatting | bytes 524288 | tf_op jit(solution)/shard_map/reshape | solution.py:79
  3.2 12.9 %all-to-all-start = ((bf16[64,16,128]{2,1,0:T(8,128)(2,1)}), bf16[64,16,128]{2,1,0:T(8,128)(2,1)S(1)}, u32[]{:S(2)}, u32[]{:S(2)}) async-start(bf16[64,16,128]{2,1,0:T(8,128)(2,1)} %reshape.78), calls=%async_computation | async-start | bytes 524288 | tf_op jit(solution)/shard_map/all_to_all | solution.py:80
  16.1 0.7 %dynamic_slice.3 = f32[2]{0:T(128)S(1)} dynamic-slice(f32[128]{0:T(128)} %param.17, s32[]{:T(128)S(6)} %select_n.8), dynamic_slice_sizes={2} | dynamic-slice | bytes 20 | tf_op jit(solution)/shard_map/dynamic_slice | solution.py:105
  16.8 0.8 %broadcast_add_fusion = f32[264,128]{1,0:T(8,128)S(1)} fusion(f32[128]{0:T(128)} %constant.46, f32[264]{0:T(512)} %constant.45), kind=kLoop, calls=%fused_computation.32 | loop fusion | flops 33792 | bytes 136736 | tf_op jit(solution)/shard_map/add | solution.py:68
  17.6 9.6 %all-to-all-done = bf16[64,16,128]{2,1,0:T(8,128)(2,1)S(1)} async-done(((bf16[64,16,128]{2,1,0:T(8,128)(2,1)}), bf16[64,16,128]{2,1,0:T(8,128)(2,1)S(1)}, u32[]{:S(2)}, u32[]{:S(2)}) %all-to-all-start) | async-done | bytes 262176 | tf_op jit(solution)/shard_map/all_to_all | solution.py:80
  27.2 0.2 reshape.79
  27.5 0.3 fusion
  27.9 1.5 %fusion.25 = f32[6,528,256]{2,1,0:T(8,128)S(1)} fusion(bf16[6,528,64]{1,2,0:T(8,128)(2,1)S(1)} %fusion, f32[64,256,1]{1,0,2:T(8,128)S(1)} %copy-done.3), kind=kOutput, calls=%fused_computation.46 | convolution fusion | flops 622854144 | bytes 3715072 | tf_op jit(solution)/shard_map/qfb,bk->qfk/dot_general | solution.py:86
  29.4 0.2 slice_add_fusion
  29.6 0.5 copy-done.5
  30.0 0.2 multiply_subtract_fusion
  30.2 0.1 multiply_add_fusion
  30.3 0.6 fusion.3
  30.9 0.1 fusion.24
  31.0 0.7 fusion.2
  31.7 0.1 copy.22
  31.8 0.1 reshape.81
  32.0 15.8 %all_to_all.10 = f32[64,4,128]{2,1,0:T(4,128)S(1)} all-to-all(f32[64,4,128]{2,1,0:T(4,128)S(1)} %reshape.81), channel_id=1, replica_groups=mesh['seq'=64,'ch'=8] {'seq'}, dimensions={0} | all-to-all | bytes 262144 | tf_op jit(solution)/shard_map/all_to_all | solution.py:110
  47.7 0.1 reshape.82
  47.8 19.4 %all-gather.1 = f32[8,1,256]{2,1,0:T(1,128)S(1)} all-gather(f32[1,1,256]{2,1,0:T(1,128)S(1)} %bitcast.46), channel_id=2, replica_groups=mesh['seq'=64,'ch'=8] {'ch'}, dimensions={0}, use_global_device_ids=true | all-gather | bytes 9216 | tf_op jit(solution)/shard_map/all_gather | solution.py:114
  67.3 0.9 %convolution_convert_fusion.2 = bf16[256,128]{1,0:T(8,128)(2,1)} fusion(f32[128,256]{1,0:T(8,128)S(1)} %reshape.82, f32[256]{0:T(256)S(1)} %add_rsqrt_fusion, f32[128]{0:T(128)S(1)} %copy-done.4), kind=kOutput, calls=%fused_computation.6 | convolution fusion | flops 16973824 | bytes 198144 | tf_op jit(solution)/shard_map/tk,ck->tc/dot_general | solution.py:118
  (17 shorter events, 0.2 us)
Async XLA Ops:
  0.0 27.5 %copy-start.1 = (bf16[528,256,1]{1,0,2:T(8,128)(2,1)S(1)}, bf16[528,256,1]{1,0,2:T(8,128)(2,1)}, u32[]{:S(2)}) copy-start(bf16[528,256,1]{1,0,2:T(8,128)(2,1)} %constant.48) | copy-start | bytes 811012
  0.0 27.9 %copy-start.3 = (f32[64,256,1]{1,0,2:T(8,128)S(1)}, f32[64,256,1]{1,0,2:T(8,128)}, u32[]{:S(2)}) copy-start(f32[64,256,1]{1,0,2:T(8,128)} %constant.49) | copy-start | bytes 196612
  3.2 24.1 %all-to-all-start = ((bf16[64,16,128]{2,1,0:T(8,128)(2,1)}), bf16[64,16,128]{2,1,0:T(8,128)(2,1)S(1)}, u32[]{:S(2)}, u32[]{:S(2)}) async-start(bf16[64,16,128]{2,1,0:T(8,128)(2,1)} %reshape.78), calls=%async_computation | async-start | bytes 524288 | tf_op jit(solution)/shard_map/all_to_all | solution.py:80
  29.4 0.7 copy-start.5
  29.4 0.9 %copy-start.2 = (f32[256,128,1]{1,0,2:T(8,128)S(1)}, f32[256,128,1]{1,0,2:T(8,128)}, u32[]{:S(2)}) copy-start(f32[256,128,1]{1,0,2:T(8,128)} %constant.50) | copy-start | bytes 393220
  29.6 1.5 %copy-start = (f32[256,528,1]{0,1,2:T(8,128)S(1)}, f32[256,528,1]{0,1,2:T(8,128)}, u32[]{:S(2)}) copy-start(f32[256,528,1]{0,1,2:T(8,128)} %constant.51) | copy-start | bytes 1622020
  30.2 37.1 %copy-start.4 = (f32[128]{0:T(128)S(1)}, f32[128]{0:T(128)}, u32[]{:S(2)}) copy-start(f32[128]{0:T(128)} %param.18) | copy-start | bytes 1540

commit v16 on v15

--- a/solution.py
+++ b/solution.py
@@ -68,9 +68,7 @@
     sh_re = jnp.asarray(sign_np, f32) + jnp.asarray(cos_np, f32)
     sh_im = jnp.asarray(msin_np, f32)
 
-    row_ids = lax.broadcasted_iota(jnp.int32, (rows_dev, 1), 0) + own_index * rows_dev
-    anti_masked = jnp.where(row_ids > 0, anti_filter, jnp.zeros_like(anti_filter))
-    stacked = jnp.stack([inputs, causal_filter, anti_masked, gate_values])
+    stacked = jnp.stack([inputs, causal_filter, anti_filter, gate_values])
     lanes = 128
     eye_ch = jnp.eye(chan_dev, dtype=jnp.bfloat16)
     by_channel = jnp.einsum(
@@ -82,6 +80,12 @@
     conv_in = series[:, :3].reshape(blocks, 3 * per, rows_dev).transpose(1, 0, 2)
 
     spec = jnp.einsum("fn,qbn->qfb", fwd, conv_in, preferred_element_type=f32)
+    first_anti = series[0, 2, :, 0].astype(f32)
+    q_ids = lax.broadcasted_iota(jnp.int32, (3 * per, 1, 1), 0)
+    row0 = jnp.where(q_ids >= 2 * per, jnp.tile(first_anti, 3)[:, None, None], f32(0.0))
+    col0 = fwd[:, 0].astype(f32)[None, :, None]
+    at_first = (lax.broadcasted_iota(jnp.int32, (1, 1, blocks), 2) == 0).astype(f32)
+    spec = spec - row0 * col0 * at_first
     spec = spec.astype(jnp.bfloat16).astype(f32)
     z = jnp.einsum("qfb,bk->qfk", spec, ofwd, precision=HIGHEST, preferred_element_type=f32)
     z_re, z_im = z[:, :fp], z[:, fp:]

time: 68.5 us -> 67.8 us (0.990)
  other arithmetic: 2.27 us -> 1.46 us
    another operation x1 -> x0, other arithmetic: 0.99 us -> none  [on_device(): stacked = jnp.stack([inputs, causal_filter, anti_masked, gate_values])]
where the time goes in v16:
time: 67.8 us; the launch traced here: 67.5 us
  blocking collectives  35.1 us (52%)
  starting transfers between devices  12.9 us (19%)
  waiting for transfers between devices  9.6 us (14%)
  matrix products  5.22 us (8%)
  local copies, waits for them, and re-layouts  2.97 us (4%)
  other arithmetic  1.46 us (2%)
    all_gather x1, blocking collectives, on_device(): lax.all_gather(partial, 'ch', axis=0, tiled=False)  19.4 us
    all_to_all x1, blocking collectives, on_device(): got = lax.all_to_all(back, 'seq', 0, 0, tiled=True)  15.8 us
    all_to_all x1, starting transfers between devices, on_device(): recv = lax.all_to_all(send, 'seq', 0, 0, tiled=True)  12.9 us
    all_to_all x1, waiting for transfers between devices, on_device(): recv = lax.all_to_all(send, 'seq', 0, 0, tiled=True)  9.6 us
    dot_general x1, matrix products, on_device(): jnp.einsum('qfb,bk->qfk', spec, ofwd, precision=HIGHEST, preferred_elemen...  1.49 us
  transfers between devices with their start and end apart: 1, of which 1 were waited for; matrix products, arithmetic and copies ran while one was open for 2% of the time, Pallas kernels for 0%

profile of v16, /device:TPU:1, one launch (start us, length us, event | category | flops | bytes accessed | tf_op | source)
XLA Modules:
  0.0 67.5 jit_solution(7817211713506502518)
XLA Ops:
  0.0 1.2 %convolution_convert_fusion = bf16[128,4,256]{2,0,1:T(8,128)(2,1)S(1)} fusion(bf16[1,256,128]{2,1,0:T(8,128)(2,1)} %bitcast.51, bf16[1,256,128]{2,1,0:T(8,128)(2,1)} %bitcast.52, bf16[1,256,128]{2,1,0:T(8,128)(2,1)} %bitcast.53, bf16[1,256,128]{2,1,0:T(8,128)(2,1)} %bitcast.54), kind=kOutput, calls=%fused_computation.3 | convolution fusion | flops 34750464 | bytes 524288 | tf_op jit(solution)/shard_map/ck,atk->cat/dot_general | solution.py:74
  1.2 0.2 copy.19
  1.4 0.8 %reshape.136 = bf16[64,16,128]{2,1,0:T(8,128)(2,1)} reshape(bf16[128,4,256]{2,1,0:T(4,128)(2,1)S(1)} %copy.19) | data formatting | bytes 524288 | tf_op jit(solution)/shard_map/reshape | solution.py:77
  2.2 12.9 %all-to-all-start = ((bf16[64,16,128]{2,1,0:T(8,128)(2,1)}), bf16[64,16,128]{2,1,0:T(8,128)(2,1)S(1)}, u32[]{:S(2)}, u32[]{:S(2)}) async-start(bf16[64,16,128]{2,1,0:T(8,128)(2,1)} %reshape.136), calls=%async_computation | async-start | bytes 524288 | tf_op jit(solution)/shard_map/all_to_all | solution.py:78
  15.2 0.7 %dynamic_slice.3 = f32[2]{0:T(128)S(1)} dynamic-slice(f32[128]{0:T(128)} %param.17, s32[]{:T(128)S(6)} %select_n.13), dynamic_slice_sizes={2} | dynamic-slice | bytes 20 | tf_op jit(solution)/shard_map/dynamic_slice | solution.py:109
  15.9 0.8 %broadcast_add_fusion = f32[264,128]{1,0:T(8,128)S(1)} fusion(f32[128]{0:T(128)} %constant.44, f32[264]{0:T(512)} %constant.43), kind=kLoop, calls=%fused_computation.33 | loop fusion | flops 33792 | bytes 136736 | tf_op jit(solution)/shard_map/add | solution.py:68
  16.7 9.6 %all-to-all-done = bf16[64,16,128]{2,1,0:T(8,128)(2,1)S(1)} async-done(((bf16[64,16,128]{2,1,0:T(8,128)(2,1)}), bf16[64,16,128]{2,1,0:T(8,128)(2,1)S(1)}, u32[]{:S(2)}, u32[]{:S(2)}) %all-to-all-start) | async-done | bytes 262176 | tf_op jit(solution)/shard_map/all_to_all | solution.py:78
  26.3 0.2 reshape.137
  26.6 0.1 fusion.22
  26.7 0.1 broadcast_in_dim_tile.3
  26.9 0.3 fusion.1
  27.2 1.5 %fusion.27 = f32[6,528,256]{2,1,0:T(8,128)S(1)} fusion(bf16[6,528,64]{1,2,0:T(8,128)(2,1)S(1)} %fusion.1, f32[64,256,1]{1,0,2:T(8,128)S(1)} %copy-done.2), kind=kOutput, calls=%fused_computation.50 | convolution fusion | flops 622854144 | bytes 3715072 | tf_op jit(solution)/shard_map/qfb,bk->qfk/dot_general | solution.py:90
  28.7 0.2 slice_add_fusion
  28.9 0.5 copy-done.5
  29.4 0.2 multiply_subtract_fusion
  29.6 0.1 multiply_add_fusion
  29.7 0.6 fusion.4
  30.3 0.1 fusion.26
  30.4 0.7 %fusion.3 = f32[64,2,256]{2,0,1:T(8,128)S(1)} fusion(f32[256,528,1]{0,1,2:T(8,128)S(1)} %copy-done, f32[2,264,64]{2,1,0:T(8,128)S(1)} %get-tuple-element.11, f32[2,264,64]{2,1,0:T(8,128)S(1)} %get-tuple-element.10, bf16[64,4,2,256]{3,0,2,1:T(8,128)(2,1)S(1)} %bitcast.48, f32[2]{0:T(128)S(1)} %dynamic_slice.3), kind=kOutput, calls=%fused_computation.6 | convolution fusion | flops 104040448 | bytes 1073160 | tf_op jit(solution)/shard_map/cfi,tf->ict/dot_general | solution.py:107
  31.1 0.1 copy.22
  31.2 0.1 reshape.139
  31.3 15.8 %all_to_all.10 = f32[64,4,128]{2,1,0:T(4,128)S(1)} all-to-all(f32[64,4,128]{2,1,0:T(4,128)S(1)} %reshape.139), channel_id=1, replica_groups=mesh['seq'=64,'ch'=8] {'seq'}, dimensions={0} | all-to-all | bytes 262144 | tf_op jit(solution)/shard_map/all_to_all | solution.py:114
  47.2 19.4 %all-gather.1 = f32[8,1,256]{2,1,0:T(1,128)S(1)} all-gather(f32[1,1,256]{2,1,0:T(1,128)S(1)} %bitcast.50), channel_id=2, replica_groups=mesh['seq'=64,'ch'=8] {'ch'}, dimensions={0}, use_global_device_ids=true | all-gather | bytes 9216 | tf_op jit(solution)/shard_map/all_gather | solution.py:118
  66.6 0.9 %convolution_convert_fusion.1 = bf16[256,128]{1,0:T(8,128)(2,1)} fusion(f32[128,256]{1,0:T(8,128)S(1)} %reshape.140, f32[256]{0:T(256)S(1)} %add_rsqrt_fusion, f32[128]{0:T(128)S(1)} %copy-done.4), kind=kOutput, calls=%fused_computation.7 | convolution fusion | flops 16973824 | bytes 198144 | tf_op jit(solution)/shard_map/tk,ck->tc/dot_general | solution.py:122
  (23 shorter events, 0.3 us)
Async XLA Ops:
  0.0 26.8 %copy-start.3 = (f32[528]{0:T(1024)S(1)}, f32[528]{0:T(1024)}, u32[]{:S(2)}) copy-start(f32[528]{0:T(1024)} %constant.47) | copy-start | bytes 6340
  0.0 26.8 %copy-start.6 = (bf16[528,256,1]{1,0,2:T(8,128)(2,1)S(1)}, bf16[528,256,1]{1,0,2:T(8,128)(2,1)}, u32[]{:S(2)}) copy-start(bf16[528,256,1]{1,0,2:T(8,128)(2,1)} %constant.49) | copy-start | bytes 811012
  0.0 27.2 %copy-start.2 = (f32[64,256,1]{1,0,2:T(8,128)S(1)}, f32[64,256,1]{1,0,2:T(8,128)}, u32[]{:S(2)}) copy-start(f32[64,256,1]{1,0,2:T(8,128)} %constant.50) | copy-start | bytes 196612
  2.2 24.1 %all-to-all-start = ((bf16[64,16,128]{2,1,0:T(8,128)(2,1)}), bf16[64,16,128]{2,1,0:T(8,128)(2,1)S(1)}, u32[]{:S(2)}, u32[]{:S(2)}) async-start(bf16[64,16,128]{2,1,0:T(8,128)(2,1)} %reshape.136), calls=%async_computation | async-start | bytes 524288 | tf_op jit(solution)/shard_map/all_to_all | solution.py:78
  28.7 0.7 copy-start.5
  28.7 0.9 %copy-start.1 = (f32[256,128,1]{1,0,2:T(8,128)S(1)}, f32[256,128,1]{1,0,2:T(8,128)}, u32[]{:S(2)}) copy-start(f32[256,128,1]{1,0,2:T(8,128)} %constant.51) | copy-start | bytes 393220
  28.9 1.5 %copy-start = (f32[256,528,1]{0,1,2:T(8,128)S(1)}, f32[256,528,1]{0,1,2:T(8,128)}, u32[]{:S(2)}) copy-start(f32[256,528,1]{0,1,2:T(8,128)} %constant.52) | copy-start | bytes 1622020
  29.5 37.1 %copy-start.4 = (f32[128]{0:T(128)S(1)}, f32[128]{0:T(128)}, u32[]{:S(2)}) copy-start(f32[128]{0:T(128)} %param.18) | copy-start | bytes 1540

commit v17 on v13

--- a/solution.py
+++ b/solution.py
@@ -65,8 +65,9 @@
     inv = jnp.asarray(inv_np, f32)
     ofwd = jnp.asarray(ofwd_np, f32)
     oinv = jnp.asarray(np.concatenate([oinv_re_np, oinv_im_np], axis=1), f32)
-    sh_re = jnp.asarray(sign_np, f32) + jnp.asarray(cos_np, f32)
-    sh_im = jnp.asarray(msin_np, f32)
+    parity = lax.broadcasted_iota(jnp.int32, (fp, 1), 0) % 2
+    sh_re = (1 - 2 * parity).astype(f32) + ofwd[1:2, :size]
+    sh_im = -ofwd[1:2, size:]
 
     stacked = jnp.stack([inputs, causal_filter, anti_filter, gate_values])
     lanes = 128

time: 67.5 us -> 67.5 us (level)
  no operation moved by 1% of the time
where the time goes in v17:
time: 67.5 us; the launch traced here: 67.3 us
  blocking collectives  35.1 us (52%)
  starting transfers between devices  12.9 us (19%)
  waiting for transfers between devices  9.53 us (14%)
  matrix products  5.21 us (8%)
  local copies, waits for them, and re-layouts  2.88 us (4%)
  other arithmetic  1.37 us (2%)
    all_gather x1, blocking collectives, on_device(): lax.all_gather(partial, 'ch', axis=0, tiled=False)  19.4 us
    all_to_all x1, blocking collectives, on_device(): got = lax.all_to_all(back, 'seq', 0, 0, tiled=True)  15.8 us
    all_to_all x1, starting transfers between devices, on_device(): recv = lax.all_to_all(send, 'seq', 0, 0, tiled=True)  12.9 us
    all_to_all x1, waiting for transfers between devices, on_device(): recv = lax.all_to_all(send, 'seq', 0, 0, tiled=True)  9.53 us
    dot_general x1, matrix products, on_device(): jnp.einsum('qfb,bk->qfk', spec, ofwd, precision=HIGHEST, preferred_elemen...  1.49 us
  transfers between devices with their start and end apart: 1, of which 1 were waited for; matrix products, arithmetic and copies ran while one was open for 2% of the time, Pallas kernels for 0%

profile of v17, /device:TPU:1, one launch (start us, length us, event | category | flops | bytes accessed | tf_op | source)
XLA Modules:
  0.0 67.3 jit_solution(5884347019923452906)
XLA Ops:
  0.0 1.2 %convolution_convert_fusion.1 = bf16[128,4,256]{2,0,1:T(8,128)(2,1)S(1)} fusion(bf16[1,256,128]{2,1,0:T(8,128)(2,1)} %bitcast.47, bf16[1,256,128]{2,1,0:T(8,128)(2,1)} %bitcast.48, bf16[1,256,128]{2,1,0:T(8,128)(2,1)} %bitcast.49, bf16[1,256,128]{2,1,0:T(8,128)(2,1)} %bitcast.50), kind=kOutput, calls=%fused_computation.2 | convolution fusion | flops 34750464 | bytes 524288 | tf_op jit(solution)/shard_map/ck,atk->cat/dot_general | solution.py:75
  1.2 0.2 copy.16
  1.4 0.8 %reshape.111 = bf16[64,16,128]{2,1,0:T(8,128)(2,1)} reshape(bf16[128,4,256]{2,1,0:T(4,128)(2,1)S(1)} %copy.16) | data formatting | bytes 524288 | tf_op jit(solution)/shard_map/reshape | solution.py:78
  2.2 12.9 %all-to-all-start = ((bf16[64,16,128]{2,1,0:T(8,128)(2,1)}), bf16[64,16,128]{2,1,0:T(8,128)(2,1)S(1)}, u32[]{:S(2)}, u32[]{:S(2)}) async-start(bf16[64,16,128]{2,1,0:T(8,128)(2,1)} %reshape.111), calls=%async_computation | async-start | bytes 524288 | tf_op jit(solution)/shard_map/all_to_all | solution.py:79
  15.2 0.7 %dynamic_slice.3 = f32[2]{0:T(128)S(1)} dynamic-slice(f32[128]{0:T(128)} %param.14, s32[]{:T(128)S(6)} %select_n.22), dynamic_slice_sizes={2} | dynamic-slice | bytes 20 | tf_op jit(solution)/shard_map/dynamic_slice | solution.py:109
  15.9 0.1 broadcast_and_fusion
  16.0 0.8 %broadcast_add_fusion = f32[264,128]{1,0:T(8,128)S(1)} fusion(f32[128]{0:T(128)} %constant.50, f32[264]{0:T(512)S(1)} %fusion.23), kind=kLoop, calls=%fused_computation.33 | loop fusion | flops 33792 | bytes 136736 | tf_op jit(solution)/shard_map/add | solution.py:69
  16.8 9.5 %all-to-all-done = bf16[64,16,128]{2,1,0:T(8,128)(2,1)S(1)} async-done(((bf16[64,16,128]{2,1,0:T(8,128)(2,1)}), bf16[64,16,128]{2,1,0:T(8,128)(2,1)S(1)}, u32[]{:S(2)}, u32[]{:S(2)}) %all-to-all-start) | async-done | bytes 262176 | tf_op jit(solution)/shard_map/all_to_all | solution.py:79
  26.3 0.2 reshape.112
  26.6 0.3 fusion
  27.0 1.5 %fusion.31 = f32[6,528,256]{2,1,0:T(8,128)S(1)} fusion(bf16[6,528,64]{1,2,0:T(8,128)(2,1)S(1)} %fusion, f32[64,256,1]{1,0,2:T(8,128)S(1)} %copy-done.3), kind=kOutput, calls=%fused_computation.57 | convolution fusion | flops 622854144 | bytes 3715072 | tf_op jit(solution)/shard_map/qfb,bk->qfk/dot_general | solution.py:90
  28.5 0.2 slice_add_fusion
  28.7 0.5 copy-done.5
  29.1 0.2 multiply_subtract_fusion
  29.3 0.1 multiply_add_fusion
  29.4 0.6 fusion.3
  30.0 0.1 fusion.30
  30.2 0.7 %fusion.2 = f32[64,2,256]{2,0,1:T(8,128)S(1)} fusion(f32[256,528,1]{0,1,2:T(8,128)S(1)} %copy-done, f32[2,264,64]{2,1,0:T(8,128)S(1)} %get-tuple-element.11, f32[2,264,64]{2,1,0:T(8,128)S(1)} %get-tuple-element.10, bf16[64,4,2,256]{3,0,2,1:T(8,128)(2,1)S(1)} %bitcast.44, f32[2]{0:T(128)S(1)} %dynamic_slice.3), kind=kOutput, calls=%fused_computation.5 | convolution fusion | flops 104040448 | bytes 1073160 | tf_op jit(solution)/shard_map/cfi,tf->ict/dot_general | solution.py:107
  30.8 0.1 copy.19
  31.0 0.1 reshape.114
  31.1 15.8 %all_to_all.10 = f32[64,4,128]{2,1,0:T(4,128)S(1)} all-to-all(f32[64,4,128]{2,1,0:T(4,128)S(1)} %reshape.114), channel_id=1, replica_groups=mesh['seq'=64,'ch'=8] {'seq'}, dimensions={0} | all-to-all | bytes 262144 | tf_op jit(solution)/shard_map/all_to_all | solution.py:114
  46.9 0.1 reshape.115
  47.0 19.4 %all-gather.1 = f32[8,1,256]{2,1,0:T(1,128)S(1)} all-gather(f32[1,1,256]{2,1,0:T(1,128)S(1)} %bitcast.46), channel_id=2, replica_groups=mesh['seq'=64,'ch'=8] {'ch'}, dimensions={0}, use_global_device_ids=true | all-gather | bytes 9216 | tf_op jit(solution)/shard_map/all_gather | solution.py:118
  66.4 0.9 %convolution_convert_fusion.2 = bf16[256,128]{1,0:T(8,128)(2,1)} fusion(f32[128,256]{1,0:T(8,128)S(1)} %reshape.115, f32[256]{0:T(256)S(1)} %add_rsqrt_fusion, f32[128]{0:T(128)S(1)} %copy-done.4), kind=kOutput, calls=%fused_computation.6 | convolution fusion | flops 16973824 | bytes 198144 | tf_op jit(solution)/shard_map/tk,ck->tc/dot_general | solution.py:122
  (21 shorter events, 0.2 us)
Async XLA Ops:
  0.0 26.6 %copy-start.1 = (bf16[528,256,1]{1,0,2:T(8,128)(2,1)S(1)}, bf16[528,256,1]{1,0,2:T(8,128)(2,1)}, u32[]{:S(2)}) copy-start(bf16[528,256,1]{1,0,2:T(8,128)(2,1)} %constant.54) | copy-start | bytes 811012
  0.0 27.0 %copy-start.3 = (f32[64,256,1]{1,0,2:T(8,128)S(1)}, f32[64,256,1]{1,0,2:T(8,128)}, u32[]{:S(2)}) copy-start(f32[64,256,1]{1,0,2:T(8,128)} %constant.55) | copy-start | bytes 196612
  2.2 24.1 %all-to-all-start = ((bf16[64,16,128]{2,1,0:T(8,128)(2,1)}), bf16[64,16,128]{2,1,0:T(8,128)(2,1)S(1)}, u32[]{:S(2)}, u32[]{:S(2)}) async-start(bf16[64,16,128]{2,1,0:T(8,128)(2,1)} %reshape.111), calls=%async_computation | async-start | bytes 524288 | tf_op jit(solution)/shard_map/all_to_all | solution.py:79
  28.5 0.7 copy-start.5
  28.5 0.9 %copy-start.2 = (f32[256,128,1]{1,0,2:T(8,128)S(1)}, f32[256,128,1]{1,0,2:T(8,128)}, u32[]{:S(2)}) copy-start(f32[256,128,1]{1,0,2:T(8,128)} %constant.56) | copy-start | bytes 393220
  28.7 1.5 %copy-start = (f32[256,528,1]{0,1,2:T(8,128)S(1)}, f32[256,528,1]{0,1,2:T(8,128)}, u32[]{:S(2)}) copy-start(f32[256,528,1]{0,1,2:T(8,128)} %constant.57) | copy-start | bytes 1622020
  29.3 37.1 %copy-start.4 = (f32[128]{0:T(128)S(1)}, f32[128]{0:T(128)}, u32[]{:S(2)}) copy-start(f32[128]{0:T(128)} %param.15) | copy-start | bytes 1540

commit v18 on v17

--- a/solution.py
+++ b/solution.py
@@ -66,8 +66,9 @@
     ofwd = jnp.asarray(ofwd_np, f32)
     oinv = jnp.asarray(np.concatenate([oinv_re_np, oinv_im_np], axis=1), f32)
     parity = lax.broadcasted_iota(jnp.int32, (fp, 1), 0) % 2
-    sh_re = (1 - 2 * parity).astype(f32) + ofwd[1:2, :size]
-    sh_im = -ofwd[1:2, size:]
+    zero = f32(0.0) * own_index.astype(f32)
+    sh_re = (1 - 2 * parity).astype(f32) + (ofwd[1:2, :size] + zero)
+    sh_im = -(ofwd[1:2, size:] + zero)
 
     stacked = jnp.stack([inputs, causal_filter, anti_filter, gate_values])
     lanes = 128

time: 67.5 us -> 67.5 us (level)
    mul x0 -> x1, other arithmetic: none -> 0.68 us  [on_device(): c_re = sh_re * x_re[1] - sh_im * x_im[1]]
where the time goes in v18:
time: 67.5 us; the launch traced here: 67.2 us
  blocking collectives  35.1 us (52%)
  starting transfers between devices  12.9 us (19%)
  waiting for transfers between devices  9.5 us (14%)
  matrix products  5.22 us (8%)
  local copies, waits for them, and re-layouts  2.86 us (4%)
  other arithmetic  1.39 us (2%)
    all_gather x1, blocking collectives, on_device(): lax.all_gather(partial, 'ch', axis=0, tiled=False)  19.4 us
    all_to_all x1, blocking collectives, on_device(): got = lax.all_to_all(back, 'seq', 0, 0, tiled=True)  15.8 us
    all_to_all x1, starting transfers between devices, on_device(): recv = lax.all_to_all(send, 'seq', 0, 0, tiled=True)  12.9 us
    all_to_all x1, waiting for transfers between devices, on_device(): recv = lax.all_to_all(send, 'seq', 0, 0, tiled=True)  9.5 us
    dot_general x1, matrix products, on_device(): jnp.einsum('qfb,bk->qfk', spec, ofwd, precision=HIGHEST, preferred_elemen...  1.49 us
  transfers between devices with their start and end apart: 1, of which 1 were waited for; matrix products, arithmetic and copies ran while one was open for 2% of the time, Pallas kernels for 0%

profile of v18, /device:TPU:1, one launch (start us, length us, event | category | flops | bytes accessed | tf_op | source)
XLA Modules:
  0.0 67.2 jit_solution(8483448804428508728)
XLA Ops:
  0.0 1.2 %convolution_convert_fusion.1 = bf16[128,4,256]{2,0,1:T(8,128)(2,1)S(1)} fusion(bf16[1,256,128]{2,1,0:T(8,128)(2,1)} %bitcast.51, bf16[1,256,128]{2,1,0:T(8,128)(2,1)} %bitcast.52, bf16[1,256,128]{2,1,0:T(8,128)(2,1)} %bitcast.53, bf16[1,256,128]{2,1,0:T(8,128)(2,1)} %bitcast.54), kind=kOutput, calls=%fused_computation.2 | convolution fusion | flops 34750464 | bytes 524288 | tf_op jit(solution)/shard_map/ck,atk->cat/dot_general | solution.py:76
  1.2 0.2 copy.16
  1.4 0.8 %reshape.111 = bf16[64,16,128]{2,1,0:T(8,128)(2,1)} reshape(bf16[128,4,256]{2,1,0:T(4,128)(2,1)S(1)} %copy.16) | data formatting | bytes 524288 | tf_op jit(solution)/shard_map/reshape | solution.py:79
  2.2 12.9 %all-to-all-start = ((bf16[64,16,128]{2,1,0:T(8,128)(2,1)}), bf16[64,16,128]{2,1,0:T(8,128)(2,1)S(1)}, u32[]{:S(2)}, u32[]{:S(2)}) async-start(bf16[64,16,128]{2,1,0:T(8,128)(2,1)} %reshape.111), calls=%async_computation | async-start | bytes 524288 | tf_op jit(solution)/shard_map/all_to_all | solution.py:80
  15.2 0.7 %dynamic_slice.3 = f32[2]{0:T(128)S(1)} dynamic-slice(f32[128]{0:T(128)} %param.14, s32[]{:T(128)S(6)} %select_n.22), dynamic_slice_sizes={2} | dynamic-slice | bytes 20 | tf_op jit(solution)/shard_map/dynamic_slice | solution.py:110
  15.9 0.7 %fusion.27 = (f32[128]{0:T(128)S(1)}, f32[128]{0:T(128)S(1)}) fusion(f32[1,128]{1,0:T(1,128)} %constant.50, f32[]{:T(128)S(6)} %mul.113, f32[1,128]{1,0:T(1,128)} %constant.49), kind=kLoop, calls=%fused_computation.53 | loop fusion | flops 384 | bytes 2052 | tf_op jit(solution)/shard_map/mul | solution.py:96
  16.6 0.1 broadcast_and_fusion
  16.7 0.1 broadcast_add_fusion
  16.8 9.5 %all-to-all-done = bf16[64,16,128]{2,1,0:T(8,128)(2,1)S(1)} async-done(((bf16[64,16,128]{2,1,0:T(8,128)(2,1)}), bf16[64,16,128]{2,1,0:T(8,128)(2,1)S(1)}, u32[]{:S(2)}, u32[]{:S(2)}) %all-to-all-start) | async-done | bytes 262176 | tf_op jit(solution)/shard_map/all_to_all | solution.py:80
  26.3 0.2 reshape.112
  26.6 0.3 fusion
  27.0 1.5 %fusion.32 = f32[6,528,256]{2,1,0:T(8,128)S(1)} fusion(bf16[6,528,64]{1,2,0:T(8,128)(2,1)S(1)} %fusion, f32[64,256,1]{1,0,2:T(8,128)S(1)} %copy-done.3), kind=kOutput, calls=%fused_computation.60 | convolution fusion | flops 622854144 | bytes 3715072 | tf_op jit(solution)/shard_map/qfb,bk->qfk/dot_general | solution.py:91
  28.5 0.2 slice_add_fusion
  28.7 0.2 multiply_subtract_fusion
  28.9 0.1 multiply_add_fusion
  28.9 0.4 copy-done.2
  29.4 0.6 fusion.3
  30.0 0.1 fusion.31
  30.1 0.7 %fusion.2 = f32[64,2,256]{2,0,1:T(8,128)S(1)} fusion(f32[256,528,1]{0,1,2:T(8,128)S(1)} %copy-done, f32[2,264,64]{2,1,0:T(8,128)S(1)} %get-tuple-element.11, f32[2,264,64]{2,1,0:T(8,128)S(1)} %get-tuple-element.10, bf16[64,4,2,256]{3,0,2,1:T(8,128)(2,1)S(1)} %bitcast.48, f32[2]{0:T(128)S(1)} %dynamic_slice.3), kind=kOutput, calls=%fused_computation.5 | convolution fusion | flops 104040448 | bytes 1073160 | tf_op jit(solution)/shard_map/cfi,tf->ict/dot_general | solution.py:108
  30.8 0.1 copy.19
  30.9 0.1 reshape.114
  31.1 15.8 %all_to_all.10 = f32[64,4,128]{2,1,0:T(4,128)S(1)} all-to-all(f32[64,4,128]{2,1,0:T(4,128)S(1)} %reshape.114), channel_id=1, replica_groups=mesh['seq'=64,'ch'=8] {'seq'}, dimensions={0} | all-to-all | bytes 262144 | tf_op jit(solution)/shard_map/all_to_all | solution.py:115
  46.9 19.4 %all-gather.1 = f32[8,1,256]{2,1,0:T(1,128)S(1)} all-gather(f32[1,1,256]{2,1,0:T(1,128)S(1)} %bitcast.50), channel_id=2, replica_groups=mesh['seq'=64,'ch'=8] {'ch'}, dimensions={0}, use_global_device_ids=true | all-gather | bytes 9216 | tf_op jit(solution)/shard_map/all_gather | solution.py:119
  66.4 0.9 %convolution_convert_fusion.2 = bf16[256,128]{1,0:T(8,128)(2,1)} fusion(f32[128,256]{1,0:T(8,128)S(1)} %reshape.115, f32[256]{0:T(256)S(1)} %add_rsqrt_fusion, f32[128]{0:T(128)S(1)} %copy-done.4), kind=kOutput, calls=%fused_computation.6 | convolution fusion | flops 16973824 | bytes 198144 | tf_op jit(solution)/shard_map/tk,ck->tc/dot_general | solution.py:123
  (20 shorter events, 0.3 us)
Async XLA Ops:
  0.0 26.6 %copy-start.1 = (bf16[528,256,1]{1,0,2:T(8,128)(2,1)S(1)}, bf16[528,256,1]{1,0,2:T(8,128)(2,1)}, u32[]{:S(2)}) copy-start(bf16[528,256,1]{1,0,2:T(8,128)(2,1)} %constant.51) | copy-start | bytes 811012
  0.0 27.0 %copy-start.3 = (f32[64,256,1]{1,0,2:T(8,128)S(1)}, f32[64,256,1]{1,0,2:T(8,128)}, u32[]{:S(2)}) copy-start(f32[64,256,1]{1,0,2:T(8,128)} %constant.52) | copy-start | bytes 196612
  2.2 24.1 %all-to-all-start = ((bf16[64,16,128]{2,1,0:T(8,128)(2,1)}), bf16[64,16,128]{2,1,0:T(8,128)(2,1)S(1)}, u32[]{:S(2)}, u32[]{:S(2)}) async-start(bf16[64,16,128]{2,1,0:T(8,128)(2,1)} %reshape.111), calls=%async_computation | async-start | bytes 524288 | tf_op jit(solution)/shard_map/all_to_all | solution.py:80
  28.5 0.9 %copy-start.2 = (f32[256,128,1]{1,0,2:T(8,128)S(1)}, f32[256,128,1]{1,0,2:T(8,128)}, u32[]{:S(2)}) copy-start(f32[256,128,1]{1,0,2:T(8,128)} %constant.53) | copy-start | bytes 393220
  28.7 1.5 %copy-start = (f32[256,528,1]{0,1,2:T(8,128)S(1)}, f32[256,528,1]{0,1,2:T(8,128)}, u32[]{:S(2)}) copy-start(f32[256,528,1]{0,1,2:T(8,128)} %constant.54) | copy-start | bytes 1622020
  28.9 37.5 %copy-start.4 = (f32[128]{0:T(128)S(1)}, f32[128]{0:T(128)}, u32[]{:S(2)}) copy-start(f32[128]{0:T(128)} %param.15) | copy-start | bytes 1540

commit v19 on v18

--- a/solution.py
+++ b/solution.py
@@ -64,7 +64,12 @@
     fwd = jnp.asarray(fwd_np, jnp.bfloat16)
     inv = jnp.asarray(inv_np, f32)
     ofwd = jnp.asarray(ofwd_np, f32)
-    oinv = jnp.asarray(np.concatenate([oinv_re_np, oinv_im_np], axis=1), f32)
+    zero_t = f32(0.0) * own_index.astype(f32)
+    cos_t = (ofwd[:, :size] + zero_t).T / f32(size)
+    sin_t = (ofwd[:, size:] + zero_t).T / f32(size)
+    oinv = jnp.concatenate(
+        [jnp.concatenate([cos_t, sin_t], axis=1), jnp.concatenate([-sin_t, cos_t], axis=1)], axis=0
+    )
     parity = lax.broadcasted_iota(jnp.int32, (fp, 1), 0) % 2
     zero = f32(0.0) * own_index.astype(f32)
     sh_re = (1 - 2 * parity).astype(f32) + (ofwd[1:2, :size] + zero)

time: 67.5 us -> 67.2 us (level)
  waiting for transfers between devices: 9.5 us -> 7.76 us
  other arithmetic: 1.39 us -> 3.13 us
    all_to_all x1, waiting for transfers between devices: 9.5 us -> 7.76 us  [on_device(): recv = lax.all_to_all(send, 'seq', 0, 0, tiled=True)]
    div x0 -> x1, other arithmetic: none -> 0.89 us  [on_device(): sin_t = (ofwd[:, size:] + zero_t).T / f32(size)]
    neg x0 -> x1, other arithmetic: none -> 0.85 us  [on_device(): -sin_t]
  transfers between devices with their start and end apart: 1 -> 1, of which waited for: 1 -> 1; matrix products, arithmetic and copies ran while one was open for 2% -> 5% of each run, Pallas kernels for 0% -> 0%
where the time goes in v19:
time: 67.2 us; the launch traced here: 66.9 us
  blocking collectives  35.1 us (52%)
  starting transfers between devices  12.9 us (19%)
  waiting for transfers between devices  7.76 us (12%)
  matrix products  5.28 us (8%)
  other arithmetic  3.13 us (5%)
  local copies, waits for them, and re-layouts  2.41 us (4%)
    all_gather x1, blocking collectives, on_device(): lax.all_gather(partial, 'ch', axis=0, tiled=False)  19.4 us
    all_to_all x1, blocking collectives, on_device(): got = lax.all_to_all(back, 'seq', 0, 0, tiled=True)  15.8 us
    all_to_all x1, starting transfers between devices, on_device(): recv = lax.all_to_all(send, 'seq', 0, 0, tiled=True)  12.9 us
    all_to_all x1, waiting for transfers between devices, on_device(): recv = lax.all_to_all(send, 'seq', 0, 0, tiled=True)  7.76 us
    dot_general x1, matrix products, on_device(): jnp.einsum('qfb,bk->qfk', spec, ofwd, precision=HIGHEST, preferred_elemen...  1.49 us
  transfers between devices with their start and end apart: 1, of which 1 were waited for; matrix products, arithmetic and copies ran while one was open for 5% of the time, Pallas kernels for 0%

profile of v19, /device:TPU:1, one launch (start us, length us, event | category | flops | bytes accessed | tf_op | source)
XLA Modules:
  0.0 66.9 jit_solution(7389838978552467631)
XLA Ops:
  0.0 1.2 %convolution_convert_fusion.1 = bf16[128,4,256]{2,0,1:T(8,128)(2,1)S(1)} fusion(bf16[1,256,128]{2,1,0:T(8,128)(2,1)} %bitcast.58, bf16[1,256,128]{2,1,0:T(8,128)(2,1)} %bitcast.59, bf16[1,256,128]{2,1,0:T(8,128)(2,1)} %bitcast.60, bf16[1,256,128]{2,1,0:T(8,128)(2,1)} %bitcast.61), kind=kOutput, calls=%fused_computation.2 | convolution fusion | flops 34750464 | bytes 524288 | tf_op jit(solution)/shard_map/ck,atk->cat/dot_general | solution.py:81
  1.2 0.2 copy.15
  1.4 0.8 %reshape.111 = bf16[64,16,128]{2,1,0:T(8,128)(2,1)} reshape(bf16[128,4,256]{2,1,0:T(4,128)(2,1)S(1)} %copy.15) | data formatting | bytes 524288 | tf_op jit(solution)/shard_map/reshape | solution.py:84
  2.2 12.9 %all-to-all-start = ((bf16[64,16,128]{2,1,0:T(8,128)(2,1)}), bf16[64,16,128]{2,1,0:T(8,128)(2,1)S(1)}, u32[]{:S(2)}, u32[]{:S(2)}) async-start(bf16[64,16,128]{2,1,0:T(8,128)(2,1)} %reshape.111), calls=%async_computation | async-start | bytes 524288 | tf_op jit(solution)/shard_map/all_to_all | solution.py:85
  15.3 0.9 %fusion.29 = f32[128,64]{1,0:T(8,128)S(1)} fusion(f32[64,128]{0,1:T(8,128)} %constant.53, f32[]{:T(128)S(6)} %mul.114), kind=kLoop, calls=%fused_computation.53 | loop fusion | flops 24576 | bytes 65540 | tf_op jit(solution)/shard_map/neg | solution.py:71
  16.1 0.7 %fusion.36 = (f32[128]{0:T(128)S(1)}, f32[128]{0:T(128)S(1)}) fusion(f32[1,128]{1,0:T(1,128)} %constant.51, f32[]{:T(128)S(6)} %mul.114, f32[1,128]{1,0:T(1,128)} %constant.50), kind=kLoop, calls=%fused_computation.65 | loop fusion | flops 384 | bytes 2052 | tf_op jit(solution)/shard_map/mul | solution.py:101
  16.8 0.7 %dynamic_slice.3 = f32[2]{0:T(128)S(1)} dynamic-slice(f32[128]{0:T(128)} %param.13, s32[]{:T(128)S(6)} %select_n.22), dynamic_slice_sizes={2} | dynamic-slice | bytes 20 | tf_op jit(solution)/shard_map/dynamic_slice | solution.py:115
  17.6 0.1 broadcast_add_fusion
  17.7 0.9 %fusion.23 = (f32[128,64]{1,0:T(8,128)S(1)}, f32[128,64]{1,0:T(8,128)S(1)}) fusion(f32[64,128]{0,1:T(8,128)} %constant.53, f32[]{:T(128)S(6)} %mul.114, f32[64,128]{0,1:T(8,128)} %constant.52), kind=kLoop, calls=%fused_computation.45 | loop fusion | flops 32768 | bytes 131076 | tf_op jit(solution)/shard_map/div | solution.py:69
  18.6 7.8 %all-to-all-done = bf16[64,16,128]{2,1,0:T(8,128)(2,1)S(1)} async-done(((bf16[64,16,128]{2,1,0:T(8,128)(2,1)}), bf16[64,16,128]{2,1,0:T(8,128)(2,1)S(1)}, u32[]{:S(2)}, u32[]{:S(2)}) %all-to-all-start) | async-done | bytes 262176 | tf_op jit(solution)/shard_map/all_to_all | solution.py:85
  26.3 0.2 reshape.112
  26.6 0.3 fusion
  27.0 1.5 %fusion.41 = f32[6,528,256]{2,1,0:T(8,128)S(1)} fusion(bf16[6,528,64]{1,2,0:T(8,128)(2,1)S(1)} %fusion, f32[64,256,1]{1,0,2:T(8,128)S(1)} %copy-done.2), kind=kOutput, calls=%fused_computation.72 | convolution fusion | flops 622854144 | bytes 3715072 | tf_op jit(solution)/shard_map/qfb,bk->qfk/dot_general | solution.py:96
  28.5 0.2 slice_add_fusion
  28.7 0.2 multiply_subtract_fusion
  28.9 0.1 multiply_add_fusion
  28.9 0.7 fusion.3
  29.6 0.1 fusion.40
  29.8 0.7 %fusion.2 = f32[64,2,256]{2,0,1:T(8,128)S(1)} fusion(f32[256,528,1]{0,1,2:T(8,128)S(1)} %copy-done, f32[2,264,64]{2,1,0:T(8,128)S(1)} %get-tuple-element.11, f32[2,264,64]{2,1,0:T(8,128)S(1)} %get-tuple-element.10, bf16[64,4,2,256]{3,0,2,1:T(8,128)(2,1)S(1)} %bitcast.55, f32[2]{0:T(128)S(1)} %dynamic_slice.3), kind=kOutput, calls=%fused_computation.5 | convolution fusion | flops 104040448 | bytes 1073160 | tf_op jit(solution)/shard_map/cfi,tf->ict/dot_general | solution.py:113
  30.4 0.1 copy.18
  30.5 0.1 reshape.114
  30.7 15.8 %all_to_all.10 = f32[64,4,128]{2,1,0:T(4,128)S(1)} all-to-all(f32[64,4,128]{2,1,0:T(4,128)S(1)} %reshape.114), channel_id=1, replica_groups=mesh['seq'=64,'ch'=8] {'seq'}, dimensions={0} | all-to-all | bytes 262144 | tf_op jit(solution)/shard_map/all_to_all | solution.py:120
  46.5 19.4 %all-gather.1 = f32[8,1,256]{2,1,0:T(1,128)S(1)} all-gather(f32[1,1,256]{2,1,0:T(1,128)S(1)} %bitcast.57), channel_id=2, replica_groups=mesh['seq'=64,'ch'=8] {'ch'}, dimensions={0}, use_global_device_ids=true | all-gather | bytes 9216 | tf_op jit(solution)/shard_map/all_gather | solution.py:124
  66.0 0.9 %convolution_convert_fusion.2 = bf16[256,128]{1,0:T(8,128)(2,1)} fusion(f32[128,256]{1,0:T(8,128)S(1)} %reshape.115, f32[256]{0:T(256)S(1)} %add_rsqrt_fusion, f32[128]{0:T(128)S(1)} %copy-done.3), kind=kOutput, calls=%fused_computation.6 | convolution fusion | flops 16973824 | bytes 198144 | tf_op jit(solution)/shard_map/tk,ck->tc/dot_general | solution.py:128
  (20 shorter events, 0.3 us)
Async XLA Ops:
  0.0 26.6 %copy-start.1 = (bf16[528,256,1]{1,0,2:T(8,128)(2,1)S(1)}, bf16[528,256,1]{1,0,2:T(8,128)(2,1)}, u32[]{:S(2)}) copy-start(bf16[528,256,1]{1,0,2:T(8,128)(2,1)} %constant.54) | copy-start | bytes 811012
  0.0 27.0 %copy-start.2 = (f32[64,256,1]{1,0,2:T(8,128)S(1)}, f32[64,256,1]{1,0,2:T(8,128)}, u32[]{:S(2)}) copy-start(f32[64,256,1]{1,0,2:T(8,128)} %constant.55) | copy-start | bytes 196612
  2.2 24.1 %all-to-all-start = ((bf16[64,16,128]{2,1,0:T(8,128)(2,1)}), bf16[64,16,128]{2,1,0:T(8,128)(2,1)S(1)}, u32[]{:S(2)}, u32[]{:S(2)}) async-start(bf16[64,16,128]{2,1,0:T(8,128)(2,1)} %reshape.111), calls=%async_computation | async-start | bytes 524288 | tf_op jit(solution)/shard_map/all_to_all | solution.py:85
  28.6 1.1 %copy-start = (f32[256,528,1]{0,1,2:T(8,128)S(1)}, f32[256,528,1]{0,1,2:T(8,128)}, u32[]{:S(2)}) copy-start(f32[256,528,1]{0,1,2:T(8,128)} %constant.56) | copy-start | bytes 1622020
  28.8 37.1 %copy-start.3 = (f32[128]{0:T(128)S(1)}, f32[128]{0:T(128)}, u32[]{:S(2)}) copy-start(f32[128]{0:T(128)} %param.14) | copy-start | bytes 1540

commit v20 on v19

--- a/solution.py
+++ b/solution.py
@@ -116,8 +116,7 @@
     mixed_local = series[:, 3].astype(f32) * (
         conv_t + skip_here[None, :, None] * series[:, 0].astype(f32)
     )
-    back = mixed_local.reshape(blocks, per * rows_dev // lanes, lanes)
-    got = lax.all_to_all(back, "seq", 0, 0, tiled=True)
+    got = lax.all_to_all(mixed_local, "seq", 0, 0, tiled=True)
     mix_t = got.reshape(blocks * per, rows_dev)
 
     partial = jnp.sum(mix_t * mix_t, axis=0)

time: 67.2 us -> 67.1 us (level)
  no operation moved by 1% of the time
where the time goes in v20:
time: 67.1 us; the launch traced here: 66.8 us
  blocking collectives  35.1 us (52%)
  starting transfers between devices  12.9 us (19%)
  waiting for transfers between devices  7.76 us (12%)
  matrix products  5.28 us (8%)
  other arithmetic  3.19 us (5%)
  local copies, waits for them, and re-layouts  2.31 us (3%)
    all_gather x1, blocking collectives, on_device(): lax.all_gather(partial, 'ch', axis=0, tiled=False)  19.4 us
    all_to_all x1, blocking collectives, on_device(): got = lax.all_to_all(mixed_local, 'seq', 0, 0, tiled=True)  15.8 us
    all_to_all x1, starting transfers between devices, on_device(): recv = lax.all_to_all(send, 'seq', 0, 0, tiled=True)  12.9 us
    all_to_all x1, waiting for transfers between devices, on_device(): recv = lax.all_to_all(send, 'seq', 0, 0, tiled=True)  7.76 us
    dot_general x1, matrix products, on_device(): jnp.einsum('qfb,bk->qfk', spec, ofwd, precision=HIGHEST, preferred_elemen...  1.49 us
  transfers between devices with their start and end apart: 1, of which 1 were waited for; matrix products, arithmetic and copies ran while one was open for 5% of the time, Pallas kernels for 0%

profile of v20, /device:TPU:1, one launch (start us, length us, event | category | flops | bytes accessed | tf_op | source)
XLA Modules:
  0.0 66.8 jit_solution(11005809721815231535)
XLA Ops:
  0.0 1.2 %convolution_convert_fusion.1 = bf16[128,4,256]{2,0,1:T(8,128)(2,1)S(1)} fusion(bf16[1,256,128]{2,1,0:T(8,128)(2,1)} %bitcast.58, bf16[1,256,128]{2,1,0:T(8,128)(2,1)} %bitcast.59, bf16[1,256,128]{2,1,0:T(8,128)(2,1)} %bitcast.60, bf16[1,256,128]{2,1,0:T(8,128)(2,1)} %bitcast.61), kind=kOutput, calls=%fused_computation.2 | convolution fusion | flops 34750464 | bytes 524288 | tf_op jit(solution)/shard_map/ck,atk->cat/dot_general | solution.py:81
  1.2 0.2 copy.15
  1.4 0.8 %reshape.108 = bf16[64,16,128]{2,1,0:T(8,128)(2,1)} reshape(bf16[128,4,256]{2,1,0:T(4,128)(2,1)S(1)} %copy.15) | data formatting | bytes 524288 | tf_op jit(solution)/shard_map/reshape | solution.py:84
  2.2 12.9 %all-to-all-start = ((bf16[64,16,128]{2,1,0:T(8,128)(2,1)}), bf16[64,16,128]{2,1,0:T(8,128)(2,1)S(1)}, u32[]{:S(2)}, u32[]{:S(2)}) async-start(bf16[64,16,128]{2,1,0:T(8,128)(2,1)} %reshape.108), calls=%async_computation | async-start | bytes 524288 | tf_op jit(solution)/shard_map/all_to_all | solution.py:85
  15.3 0.9 %fusion.29 = f32[128,64]{1,0:T(8,128)S(1)} fusion(f32[64,128]{0,1:T(8,128)} %constant.53, f32[]{:T(128)S(6)} %mul.115), kind=kLoop, calls=%fused_computation.53 | loop fusion | flops 24576 | bytes 65540 | tf_op jit(solution)/shard_map/neg | solution.py:71
  16.1 0.7 %fusion.36 = (f32[128]{0:T(128)S(1)}, f32[128]{0:T(128)S(1)}) fusion(f32[1,128]{1,0:T(1,128)} %constant.51, f32[]{:T(128)S(6)} %mul.115, f32[1,128]{1,0:T(1,128)} %constant.50), kind=kLoop, calls=%fused_computation.65 | loop fusion | flops 384 | bytes 2052 | tf_op jit(solution)/shard_map/mul | solution.py:101
  16.8 0.7 %dynamic_slice.3 = f32[2]{0:T(128)S(1)} dynamic-slice(f32[128]{0:T(128)} %param.13, s32[]{:T(128)S(6)} %select_n.22), dynamic_slice_sizes={2} | dynamic-slice | bytes 20 | tf_op jit(solution)/shard_map/dynamic_slice | solution.py:115
  17.6 0.1 broadcast_add_fusion
  17.7 0.9 %fusion.23 = (f32[128,64]{1,0:T(8,128)S(1)}, f32[128,64]{1,0:T(8,128)S(1)}) fusion(f32[64,128]{0,1:T(8,128)} %constant.53, f32[]{:T(128)S(6)} %mul.115, f32[64,128]{0,1:T(8,128)} %constant.52), kind=kLoop, calls=%fused_computation.45 | loop fusion | flops 32768 | bytes 131076 | tf_op jit(solution)/shard_map/div | solution.py:69
  18.6 7.8 %all-to-all-done = bf16[64,16,128]{2,1,0:T(8,128)(2,1)S(1)} async-done(((bf16[64,16,128]{2,1,0:T(8,128)(2,1)}), bf16[64,16,128]{2,1,0:T(8,128)(2,1)S(1)}, u32[]{:S(2)}, u32[]{:S(2)}) %all-to-all-start) | async-done | bytes 262176 | tf_op jit(solution)/shard_map/all_to_all | solution.py:85
  26.3 0.2 reshape.109
  26.6 0.3 fusion
  27.0 1.5 %fusion.41 = f32[6,528,256]{2,1,0:T(8,128)S(1)} fusion(bf16[6,528,64]{1,2,0:T(8,128)(2,1)S(1)} %fusion, f32[64,256,1]{1,0,2:T(8,128)S(1)} %copy-done.2), kind=kOutput, calls=%fused_computation.72 | convolution fusion | flops 622854144 | bytes 3715072 | tf_op jit(solution)/shard_map/qfb,bk->qfk/dot_general | solution.py:96
  28.5 0.2 slice_add_fusion
  28.7 0.2 multiply_subtract_fusion
  28.9 0.7 fusion.3
  29.6 0.1 fusion.40
  29.8 0.7 %fusion.2 = f32[64,2,256]{2,0,1:T(8,128)S(1)} fusion(f32[256,528,1]{0,1,2:T(8,128)S(1)} %copy-done, f32[2,264,64]{2,1,0:T(8,128)S(1)} %get-tuple-element.11, f32[2,264,64]{2,1,0:T(8,128)S(1)} %get-tuple-element.10, bf16[64,4,2,256]{3,0,2,1:T(8,128)(2,1)S(1)} %bitcast.55, f32[2]{0:T(128)S(1)} %dynamic_slice.3), kind=kOutput, calls=%fused_computation.5 | convolution fusion | flops 104040448 | bytes 1073160 | tf_op jit(solution)/shard_map/cfi,tf->ict/dot_general | solution.py:113
  30.4 0.1 copy.18
  30.5 15.8 %all_to_all.10 = f32[64,2,256]{2,1,0:T(2,128)S(1)} all-to-all(f32[64,2,256]{2,1,0:T(2,128)S(1)} %copy.18), channel_id=1, replica_groups=mesh['seq'=64,'ch'=8] {'seq'}, dimensions={0} | all-to-all | bytes 262144 | tf_op jit(solution)/shard_map/all_to_all | solution.py:119
  46.3 0.1 multiply_reduce_fusion
  46.4 19.4 %all-gather.1 = f32[8,1,256]{2,1,0:T(1,128)S(1)} all-gather(f32[1,1,256]{2,1,0:T(1,128)S(1)} %bitcast.57), channel_id=2, replica_groups=mesh['seq'=64,'ch'=8] {'ch'}, dimensions={0}, use_global_device_ids=true | all-gather | bytes 9216 | tf_op jit(solution)/shard_map/all_gather | solution.py:123
  65.8 0.1 reshape.111
  65.9 0.9 %convolution_convert_fusion.2 = bf16[256,128]{1,0:T(8,128)(2,1)} fusion(f32[128,256]{1,0:T(8,128)S(1)} %reshape.111, f32[256]{0:T(256)S(1)} %add_rsqrt_fusion, f32[128]{0:T(128)S(1)} %copy-done.3), kind=kOutput, calls=%fused_computation.6 | convolution fusion | flops 16973824 | bytes 198144 | tf_op jit(solution)/shard_map/tk,ck->tc/dot_general | solution.py:127
  (19 shorter events, 0.3 us)
Async XLA Ops:
  0.0 26.6 %copy-start.1 = (bf16[528,256,1]{1,0,2:T(8,128)(2,1)S(1)}, bf16[528,256,1]{1,0,2:T(8,128)(2,1)}, u32[]{:S(2)}) copy-start(bf16[528,256,1]{1,0,2:T(8,128)(2,1)} %constant.54) | copy-start | bytes 811012
  0.0 27.0 %copy-start.2 = (f32[64,256,1]{1,0,2:T(8,128)S(1)}, f32[64,256,1]{1,0,2:T(8,128)}, u32[]{:S(2)}) copy-start(f32[64,256,1]{1,0,2:T(8,128)} %constant.55) | copy-start | bytes 196612
  2.2 24.1 %all-to-all-start = ((bf16[64,16,128]{2,1,0:T(8,128)(2,1)}), bf16[64,16,128]{2,1,0:T(8,128)(2,1)S(1)}, u32[]{:S(2)}, u32[]{:S(2)}) async-start(bf16[64,16,128]{2,1,0:T(8,128)(2,1)} %reshape.108), calls=%async_computation | async-start | bytes 524288 | tf_op jit(solution)/shard_map/all_to_all | solution.py:85
  28.6 1.1 %copy-start = (f32[256,528,1]{0,1,2:T(8,128)S(1)}, f32[256,528,1]{0,1,2:T(8,128)}, u32[]{:S(2)}) copy-start(f32[256,528,1]{0,1,2:T(8,128)} %constant.56) | copy-start | bytes 1622020
  28.8 37.1 %copy-start.3 = (f32[128]{0:T(128)S(1)}, f32[128]{0:T(128)}, u32[]{:S(2)}) copy-start(f32[128]{0:T(128)} %param.14) | copy-start | bytes 1540

commit v21 on v20

--- a/solution.py
+++ b/solution.py
@@ -123,10 +123,7 @@
     squares = jnp.sum(lax.all_gather(partial, "ch", axis=0, tiled=False), axis=0)
     inv_norm = lax.rsqrt(squares / D + 1e-06)
     out_t = (norm_gain[:, None] * mix_t * inv_norm[None, :]).astype(jnp.bfloat16)
-    eye_tok = jnp.eye(rows_dev, dtype=jnp.bfloat16)
-    return jnp.einsum("tk,ck->tc", eye_tok, out_t, preferred_element_type=f32).astype(
-        jnp.bfloat16
-    )
+    return out_t.T
 
 
 def solution(mesh):

time: 67.1 us -> 67.1 us (level)
  matrix products: 5.28 us -> 4.39 us
  local copies, waits for them, and re-layouts: 2.31 us -> 3.04 us
    dot_general x1 -> x0, matrix products: 0.89 us -> none  [on_device(): jnp.einsum('tk,ck->tc', eye_tok, out_t, preferred_element_type=f32)]
    transpose x0 -> x1, local copies, waits for them, and re-layouts: none -> 0.73 us  [on_device(): return out_t.T]
where the time goes in v21:
time: 67.1 us; the launch traced here: 66.7 us
  blocking collectives  35.1 us (52%)
  starting transfers between devices  12.9 us (19%)
  waiting for transfers between devices  7.76 us (12%)
  matrix products  4.39 us (7%)
  other arithmetic  3.28 us (5%)
  local copies, waits for them, and re-layouts  3.04 us (5%)
    all_gather x1, blocking collectives, on_device(): lax.all_gather(partial, 'ch', axis=0, tiled=False)  19.4 us
    all_to_all x1, blocking collectives, on_device(): got = lax.all_to_all(mixed_local, 'seq', 0, 0, tiled=True)  15.8 us
    all_to_all x1, starting transfers between devices, on_device(): recv = lax.all_to_all(send, 'seq', 0, 0, tiled=True)  12.9 us
    all_to_all x1, waiting for transfers between devices, on_device(): recv = lax.all_to_all(send, 'seq', 0, 0, tiled=True)  7.76 us
    dot_general x1, matrix products, on_device(): jnp.einsum('qfb,bk->qfk', spec, ofwd, precision=HIGHEST, preferred_elemen...  1.49 us
  transfers between devices with their start and end apart: 1, of which 1 were waited for; matrix products, arithmetic and copies ran while one was open for 5% of the time, Pallas kernels for 0%

profile of v21, /device:TPU:1, one launch (start us, length us, event | category | flops | bytes accessed | tf_op | source)
XLA Modules:
  0.0 66.7 jit_solution(5559094021296065555)
XLA Ops:
  0.0 1.2 %convolution_convert_fusion.1 = bf16[128,4,256]{2,0,1:T(8,128)(2,1)S(1)} fusion(bf16[1,256,128]{2,1,0:T(8,128)(2,1)} %bitcast.60, bf16[1,256,128]{2,1,0:T(8,128)(2,1)} %bitcast.61, bf16[1,256,128]{2,1,0:T(8,128)(2,1)} %bitcast.62, bf16[1,256,128]{2,1,0:T(8,128)(2,1)} %bitcast.63), kind=kOutput, calls=%fused_computation.2 | convolution fusion | flops 34750464 | bytes 524288 | tf_op jit(solution)/shard_map/ck,atk->cat/dot_general | solution.py:81
  1.2 0.2 copy.16
  1.4 0.8 %reshape.108 = bf16[64,16,128]{2,1,0:T(8,128)(2,1)} reshape(bf16[128,4,256]{2,1,0:T(4,128)(2,1)S(1)} %copy.16) | data formatting | bytes 524288 | tf_op jit(solution)/shard_map/reshape | solution.py:84
  2.2 12.9 %all-to-all-start = ((bf16[64,16,128]{2,1,0:T(8,128)(2,1)}), bf16[64,16,128]{2,1,0:T(8,128)(2,1)S(1)}, u32[]{:S(2)}, u32[]{:S(2)}) async-start(bf16[64,16,128]{2,1,0:T(8,128)(2,1)} %reshape.108), calls=%async_computation | async-start | bytes 524288 | tf_op jit(solution)/shard_map/all_to_all | solution.py:85
  15.3 0.9 %fusion.28 = f32[128,64]{1,0:T(8,128)S(1)} fusion(f32[64,128]{0,1:T(8,128)} %constant.53, f32[]{:T(128)S(6)} %mul.115), kind=kLoop, calls=%fused_computation.50 | loop fusion | flops 24576 | bytes 65540 | tf_op jit(solution)/shard_map/neg | solution.py:71
  16.1 0.7 %fusion.35 = (f32[128]{0:T(128)S(1)}, f32[128]{0:T(128)S(1)}) fusion(f32[1,128]{1,0:T(1,128)} %constant.51, f32[]{:T(128)S(6)} %mul.115, f32[1,128]{1,0:T(1,128)} %constant.50), kind=kLoop, calls=%fused_computation.62 | loop fusion | flops 384 | bytes 2052 | tf_op jit(solution)/shard_map/mul | solution.py:101
  16.8 0.7 %dynamic_slice.3 = f32[2]{0:T(128)S(1)} dynamic-slice(f32[128]{0:T(128)} %param.13, s32[]{:T(128)S(6)} %select_n.22), dynamic_slice_sizes={2} | dynamic-slice | bytes 20 | tf_op jit(solution)/shard_map/dynamic_slice | solution.py:115
  17.6 0.1 broadcast_add_fusion
  17.7 0.9 %fusion.24 = (f32[128,64]{1,0:T(8,128)S(1)}, f32[128,64]{1,0:T(8,128)S(1)}) fusion(f32[64,128]{0,1:T(8,128)} %constant.53, f32[]{:T(128)S(6)} %mul.115, f32[64,128]{0,1:T(8,128)} %constant.52), kind=kLoop, calls=%fused_computation.44 | loop fusion | flops 32768 | bytes 131076 | tf_op jit(solution)/shard_map/div | solution.py:69
  18.6 7.8 %all-to-all-done = bf16[64,16,128]{2,1,0:T(8,128)(2,1)S(1)} async-done(((bf16[64,16,128]{2,1,0:T(8,128)(2,1)}), bf16[64,16,128]{2,1,0:T(8,128)(2,1)S(1)}, u32[]{:S(2)}, u32[]{:S(2)}) %all-to-all-start) | async-done | bytes 262176 | tf_op jit(solution)/shard_map/all_to_all | solution.py:85
  26.3 0.2 reshape.109
  26.6 0.3 fusion
  27.0 1.5 %fusion.40 = f32[6,528,256]{2,1,0:T(8,128)S(1)} fusion(bf16[6,528,64]{1,2,0:T(8,128)(2,1)S(1)} %fusion, f32[64,256,1]{1,0,2:T(8,128)S(1)} %copy-done.2), kind=kOutput, calls=%fused_computation.69 | convolution fusion | flops 622854144 | bytes 3715072 | tf_op jit(solution)/shard_map/qfb,bk->qfk/dot_general | solution.py:96
  28.5 0.2 slice_add_fusion
  28.7 0.2 multiply_subtract_fusion
  28.9 0.7 fusion.3
  29.6 0.1 fusion.39
  29.8 0.7 %fusion.2 = f32[64,2,256]{2,0,1:T(8,128)S(1)} fusion(f32[256,528,1]{0,1,2:T(8,128)S(1)} %copy-done, f32[2,264,64]{2,1,0:T(8,128)S(1)} %get-tuple-element.11, f32[2,264,64]{2,1,0:T(8,128)S(1)} %get-tuple-element.10, bf16[64,4,2,256]{3,0,2,1:T(8,128)(2,1)S(1)} %bitcast.57, f32[2]{0:T(128)S(1)} %dynamic_slice.3), kind=kOutput, calls=%fused_computation.5 | convolution fusion | flops 104040448 | bytes 1073160 | tf_op jit(solution)/shard_map/cfi,tf->ict/dot_general | solution.py:113
  30.4 0.1 copy.19
  30.5 15.8 %all_to_all.10 = f32[64,2,256]{2,1,0:T(2,128)S(1)} all-to-all(f32[64,2,256]{2,1,0:T(2,128)S(1)} %copy.19), channel_id=1, replica_groups=mesh['seq'=64,'ch'=8] {'seq'}, dimensions={0} | all-to-all | bytes 262144 | tf_op jit(solution)/shard_map/all_to_all | solution.py:119
  46.3 0.1 multiply_reduce_fusion
  46.4 19.4 %all-gather.1 = f32[8,1,256]{2,1,0:T(1,128)S(1)} all-gather(f32[1,1,256]{2,1,0:T(1,128)S(1)} %bitcast.59), channel_id=2, replica_groups=mesh['seq'=64,'ch'=8] {'ch'}, dimensions={0}, use_global_device_ids=true | all-gather | bytes 9216 | tf_op jit(solution)/shard_map/all_gather | solution.py:123
  65.8 0.1 reshape.111
  66.0 0.7 %copy.20 = bf16[256,128]{1,0:T(8,128)(2,1)} copy(bf16[256,128]{0,1:T(8,128)(2,1)S(1)} %fusion.23) | data formatting | bytes 131072 | tf_op jit(solution)/shard_map/transpose | solution.py:126
  (20 shorter events, 0.4 us)
Async XLA Ops:
  0.0 26.6 %copy-start.1 = (bf16[528,256,1]{1,0,2:T(8,128)(2,1)S(1)}, bf16[528,256,1]{1,0,2:T(8,128)(2,1)}, u32[]{:S(2)}) copy-start(bf16[528,256,1]{1,0,2:T(8,128)(2,1)} %constant.54) | copy-start | bytes 811012
  0.0 27.0 %copy-start.2 = (f32[64,256,1]{1,0,2:T(8,128)S(1)}, f32[64,256,1]{1,0,2:T(8,128)}, u32[]{:S(2)}) copy-start(f32[64,256,1]{1,0,2:T(8,128)} %constant.55) | copy-start | bytes 196612
  2.2 24.1 %all-to-all-start = ((bf16[64,16,128]{2,1,0:T(8,128)(2,1)}), bf16[64,16,128]{2,1,0:T(8,128)(2,1)S(1)}, u32[]{:S(2)}, u32[]{:S(2)}) async-start(bf16[64,16,128]{2,1,0:T(8,128)(2,1)} %reshape.108), calls=%async_computation | async-start | bytes 524288 | tf_op jit(solution)/shard_map/all_to_all | solution.py:85
  28.6 1.1 %copy-start = (f32[256,528,1]{0,1,2:T(8,128)S(1)}, f32[256,528,1]{0,1,2:T(8,128)}, u32[]{:S(2)}) copy-start(f32[256,528,1]{0,1,2:T(8,128)} %constant.56) | copy-start | bytes 1622020
  28.8 37.1 %copy-start.3 = (f32[128]{0:T(128)S(1)}, f32[128]{0:T(128)}, u32[]{:S(2)}) copy-start(f32[128]{0:T(128)} %param.14) | copy-start | bytes 1540
